TPU v7x, 256 devices: a whole 4x4x8 slice. The times are simulated.
256 devices in a mesh: leaf: 256 (over y, x, z, core).
Axes of the slice: x: 4, y: 4, z: 8, core: 2. Of those that a mesh axis runs over, the one named last changes fastest.
Arguments:
- vectors: bfloat16 [1048576, 64], P('leaf'), may hold values from -6 to 6
- contexts: float32 [8, 1048576], P(None, 'leaf'), may hold values from -6 to 6
- tree_order: int32 [256, 4096], P('leaf'), may hold values from 0 to 4095, each once within a row
- live_counts: int32 [512], P('leaf'), may hold values from 1024 to 2048, as said below
- level_bases: bfloat16 [9, 1048576, 128], P(None, 'leaf'), may hold values from -6 to 6
- coupling: float32 [9, 128], replicated, may hold values from 0.3 to 1.5
- length_scale: float32 [8], replicated, may hold values from 0.7 to 2
Outputs:
- kernel_product: bfloat16 [1048576, 64], P('leaf')
Inputs may be any that keep to these rules, and one draw needn't show every extreme that they name: `tree_order`: each device's row is a permutation of its 4096 context indices. `live_counts`: some leaf has exactly 1024 live slots and some leaf is full.
All inputs are finite; a program needn't handle non-finite values.
Results may differ from a plain program's by a relative error of at most 0.0048.
Values sent between devices are 32-bit elements; how exact they have to be, the bound alone decides.
No kernel may reach another device: no remote copies, remote signals or barrier semaphores. Data moves between devices by JAX's collectives and lax.ppermute only.
A program may use at most 64 MiB of HBM per device.

v0:
```python
import math

import jax
import jax.numpy as jnp
from jax import lax
from jax.experimental import pallas as pl
from jax.sharding import PartitionSpec as P

LEAF = 2048
RANK = 128
PANEL = 64
DIM = 8


root_three = math.sqrt(3.0)
FEATURES = 64
BLOCK = 256
BUTTERFLY_LEVELS = 4


def gram_features(points):
    def split(value):
        high = lax.reduce_precision(value, exponent_bits=8, mantissa_bits=7)
        rest = value - high
        middle = lax.reduce_precision(rest, exponent_bits=8, mantissa_bits=7)
        low = rest - middle
        return (
            high.astype(jnp.bfloat16),
            middle.astype(jnp.bfloat16),
            low.astype(jnp.bfloat16),
        )

    norm = jnp.zeros_like(points[0])
    for coord_index in range(points.shape[0]):
        norm = norm + points[coord_index] * points[coord_index]
    high, middle, low = split(points)
    norm_parts = jnp.stack(split(norm))
    ones = jnp.ones((3, points.shape[1]), jnp.bfloat16)
    pad = jnp.zeros((FEATURES - 6 * DIM - 6, points.shape[1]), jnp.bfloat16)
    twice = lambda part: part * jnp.asarray(-2.0, jnp.bfloat16)
    lhs = jnp.concatenate(
        [twice(high), twice(high), twice(middle), twice(middle), twice(high), twice(low), norm_parts, ones, pad]
    )
    rhs = jnp.concatenate([high, middle, high, middle, low, high, ones, norm_parts, pad])
    return lhs.T, rhs


def dense_kernel(lhs_ref, rhs_ref, vec_ref, out_ref):
    squared = jnp.dot(lhs_ref[...], rhs_ref[...], preferred_element_type=jnp.float32)
    scaled = root_three * jnp.sqrt(jnp.maximum(squared, 0.0))
    kernel = ((1.0 + scaled) * jnp.exp(-scaled)).astype(jnp.bfloat16)
    out_ref[...] = jnp.dot(kernel, vec_ref[...], preferred_element_type=jnp.float32)


def dense_rows(lhs, rhs, vec, row_start, rows):
    leaf = row_start // LEAF
    first = row_start // BLOCK
    return pl.pallas_call(
        dense_kernel,
        grid=(rows // BLOCK,),
        in_specs=[
            pl.BlockSpec((BLOCK, FEATURES), lambda i: (first + i, 0)),
            pl.BlockSpec((FEATURES, LEAF), lambda i: (0, leaf)),
            pl.BlockSpec((LEAF, PANEL), lambda i: (leaf, 0)),
        ],
        out_specs=pl.BlockSpec((BLOCK, PANEL), lambda i: (i, 0)),
        out_shape=jax.ShapeDtypeStruct((rows, PANEL), jnp.float32),
    )(lhs, rhs, vec)


def swapped(x, axis, bit):
    return lax.ppermute(x, axis, [(i, i ^ 1 << bit) for i in range(lax.axis_size(axis))])


def gram_features(points):
    def split(value):
        high = lax.reduce_precision(value, exponent_bits=8, mantissa_bits=7)
        rest = value - high
        middle = lax.reduce_precision(rest, exponent_bits=8, mantissa_bits=7)
        low = rest - middle
        return (
            high.astype(jnp.bfloat16),
            middle.astype(jnp.bfloat16),
            low.astype(jnp.bfloat16),
        )

    norm = jnp.zeros_like(points[0])
    for coord_index in range(points.shape[0]):
        norm = norm + points[coord_index] * points[coord_index]
    high, middle, low = split(points)
    norm_parts = jnp.stack(split(norm))
    ones = jnp.ones((3, points.shape[1]), jnp.bfloat16)
    pad = jnp.zeros((FEATURES - 6 * DIM - 6, points.shape[1]), jnp.bfloat16)
    twice = lambda part: part * jnp.asarray(-2.0, jnp.bfloat16)
    lhs = jnp.concatenate(
        [twice(high), twice(high), twice(middle), twice(middle), twice(high), twice(low), norm_parts, ones, pad]
    )
    rhs = jnp.concatenate([high, middle, high, middle, low, high, ones, norm_parts, pad])
    return lhs, rhs


def dense_kernel(lhs_ref, rhs_ref, vec_ref, out_ref):
    squared = jnp.dot(lhs_ref[...], rhs_ref[...], preferred_element_type=jnp.float32)
    scaled = root_three * jnp.sqrt(jnp.maximum(squared, 0.0))
    kernel = ((1.0 + scaled) * jnp.exp(-scaled)).astype(jnp.bfloat16)
    out_ref[...] = jnp.dot(kernel, vec_ref[...], preferred_element_type=jnp.float32)


def dense_leaves(lhs, rhs, vec):
    rows = lhs.shape[0]
    per_leaf = LEAF // BLOCK
    return pl.pallas_call(
        dense_kernel,
        grid=(rows // BLOCK,),
        in_specs=[
            pl.BlockSpec((BLOCK, FEATURES), lambda i: (i, 0)),
            pl.BlockSpec((FEATURES, LEAF), lambda i: (0, i // per_leaf)),
            pl.BlockSpec((LEAF, PANEL), lambda i: (i // per_leaf, 0)),
        ],
        out_specs=pl.BlockSpec((BLOCK, PANEL), lambda i: (i, 0)),
        out_shape=jax.ShapeDtypeStruct((rows, PANEL), jnp.float32),
    )(lhs, rhs, vec)


def body(vectors, contexts, tree_order, live_counts, level_bases, coupling, length_scale):
    per_device = vectors.shape[0]
    leaf_count = live_counts.shape[0]
    local_levels = leaf_count.bit_length() - 1
    device_count = lax.axis_size("leaf")
    device_levels = device_count.bit_length() - 1
    slot_order = tree_order[0]
    onehot = (slot_order[:, None] == jnp.arange(per_device, dtype=jnp.int32)[None, :]).astype(
        jnp.bfloat16
    )
    lhs_features, rhs_features = gram_features(contexts / length_scale[:, None])
    gathered = lax.dot_general(
        onehot,
        jnp.concatenate([vectors, lhs_features.T], axis=1),
        (((1,), (0,)), ((), ())),
        preferred_element_type=jnp.float32,
    ).astype(jnp.bfloat16)
    ordered = gathered[:, :PANEL]
    lhs = gathered[:, PANEL:]
    rhs = lax.dot_general(
        rhs_features, onehot, (((1,), (1,)), ((), ())), preferred_element_type=jnp.float32
    ).astype(jnp.bfloat16)
    slot_limit = jnp.repeat(live_counts, LEAF)
    within = jnp.arange(per_device, dtype=jnp.int32) % LEAF
    live_rows = (within < slot_limit)[:, None]
    masked = jnp.where(live_rows, ordered, jnp.zeros_like(ordered))

    partials = jnp.einsum(
        "rp,lrk->lpk", masked, level_bases[local_levels:], preferred_element_type=jnp.float32
    )
    split_level = min(BUTTERFLY_LEVELS, device_levels)
    stack = partials[:split_level]
    finished = []
    for bit_index in range(split_level):
        received = swapped(stack, "leaf", bit_index)
        finished.append(received[0])
        stack = stack[1:] + received[1:]
    me = lax.axis_index("leaf")
    slots = []
    for step_index in range(split_level, device_levels):
        count = device_count >> step_index
        hot = (jnp.arange(count, dtype=jnp.int32) == (me >> step_index)).astype(jnp.float32)
        slots.append(hot[:, None, None] * partials[step_index][None])
    if slots:
        summed = lax.psum(jnp.concatenate(slots), "leaf")
        offset = 0
        for step_index in range(split_level, device_levels):
            count = device_count >> step_index
            finished.append(
                lax.dynamic_index_in_dim(summed, offset + ((me >> step_index) ^ 1), 0, keepdims=False)
            )
            offset += count
    sibling_totals = jnp.stack(finished)

    accumulated = dense_leaves(lhs, rhs, masked)

    level_index = 0
    node_rows = LEAF * 2**level_index
    node_count = per_device // node_rows
    basis_nodes = level_bases[level_index].reshape(node_count, node_rows, RANK)
    vector_nodes = masked.reshape(node_count, node_rows, PANEL)
    node_sums = jnp.einsum(
        "nrp,nrk->npk", vector_nodes, basis_nodes, preferred_element_type=jnp.float32
    )
    node_coef = node_sums * (1.0 / math.sqrt(node_rows))
    sibling = node_coef.reshape(node_count // 2, 2, PANEL, RANK)[:, ::-1].reshape(
        node_count, PANEL, RANK
    )
    weights = (sibling * (coupling[level_index] / math.sqrt(RANK))).astype(jnp.bfloat16)
    accumulated = accumulated + jnp.einsum(
        "nrk,npk->nrp", basis_nodes, weights, preferred_element_type=jnp.float32
    ).reshape(per_device, PANEL)

    node_scale = jnp.array(
        [1.0 / math.sqrt(LEAF * 2 ** (local_levels + s)) for s in range(device_levels)],
        jnp.float32,
    )[:, None, None]
    node_coef = sibling_totals * node_scale
    weights = (node_coef * (coupling[local_levels:, None, :] / math.sqrt(RANK))).astype(
        jnp.bfloat16
    )
    accumulated = accumulated + jnp.einsum(
        "lrk,lpk->rp", level_bases[local_levels:], weights, preferred_element_type=jnp.float32
    )
    result = jnp.where(live_rows, accumulated, jnp.zeros_like(accumulated)).astype(jnp.bfloat16)
    return lax.dot_general(
        onehot, result, (((0,), (0,)), ((), ())), preferred_element_type=jnp.float32
    ).astype(jnp.bfloat16)


def solution(mesh):
    in_specs = (
        P("leaf", None),
        P(None, "leaf"),
        P("leaf", None),
        P("leaf"),
        P(None, "leaf", None),
        P(),
        P(),
    )
    out_specs = P("leaf", None)
    return jax.shard_map(body, mesh=mesh, in_specs=in_specs, out_specs=out_specs, check_vma=False)
```

profile of v0, /device:TPU:6, one launch (start us, length us, event | category | flops | bytes accessed | tf_op | source)
XLA Modules:
  0.0 320.5 jit_solution(7053664452837523335)
XLA Ops:
  6.5 0.0 copy-start
  6.5 0.0 all-reduce.2.cloned.1.call-start
  6.5 1.0 broadcast_multiply_fusion.4
  7.6 0.2 fusion.35
  7.8 0.0 copy-done
  7.8 0.0 copy-start.2
  7.8 0.1 broadcast_bitcast_fusion
  8.0 0.0 slice-start
  8.0 0.5 concatenate.14
  8.4 0.0 slice-start.1
  8.4 0.0 slice-start.2
  8.5 12.7 %fusion.16 = bf16[4096,128]{1,0:T(8,128)(2,1)S(1)} fusion(s32[4096]{0:T(1024)} %bitcast.49, bf16[4096,64]{0,1:T(8,128)(2,1)S(1)} %bitcast.47, bf16[4096,64]{0,1:T(8,128)(2,1)} %param.8), kind=kOutput, calls=%fused_computation.13 | convolution fusion | flops 4314365952 | bytes 2113536 | tf_op jit(solution)/shard_map/dot_general | solution.py:136
  21.2 2.9 slice_select_fusion
  24.1 0.0 copy-start.1
  24.1 0.0 slice-done
  24.1 0.0 slice-done.1
  24.1 0.0 slice-done.2
  24.1 1.6 fusion.25
  25.7 0.0 copy-done.2
  25.8 0.1 broadcast_multiply_fusion
  25.9 0.1 broadcast_multiply_fusion.1
  26.0 0.1 broadcast_multiply_fusion.2
  26.1 0.1 broadcast_multiply_fusion.3
  26.2 1.0 pad_maximum_fusion
  27.2 0.0 all-reduce.2.cloned.1.call-update
  27.2 0.7 slice.132
  27.9 0.0 collective-permute-start
  27.9 1.3 slice.104
  29.2 1.2 concatenate.16
  30.4 0.0 copy-start.3
  30.4 17.8 %fusion.24.rhs_ref = bf16[64,4096]{1,0:T(8,128)(2,1)} fusion(bf16[64,4096]{1,0:T(8,128)(2,1)S(1)} %concatenate.16, s32[4096]{0:T(1024)} %bitcast.50), kind=kOutput, calls=%fused_computation.17 | convolution fusion | flops 2164523008 | bytes 1064960 | tf_op jit(solution)/shard_map/dot_general | solution.py:144
  48.2 0.0 copy-done.3
  48.2 0.0 copy-done.1
  48.2 0.5 fusion.50
  48.8 0.0 copy-start.5
  48.8 0.5 convolution_bitcast_fusion
  49.3 0.6 copy.10
  49.9 24.3 %shard_map.82 = f32[4096,64]{1,0:T(8,128)} custom-call(bf16[4096,64]{1,0:T(8,128)(2,1)} %get-tuple-element.15.lhs_ref, bf16[64,4096]{1,0:T(8,128)(2,1)} %fusion.24.rhs_ref, bf16[4096,64]{1,0:T(8,128)(2,1)} %copy-done.1), custom_call_target="tpu_custom_call" | custom-call | tf_op jit(solution)/shard_map/pallas_call | solution.py:112
  74.1 3.1 bitcast_add_fusion
  77.3 0.0 collective-permute-done
  77.3 0.9 slice_add_fusion
  78.2 2.0 collective-permute-start.1
  80.2 0.8 slice_dynamic-update-slice_fusion.2
  81.0 2.9 collective-permute-done.1
  83.9 3.3 %collective-permute-start.2 = (f32[2,64,128]{2,1,0:T(8,128)S(1)}, f32[2,64,128]{2,1,0:T(8,128)S(1)}, u32[]{:S(2)}, u32[]{:S(2)}) collective-permute-start(f32[2,64,128]{2,1,0:T(8,128)S(1)} %slice_add_fusion.1), channel_id=1, source_target_pairs={{0,4},{1,5},{2,6},{3,7},{4,0},{5,1},{6,2},{7,3},{8,12},{9,13},{10,... | collective-permute-start | bytes 196616 | tf_op jit(solution)/shard_map/ppermute | solution.py:72
  87.2 3.6 %collective-permute-done.2 = f32[2,64,128]{2,1,0:T(8,128)S(1)} collective-permute-done((f32[2,64,128]{2,1,0:T(8,128)S(1)}, f32[2,64,128]{2,1,0:T(8,128)S(1)}, u32[]{:S(2)}, u32[]{:S(2)}) %collective-permute-start.2) | collective-permute-done | bytes 65568 | tf_op jit(solution)/shard_map/ppermute | solution.py:72
  90.8 6.2 %collective-permute-start.3 = (f32[1,64,128]{2,1,0:T(8,128)S(1)}, f32[1,64,128]{2,1,0:T(8,128)S(1)}, u32[]{:S(2)}, u32[]{:S(2)}) collective-permute-start(f32[1,64,128]{2,1,0:T(8,128)S(1)} %get-tuple-element.22), channel_id=1, source_target_pairs={{0,8},{1,9},{2,10},{3,11},{4,12},{5,13},{6,14},{7,15},{8,0},{9,1},... | collective-permute-start | bytes 98312 | tf_op jit(solution)/shard_map/ppermute | solution.py:72
  97.0 1.9 collective-permute-done.3
  98.9 190.6 %all-reduce.2.cloned.1.call-done = f32[30,64,128]{2,1,0:T(8,128)} async-done(((f32[30,64,128]{2,1,0:T(8,128)}), f32[30,64,128]{2,1,0:T(8,128)}) %all-reduce.2.cloned.1.call-update) | async-done | bytes 983056 | tf_op jit(solution)/shard_map/psum | solution.py:169
  289.5 0.8 dynamic-slice_dynamic-update-slice_fusion.3
  290.2 0.8 dynamic-slice_dynamic-update-slice_fusion.2
  291.0 0.8 dynamic-slice_dynamic-update-slice_fusion.1
  291.7 0.8 dynamic-slice_dynamic-update-slice_fusion
  292.5 0.0 copy-done.5
  292.5 0.0 copy-start.4
  292.5 5.3 %fusion.20 = bf16[4096,64]{1,0:T(8,128)(2,1)S(1)} fusion(f32[4096,64]{1,0:T(8,128)} %bitcast_add_fusion, bf16[9,4096,128]{2,1,0:T(8,128)(2,1)} %param.12, pred[4096]{0:T(1024)(128)(4,1)S(1)} %fusion.36, f32[8,64,128]{2,1,0:T(8,128)S(1)} %dynamic-slice_dynamic-update-slice_fusion, f32[8,128]{1,0:T(8,128)S(1)} %slice_multiply_fusion.8, f32[8]{0:T(128)S(1)} %copy-done.5), kind=kOutput, calls=%fused_computation.15 | convolution fusion | flops 537853952 | bytes 11280416 | tf_op jit(solution)/shard_map/lrk,lpk->rp/dot_general | solution.py:206
  297.9 0.0 copy-done.4
  297.9 15.8 %fusion.23 = bf16[4096,64]{0,1:T(8,128)(2,1)} fusion(bf16[4096,64]{1,0:T(8,128)(2,1)S(1)} %fusion.20, s32[4096]{0:T(1024)S(1)} %bitcast.51), kind=kOutput, calls=%fused_computation.16 | convolution fusion | flops 2164523008 | bytes 1064960 | tf_op jit(solution)/shard_map/dot_general | solution.py:210
  (19 shorter events, 0.2 us)
Async XLA Ops:
  6.5 1.3 copy-start
  6.5 282.9 %all-reduce.2.cloned.1.call-start = ((), (), s32[]{:S(2)}) async-start(), calls=%async_computation | async-start | bytes 1966080 | tf_op jit(solution)/shard_map/psum | solution.py:169
  7.8 17.9 %copy-start.2 = (bf16[1,4096]{1,0:T(2,128)(2,1)}, bf16[1,4096]{1,0:T(2,128)(2,1)S(1)}, u32[]{:S(2)}) copy-start(bf16[1,4096]{1,0:T(2,128)(2,1)S(1)} %get-tuple-element.25) | copy-start | bytes 24580
  8.0 16.2 %slice-start = ((s8[9437184]{0:T(1024)(128)(4,1)}), s8[1048576]{0:T(1024)(128)(4,1)S(1)}, s32[]{:S(2)}) async-start(s8[9437184]{0:T(1024)(128)(4,1)} %bitcast.42), calls=%async_computation.1 | async-start | bytes 2097152
  8.4 15.7 %slice-start.1 = ((s8[9437184]{0:T(1024)(128)(4,1)}), s8[4194304]{0:T(1024)(128)(4,1)S(1)}, s32[]{:S(2)}) async-start(s8[9437184]{0:T(1024)(128)(4,1)} %bitcast.42), calls=%async_computation.2 | async-start | bytes 8388608
  8.4 15.7 %slice-start.2 = ((s8[9437184]{0:T(1024)(128)(4,1)}), s8[4194304]{0:T(1024)(128)(4,1)S(1)}, s32[]{:S(2)}) async-start(s8[9437184]{0:T(1024)(128)(4,1)} %bitcast.42), calls=%async_computation.3 | async-start | bytes 8388608
  24.1 24.1 %copy-start.1 = (bf16[4096,64]{1,0:T(8,128)(2,1)}, bf16[4096,64]{1,0:T(8,128)(2,1)S(1)}, u32[]{:S(2)}) copy-start(bf16[4096,64]{1,0:T(8,128)(2,1)S(1)} %get-tuple-element.14.vec_ref) | copy-start | bytes 1572868
  27.9 49.4 %collective-permute-start = (f32[4,64,128]{2,1,0:T(8,128)}, f32[4,64,128]{2,1,0:T(8,128)}, u32[]{:S(2)}, u32[]{:S(2)}) collective-permute-start(f32[4,64,128]{2,1,0:T(8,128)} %slice.132), channel_id=1, source_target_pairs={{0,1},{1,0},{2,3},{3,2},{4,5},{5,4},{6,7},{7,6},{8,9},{9,8},{10,11... | collective-permute-start | bytes 393224 | tf_op jit(solution)/shard_map/ppermute | solution.py:72
  30.4 17.9 %copy-start.3 = (f32[9,128]{1,0:T(8,128)S(1)}, f32[9,128]{1,0:T(8,128)}, u32[]{:S(2)}) copy-start(f32[9,128]{1,0:T(8,128)} %param.13) | copy-start | bytes 13828
  48.8 243.7 %copy-start.5 = (f32[8]{0:T(128)S(1)}, f32[8]{0:T(128)}, u32[]{:S(2)}) copy-start(f32[8]{0:T(128)} %constant.72.clone) | copy-start | bytes 100
  78.2 5.7 %collective-permute-start.1 = (f32[3,64,128]{2,1,0:T(8,128)S(1)}, f32[3,64,128]{2,1,0:T(8,128)S(1)}, u32[]{:S(2)}, u32[]{:S(2)}) collective-permute-start(f32[3,64,128]{2,1,0:T(8,128)S(1)} %slice_add_fusion), channel_id=1, source_target_pairs={{0,2},{1,3},{2,0},{3,1},{4,6},{5,7},{6,4},{7,5},{8,10},{9,11},{10,... | collective-permute-start | bytes 294920 | tf_op jit(solution)/shard_map/ppermute | solution.py:72
  83.9 7.0 %collective-permute-start.2 = (f32[2,64,128]{2,1,0:T(8,128)S(1)}, f32[2,64,128]{2,1,0:T(8,128)S(1)}, u32[]{:S(2)}, u32[]{:S(2)}) collective-permute-start(f32[2,64,128]{2,1,0:T(8,128)S(1)} %slice_add_fusion.1), channel_id=1, source_target_pairs={{0,4},{1,5},{2,6},{3,7},{4,0},{5,1},{6,2},{7,3},{8,12},{9,13},{10,... | collective-permute-start | bytes 196616 | tf_op jit(solution)/shard_map/ppermute | solution.py:72
  90.8 8.1 %collective-permute-start.3 = (f32[1,64,128]{2,1,0:T(8,128)S(1)}, f32[1,64,128]{2,1,0:T(8,128)S(1)}, u32[]{:S(2)}, u32[]{:S(2)}) collective-permute-start(f32[1,64,128]{2,1,0:T(8,128)S(1)} %get-tuple-element.22), channel_id=1, source_target_pairs={{0,8},{1,9},{2,10},{3,11},{4,12},{5,13},{6,14},{7,15},{8,0},{9,1},... | collective-permute-start | bytes 98312 | tf_op jit(solution)/shard_map/ppermute | solution.py:72
  292.5 5.4 %copy-start.4 = (s32[1,4096]{1,0:T(1,128)S(1)}, s32[1,4096]{1,0:T(1,128)}, u32[]{:S(2)}) copy-start(s32[1,4096]{1,0:T(1,128)} %param.10) | copy-start | bytes 49156
Sparse Core Ops, SparseCore 0:
  27.4 262.0 all-reduce.1
where the time goes:
time: 321 us
  waiting for transfers between devices  199 us (62%)
  matrix products  54.3 us (17%)
  Pallas kernels  24.3 us (8%)
  between operations  13.7 us (4%)
  starting transfers between devices  11.5 us (4%)
  other arithmetic  9.64 us (3%)
  local copies, waits for them, and re-layouts  8.15 us (3%)
    psum x1, waiting for transfers between devices, body(): summed = lax.psum(jnp.concatenate(slots), 'leaf')  191 us
    pallas_call x1, Pallas kernels, dense_leaves(): pl.pallas_call(dense_kernel, grid=(rows // BLOCK,), in_specs=[pl.BlockSpe...  24.3 us
    dot_general x1, matrix products, body(): lax.dot_general(rhs_features, onehot, (((1,), (1,)), ((), ())), preferred...  17.8 us
    dot_general x1, matrix products, body(): lax.dot_general(onehot, result, (((0,), (0,)), ((), ())), preferred_eleme...  15.8 us
    dot_general x1, matrix products, body(): lax.dot_general(onehot, jnp.concatenate([vectors, lhs_features.T], axis=1...  12.7 us
    ppermute x4, starting transfers between devices, swapped(): lax.ppermute(x, axis, [(i, i ^ 1 << bit) for i in range(lax.axis_size(axi...  11.5 us
    ppermute x4, waiting for transfers between devices, swapped(): lax.ppermute(x, axis, [(i, i ^ 1 << bit) for i in range(lax.axis_size(axi...  8.42 us
  transfers between devices with their start and end apart: 5, of which 4 were waited for; matrix products, arithmetic and copies ran while one was open for 9% of the time, Pallas kernels for 8%

commit v1 on v0

v1 whole, which is shorter than its diff:
```python
import math

import jax
import jax.numpy as jnp
from jax import lax
from jax.experimental import pallas as pl
from jax.sharding import PartitionSpec as P

LEAF = 2048
RANK = 128
PANEL = 64
DIM = 8


root_three = math.sqrt(3.0)
FEATURES = 64
BLOCK = 256


def swapped(x, axis, bit):
    return lax.ppermute(x, axis, [(i, i ^ 1 << bit) for i in range(lax.axis_size(axis))])


def gram_features(points):
    def split(value):
        high = lax.reduce_precision(value, exponent_bits=8, mantissa_bits=7)
        rest = value - high
        middle = lax.reduce_precision(rest, exponent_bits=8, mantissa_bits=7)
        low = rest - middle
        return (
            high.astype(jnp.bfloat16),
            middle.astype(jnp.bfloat16),
            low.astype(jnp.bfloat16),
        )

    norm = jnp.zeros_like(points[0])
    for coord_index in range(points.shape[0]):
        norm = norm + points[coord_index] * points[coord_index]
    high, middle, low = split(points)
    norm_parts = jnp.stack(split(norm))
    ones = jnp.ones((3, points.shape[1]), jnp.bfloat16)
    pad = jnp.zeros((FEATURES - 6 * DIM - 6, points.shape[1]), jnp.bfloat16)
    twice = lambda part: part * jnp.asarray(-2.0, jnp.bfloat16)
    lhs = jnp.concatenate(
        [twice(high), twice(high), twice(middle), twice(middle), twice(high), twice(low), norm_parts, ones, pad]
    )
    rhs = jnp.concatenate([high, middle, high, middle, low, high, ones, norm_parts, pad])
    return lhs.T, rhs


def dense_kernel(lhs_ref, rhs_ref, vec_ref, gate_ref, acc_ref, out_ref):
    del gate_ref, acc_ref
    squared = jnp.dot(lhs_ref[...], rhs_ref[...], preferred_element_type=jnp.float32)
    scaled = root_three * jnp.sqrt(jnp.maximum(squared, 0.0))
    kernel = ((1.0 + scaled) * jnp.exp(-scaled)).astype(jnp.bfloat16)
    out_ref[...] = jnp.dot(kernel, vec_ref[...], preferred_element_type=jnp.float32)


def dense_rows(acc, lhs, rhs, vec, gate, row_start, rows):
    leaf = row_start // LEAF
    first = row_start // BLOCK
    return pl.pallas_call(
        dense_kernel,
        grid=(rows // BLOCK,),
        in_specs=[
            pl.BlockSpec((BLOCK, FEATURES), lambda i: (first + i, 0)),
            pl.BlockSpec((FEATURES, LEAF), lambda i: (0, leaf)),
            pl.BlockSpec((LEAF, PANEL), lambda i: (leaf, 0)),
            pl.BlockSpec(memory_space=pl.ANY),
            pl.BlockSpec(memory_space=pl.ANY),
        ],
        out_specs=pl.BlockSpec((BLOCK, PANEL), lambda i: (first + i, 0)),
        out_shape=jax.ShapeDtypeStruct(acc.shape, jnp.float32),
        input_output_aliases={4: 0},
    )(lhs, rhs, vec, gate, acc)


def body(vectors, contexts, tree_order, live_counts, level_bases, coupling, length_scale):
    per_device = vectors.shape[0]
    leaf_count = live_counts.shape[0]
    local_levels = leaf_count.bit_length() - 1
    device_count = lax.axis_size("leaf")
    device_levels = device_count.bit_length() - 1
    slot_order = tree_order[0]
    onehot = (slot_order[:, None] == jnp.arange(per_device, dtype=jnp.int32)[None, :]).astype(
        jnp.bfloat16
    )
    lhs_features, _ = gram_features(contexts / length_scale[:, None])
    gathered = lax.dot_general(
        onehot,
        jnp.concatenate([vectors, lhs_features], axis=1),
        (((1,), (0,)), ((), ())),
        preferred_element_type=jnp.float32,
    ).astype(jnp.bfloat16)
    ordered = gathered[:, :PANEL]
    lhs = gathered[:, PANEL:]
    half = jnp.asarray(-0.5, jnp.bfloat16)
    high = lhs[:, 0:DIM] * half
    middle = lhs[:, 2 * DIM : 3 * DIM] * half
    low = lhs[:, 5 * DIM : 6 * DIM] * half
    norm_parts = lhs[:, 6 * DIM : 6 * DIM + 3]
    ones = lhs[:, 6 * DIM + 3 : 6 * DIM + 6]
    rhs = jnp.concatenate(
        [high, middle, high, middle, low, high, ones, norm_parts, lhs[:, 6 * DIM + 6 :]], axis=1
    ).T
    slot_limit = jnp.repeat(live_counts, LEAF)
    within = jnp.arange(per_device, dtype=jnp.int32) % LEAF
    live_rows = (within < slot_limit)[:, None]
    masked = jnp.where(live_rows, ordered, jnp.zeros_like(ordered))

    partials = jnp.einsum(
        "rp,lrk->lpk", masked, level_bases[local_levels:], preferred_element_type=jnp.float32
    )
    block_rows = min(512, LEAF)
    chunk_starts = list(range(0, per_device, block_rows))
    accumulated = jnp.zeros((per_device, PANEL), jnp.float32)
    stack = partials
    finished = []
    gate = jnp.zeros((8, RANK), jnp.float32)
    done = 0
    for bit_index in range(device_levels):
        received = swapped(stack, "leaf", bit_index)
        upto = (bit_index + 1) * len(chunk_starts) // device_levels
        for row_start in chunk_starts[done:upto]:
            accumulated = dense_rows(accumulated, lhs, rhs, masked, gate, row_start, block_rows)
        done = upto
        finished.append(received[0])
        stack = stack[1:] + received[1:]
        gate = received[0, :8]
    for row_start in chunk_starts[done:]:
        accumulated = dense_rows(accumulated, lhs, rhs, masked, gate, row_start, block_rows)
    sibling_totals = jnp.stack(finished)


    level_index = 0
    node_rows = LEAF * 2**level_index
    node_count = per_device // node_rows
    basis_nodes = level_bases[level_index].reshape(node_count, node_rows, RANK)
    vector_nodes = masked.reshape(node_count, node_rows, PANEL)
    node_sums = jnp.einsum(
        "nrp,nrk->npk", vector_nodes, basis_nodes, preferred_element_type=jnp.float32
    )
    node_coef = node_sums * (1.0 / math.sqrt(node_rows))
    sibling = node_coef.reshape(node_count // 2, 2, PANEL, RANK)[:, ::-1].reshape(
        node_count, PANEL, RANK
    )
    weights = (sibling * (coupling[level_index] / math.sqrt(RANK))).astype(jnp.bfloat16)
    accumulated = accumulated + jnp.einsum(
        "nrk,npk->nrp", basis_nodes, weights, preferred_element_type=jnp.float32
    ).reshape(per_device, PANEL)

    node_scale = jnp.array(
        [1.0 / math.sqrt(LEAF * 2 ** (local_levels + s)) for s in range(device_levels)],
        jnp.float32,
    )[:, None, None]
    node_coef = sibling_totals * node_scale
    weights = (node_coef * (coupling[local_levels:, None, :] / math.sqrt(RANK))).astype(
        jnp.bfloat16
    )
    accumulated = accumulated + jnp.einsum(
        "lrk,lpk->rp", level_bases[local_levels:], weights, preferred_element_type=jnp.float32
    )
    result = jnp.where(live_rows, accumulated, jnp.zeros_like(accumulated)).astype(jnp.bfloat16)
    return lax.dot_general(
        onehot, result, (((0,), (0,)), ((), ())), preferred_element_type=jnp.float32
    ).astype(jnp.bfloat16)


def solution(mesh):
    in_specs = (
        P("leaf", None),
        P(None, "leaf"),
        P("leaf", None),
        P("leaf"),
        P(None, "leaf", None),
        P(),
        P(),
    )
    out_specs = P("leaf", None)
    return jax.shard_map(body, mesh=mesh, in_specs=in_specs, out_specs=out_specs, check_vma=False)
```

time: 321 us -> 132 us (0.41)
  waiting for transfers between devices: 199 us -> 6.23 us
  matrix products: 54.3 us -> 35.7 us
  local copies, waits for them, and re-layouts: 8.15 us -> 25.8 us
  between operations: 13.7 us -> 0.24 us
  Pallas kernels: 24.3 us -> 36.5 us
  starting transfers between devices: 11.5 us -> 18.4 us
    psum x1 -> x0, waiting for transfers between devices: 191 us -> none  [body(): summed = lax.psum(jnp.concatenate(slots), 'leaf')]
    dot_general x2 -> x1, matrix products: 30.6 us -> 12 us  [body(): lax.dot_general(onehot, jnp.concatenate([vectors, lhs_features], axis=1),...]
    pallas_call x1 -> x8, Pallas kernels: 24.3 us -> 36.5 us  [dense_rows(): pl.pallas_call(dense_kernel, grid=(rows // BLOCK,), in_specs=[pl.BlockSpe...]
    concatenate x1, local copies, waits for them, and re-layouts: 1.16 us -> 10.6 us  [body(): jnp.concatenate([high, middle, high, middle, low, high, ones, norm_parts,...]
    ppermute x4 -> x8, starting transfers between devices: 11.5 us -> 18.4 us  [swapped(): lax.ppermute(x, axis, [(i, i ^ 1 << bit) for i in range(lax.axis_size(axi...]
    squeeze x0 -> x7, local copies, waits for them, and re-layouts: none -> 4.83 us  [body(): gate = received[0, :8]]
    ppermute x4 -> x8, waiting for transfers between devices: 8.42 us -> 6.23 us  [swapped(): lax.ppermute(x, axis, [(i, i ^ 1 << bit) for i in range(lax.axis_size(axi...]
  transfers between devices with their start and end apart: 5 -> 8, of which waited for: 4 -> 2; matrix products, arithmetic and copies ran while one was open for 9% -> 21% of each run, Pallas kernels for 8% -> 28%
where the time goes in v1:
time: 132 us; the launch traced here: 130 us
  Pallas kernels  36.5 us (28%)
  matrix products  35.7 us (27%)
  local copies, waits for them, and re-layouts  25.8 us (20%)
  starting transfers between devices  18.4 us (14%)
  other arithmetic  7.19 us (5%)
  waiting for transfers between devices  6.23 us (5%)
    pallas_call x8, Pallas kernels, dense_rows(): pl.pallas_call(dense_kernel, grid=(rows // BLOCK,), in_specs=[pl.BlockSpe...  36.5 us
    ppermute x8, starting transfers between devices, swapped(): lax.ppermute(x, axis, [(i, i ^ 1 << bit) for i in range(lax.axis_size(axi...  18.4 us
    dot_general x1, matrix products, body(): lax.dot_general(onehot, result, (((0,), (0,)), ((), ())), preferred_eleme...  15.8 us
    dot_general x1, matrix products, body(): lax.dot_general(onehot, jnp.concatenate([vectors, lhs_features], axis=1),...  12 us
    concatenate x1, local copies, waits for them, and re-layouts, body(): jnp.concatenate([high, middle, high, middle, low, high, ones, norm_parts,...  10.6 us
    ppermute x8, waiting for transfers between devices, swapped(): lax.ppermute(x, axis, [(i, i ^ 1 << bit) for i in range(lax.axis_size(axi...  6.23 us
    dot_general x1, matrix products, body(): jnp.einsum('lrk,lpk->rp', level_bases[local_levels:], weights, preferred_...  5.37 us
    squeeze x7, local copies, waits for them, and re-layouts, body(): gate = received[0, :8]  4.83 us
  transfers between devices with their start and end apart: 8, of which 2 were waited for; matrix products, arithmetic and copies ran while one was open for 21% of the time, Pallas kernels for 28%

profile of v1, /device:TPU:6, one launch (start us, length us, event | category | flops | bytes accessed | tf_op | source)
XLA Modules:
  0.0 130.1 jit_solution(12706099208299335402)
XLA Ops:
  0.0 0.0 copy-start
  0.0 1.1 fusion.28
  1.1 0.2 fusion.31
  1.3 0.0 copy-done
  1.3 0.1 broadcast_bitcast_fusion
  1.5 0.0 slice-start
  1.5 0.5 concatenate.9
  1.9 0.0 copy-done.4
  1.9 0.0 copy-done.3
  2.0 0.0 slice-start.1
  2.0 0.0 slice-start.2
  2.0 12.0 %fusion.11 = bf16[4096,128]{1,0:T(8,128)(2,1)S(1)} fusion(s32[4096]{0:T(1024)S(1)} %bitcast.58, bf16[4096,64]{0,1:T(8,128)(2,1)S(1)} %bitcast.56, bf16[4096,64]{0,1:T(8,128)(2,1)S(1)} %copy-done.3), kind=kOutput, calls=%fused_computation.10 | convolution fusion | flops 4314365952 | bytes 2113536 | tf_op jit(solution)/shard_map/dot_general | solution.py:89
  14.0 2.9 %slice_select_fusion = (bf16[4096,64]{1,0:T(8,128)(2,1)S(1)}, bf16[4096,64]{1,0:T(8,128)(2,1)}) fusion(bf16[4096,128]{1,0:T(8,128)(2,1)S(1)} %fusion.11, pred[4096]{0:T(1024)(128)(4,1)S(1)} %fusion.32), kind=kLoop, calls=%fused_computation.18 | loop fusion | flops 262144 | bytes 2101248 | tf_op jit(solution)/shard_map/jit(_where)/select_n | solution.py:109
  16.9 0.0 slice-done
  16.9 0.0 slice-done.2
  17.0 1.6 %fusion.16 = f32[8,64,128]{2,1,0:T(8,128)S(1)} fusion(bf16[9,4096,128]{2,1,0:T(8,128)(2,1)S(1)} %bitcast.52, bf16[4096,64]{1,0:T(8,128)(2,1)S(1)} %get-tuple-element.9.vec_ref), kind=kOutput, calls=%fused_computation.17 | convolution fusion | flops 536870912 | bytes 9699328 | tf_op jit(solution)/shard_map/rp,lrk->lpk/dot_general | solution.py:111
  18.6 0.3 collective-permute-start
  18.8 1.9 %slice_multiply_fusion = (bf16[4096,8]{1,0:T(8,128)(2,1)}, bf16[4096,8]{1,0:T(8,128)(2,1)S(1)}, bf16[4096,8]{1,0:T(8,128)(2,1)S(1)}) fusion(bf16[4096,128]{1,0:T(8,128)(2,1)S(1)} %fusion.11), kind=kLoop, calls=%fused_computation.19 | loop fusion | flops 98304 | bytes 393216 | tf_op jit(solution)/shard_map/mul | solution.py:100
  20.7 2.0 %fusion.45 = (bf16[4096,3]{1,0:T(8,128)(2,1)}, bf16[4096,3]{1,0:T(8,128)(2,1)}) fusion(bf16[4096,128]{1,0:T(8,128)(2,1)S(1)} %fusion.11), kind=kLoop, calls=%fused_computation.91 | loop fusion | bytes 98304 | tf_op jit(solution)/shard_map/slice | solution.py:101
  22.7 0.1 slice.195
  22.8 0.6 copy-done.2
  23.4 0.5 fusion.46
  23.9 0.5 convolution_bitcast_fusion
  24.4 1.3 %slice.221 = bf16[4096,10]{1,0:T(8,128)(2,1)} slice(bf16[4096,128]{1,0:T(8,128)(2,1)S(1)} %fusion.11), slice={[0:4096], [118:128]} | slice | bytes 163840 | tf_op jit(solution)/shard_map/slice | solution.py:104
  25.7 10.6 %concatenate.11 = bf16[4096,64]{1,0:T(8,128)(2,1)} concatenate(bf16[4096,8]{1,0:T(8,128)(2,1)S(1)} %get-tuple-element.15, bf16[4096,8]{1,0:T(8,128)(2,1)S(1)} %get-tuple-element.14, bf16[4096,8]{1,0:T(8,128)(2,1)S(1)} %get-tuple-element.15, bf16[4096,8]{1,0:T(8,128)(2,1)S(1)} %get-tuple-element.14, bf16[4096,8]{1,0:T(8,128)(2,1)} %get-tuple-element.13, ...), dimensions={1} | concatenate | bytes 1048576 | tf_op jit(solution)/shard_map/concatenate | solution.py:103
  36.3 2.3 %copy.25.rhs_ref = bf16[64,4096]{1,0:T(8,128)(2,1)} copy(bf16[64,4096]{0,1:T(8,128)(2,1)} %bitcast.55) | data formatting | bytes 1048576 | tf_op jit(solution)/shard_map/transpose | solution.py:105
  38.7 0.6 copy.26
  39.3 0.6 broadcast_in_dim.40.gate_ref
  39.9 1.5 %broadcast_5_acc_ref.2.acc_ref = f32[4096,64]{1,0:T(8,128)} broadcast(f32[]{:T(128)} %constant.35.clone.1), dimensions={} | broadcast | bytes 1048580 | tf_op jit(solution)/shard_map/broadcast.5.acc_ref
  41.4 4.6 %shard_map.82.acc_ref = f32[4096,64]{1,0:T(8,128)} custom-call(bf16[4096,64]{1,0:T(8,128)(2,1)} %get-tuple-element.10.lhs_ref, bf16[64,4096]{1,0:T(8,128)(2,1)} %copy.25.rhs_ref, bf16[4096,64]{1,0:T(8,128)(2,1)} %copy-done.1, f32[8,128]{1,0:T(8,128)} %broadcast_in_dim.40.gate_ref, f32[4096,64]{1,0:T(8,128)} %broadcast_5_acc_ref.2.acc_ref), custom_call_target="tpu_custom_call", output_to_operand_aliasing={{}: (4, {})} | custom-call | tf_op jit(solution)/shard_map/pallas_call | solution.py:62
  45.9 0.0 collective-permute-done
  45.9 1.0 slice_add_fusion
  46.9 2.0 %collective-permute-start.1 = (f32[7,64,128]{2,1,0:T(8,128)S(1)}, f32[7,64,128]{2,1,0:T(8,128)S(1)}, u32[]{:S(2)}, u32[]{:S(2)}) collective-permute-start(f32[7,64,128]{2,1,0:T(8,128)S(1)} %slice_add_fusion), channel_id=1, source_target_pairs={{0,2},{1,3},{2,0},{3,1},{4,6},{5,7},{6,4},{7,5},{8,10},{9,11},{10,... | collective-permute-start | bytes 688136 | tf_op jit(solution)/shard_map/ppermute | solution.py:21
  48.9 1.3 slice_bitcast_fusion.gate_ref
  50.2 4.6 %shard_map.83.acc_ref = f32[4096,64]{1,0:T(8,128)} custom-call(bf16[4096,64]{1,0:T(8,128)(2,1)} %get-tuple-element.10.lhs_ref, bf16[64,4096]{1,0:T(8,128)(2,1)} %copy.25.rhs_ref, bf16[4096,64]{1,0:T(8,128)(2,1)} %copy-done.1, f32[8,128]{1,0:T(8,128)} %slice_bitcast_fusion.gate_ref, f32[4096,64]{1,0:T(8,128)} %shard_map.82.acc_ref), custom_call_target="tpu_custom_call", output_to_operand_aliasing={{}: (4, {})} | custom-call | tf_op jit(solution)/shard_map/pallas_call | solution.py:62
  54.7 0.8 slice_dynamic-update-slice_fusion.6
  55.5 0.0 collective-permute-done.1
  55.5 3.4 %collective-permute-start.2 = (f32[6,64,128]{2,1,0:T(8,128)S(1)}, f32[6,64,128]{2,1,0:T(8,128)S(1)}, u32[]{:S(2)}, u32[]{:S(2)}) collective-permute-start(f32[6,64,128]{2,1,0:T(8,128)S(1)} %slice_add_fusion.1), channel_id=1, source_target_pairs={{0,4},{1,5},{2,6},{3,7},{4,0},{5,1},{6,2},{7,3},{8,12},{9,13},{10,... | collective-permute-start | bytes 589832 | tf_op jit(solution)/shard_map/ppermute | solution.py:21
  58.9 0.6 slice_bitcast_fusion.1.gate_ref
  59.5 4.6 %shard_map.84.acc_ref = f32[4096,64]{1,0:T(8,128)} custom-call(bf16[4096,64]{1,0:T(8,128)(2,1)} %get-tuple-element.10.lhs_ref, bf16[64,4096]{1,0:T(8,128)(2,1)} %copy.25.rhs_ref, bf16[4096,64]{1,0:T(8,128)(2,1)} %copy-done.1, f32[8,128]{1,0:T(8,128)} %slice_bitcast_fusion.1.gate_ref, f32[4096,64]{1,0:T(8,128)} %shard_map.83.acc_ref), custom_call_target="tpu_custom_call", output_to_operand_aliasing={{}: (4, {})} | custom-call | tf_op jit(solution)/shard_map/pallas_call | solution.py:62
  64.1 4.3 %collective-permute-done.2 = f32[6,64,128]{2,1,0:T(8,128)S(1)} collective-permute-done((f32[6,64,128]{2,1,0:T(8,128)S(1)}, f32[6,64,128]{2,1,0:T(8,128)S(1)}, u32[]{:S(2)}, u32[]{:S(2)}) %collective-permute-start.2) | collective-permute-done | bytes 196640 | tf_op jit(solution)/shard_map/ppermute | solution.py:21
  68.4 5.7 %collective-permute-start.3 = (f32[5,64,128]{2,1,0:T(8,128)S(1)}, f32[5,64,128]{2,1,0:T(8,128)S(1)}, u32[]{:S(2)}, u32[]{:S(2)}) collective-permute-start(f32[5,64,128]{2,1,0:T(8,128)S(1)} %slice_add_fusion.2), channel_id=1, source_target_pairs={{0,8},{1,9},{2,10},{3,11},{4,12},{5,13},{6,14},{7,15},{8,0},{9,1},... | collective-permute-start | bytes 491528 | tf_op jit(solution)/shard_map/ppermute | solution.py:21
  74.2 0.6 slice_bitcast_fusion.2.gate_ref
  74.7 4.6 %shard_map.85.acc_ref = f32[4096,64]{1,0:T(8,128)} custom-call(bf16[4096,64]{1,0:T(8,128)(2,1)} %get-tuple-element.10.lhs_ref, bf16[64,4096]{1,0:T(8,128)(2,1)} %copy.25.rhs_ref, bf16[4096,64]{1,0:T(8,128)(2,1)} %copy-done.1, f32[8,128]{1,0:T(8,128)} %slice_bitcast_fusion.2.gate_ref, f32[4096,64]{1,0:T(8,128)} %shard_map.84.acc_ref), custom_call_target="tpu_custom_call", output_to_operand_aliasing={{}: (4, {})} | custom-call | tf_op jit(solution)/shard_map/pallas_call | solution.py:62
  79.3 1.9 %collective-permute-done.3 = f32[5,64,128]{2,1,0:T(8,128)S(1)} collective-permute-done((f32[5,64,128]{2,1,0:T(8,128)S(1)}, f32[5,64,128]{2,1,0:T(8,128)S(1)}, u32[]{:S(2)}, u32[]{:S(2)}) %collective-permute-start.3) | collective-permute-done | bytes 163872 | tf_op jit(solution)/shard_map/ppermute | solution.py:21
  81.2 1.1 collective-permute-start.4
  82.4 0.6 slice_bitcast_fusion.3.gate_ref
  83.0 4.6 %shard_map.86.acc_ref = f32[4096,64]{1,0:T(8,128)} custom-call(bf16[4096,64]{1,0:T(8,128)(2,1)} %get-tuple-element.10.lhs_ref, bf16[64,4096]{1,0:T(8,128)(2,1)} %copy.25.rhs_ref, bf16[4096,64]{1,0:T(8,128)(2,1)} %copy-done.1, f32[8,128]{1,0:T(8,128)} %slice_bitcast_fusion.3.gate_ref, f32[4096,64]{1,0:T(8,128)} %shard_map.85.acc_ref), custom_call_target="tpu_custom_call", output_to_operand_aliasing={{}: (4, {})} | custom-call | tf_op jit(solution)/shard_map/pallas_call | solution.py:62
  87.5 0.0 collective-permute-done.4
  87.6 1.1 collective-permute-start.5
  88.6 0.6 slice_bitcast_fusion.4.gate_ref
  89.2 4.6 %shard_map.87.acc_ref = f32[4096,64]{1,0:T(8,128)} custom-call(bf16[4096,64]{1,0:T(8,128)(2,1)} %get-tuple-element.10.lhs_ref, bf16[64,4096]{1,0:T(8,128)(2,1)} %copy.25.rhs_ref, bf16[4096,64]{1,0:T(8,128)(2,1)} %copy-done.1, f32[8,128]{1,0:T(8,128)} %slice_bitcast_fusion.4.gate_ref, f32[4096,64]{1,0:T(8,128)} %shard_map.86.acc_ref), custom_call_target="tpu_custom_call", output_to_operand_aliasing={{}: (4, {})} | custom-call | tf_op jit(solution)/shard_map/pallas_call | solution.py:62
  93.8 0.0 collective-permute-done.5
  93.8 1.8 %collective-permute-start.6 = (f32[2,64,128]{2,1,0:T(8,128)S(1)}, f32[2,64,128]{2,1,0:T(8,128)S(1)}, u32[]{:S(2)}, u32[]{:S(2)}) collective-permute-start(f32[2,64,128]{2,1,0:T(8,128)S(1)} %slice_add_fusion.5), channel_id=1, source_target_pairs={{0,64},{1,65},{2,66},{3,67},{4,68},{5,69},{6,70},{7,71},{8,72},{9,... | collective-permute-start | bytes 196616 | tf_op jit(solution)/shard_map/ppermute | solution.py:21
  95.6 0.6 slice_bitcast_fusion.5.gate_ref
  96.2 4.6 %shard_map.88.acc_ref = f32[4096,64]{1,0:T(8,128)} custom-call(bf16[4096,64]{1,0:T(8,128)(2,1)} %get-tuple-element.10.lhs_ref, bf16[64,4096]{1,0:T(8,128)(2,1)} %copy.25.rhs_ref, bf16[4096,64]{1,0:T(8,128)(2,1)} %copy-done.1, f32[8,128]{1,0:T(8,128)} %slice_bitcast_fusion.5.gate_ref, f32[4096,64]{1,0:T(8,128)} %shard_map.87.acc_ref), custom_call_target="tpu_custom_call", output_to_operand_aliasing={{}: (4, {})} | custom-call | tf_op jit(solution)/shard_map/pallas_call | solution.py:62
  100.8 0.0 collective-permute-done.6
  100.8 3.0 %collective-permute-start.7 = (f32[1,64,128]{2,1,0:T(8,128)S(1)}, f32[1,64,128]{2,1,0:T(8,128)S(1)}, u32[]{:S(2)}, u32[]{:S(2)}) collective-permute-start(f32[1,64,128]{2,1,0:T(8,128)S(1)} %get-tuple-element.18), channel_id=1, source_target_pairs={{0,128},{1,129},{2,130},{3,131},{4,132},{5,133},{6,134},{7,135},{8... | collective-permute-start | bytes 98312 | tf_op jit(solution)/shard_map/ppermute | solution.py:21
  103.8 0.6 slice_bitcast_fusion.6.gate_ref
  104.4 4.6 %shard_map.89 = f32[4096,64]{1,0:T(8,128)} custom-call(bf16[4096,64]{1,0:T(8,128)(2,1)} %get-tuple-element.10.lhs_ref, bf16[64,4096]{1,0:T(8,128)(2,1)} %copy.25.rhs_ref, bf16[4096,64]{1,0:T(8,128)(2,1)} %copy-done.1, f32[8,128]{1,0:T(8,128)} %slice_bitcast_fusion.6.gate_ref, f32[4096,64]{1,0:T(8,128)} %shard_map.88.acc_ref), custom_call_target="tpu_custom_call", output_to_operand_aliasing={{}: (4, {})} | custom-call | tf_op jit(solution)/shard_map/pallas_call | solution.py:62
  108.9 0.0 collective-permute-done.7
  108.9 0.0 copy-done.5
  109.0 5.4 %fusion.15 = bf16[4096,64]{1,0:T(8,128)(2,1)S(1)} fusion(f32[4096,64]{1,0:T(8,128)} %shard_map.89, f32[2,2048,64]{2,1,0:T(8,128)S(1)} %copy.26, pred[4096]{0:T(1024)(128)(4,1)S(1)} %fusion.32, bf16[9,4096,128]{2,1,0:T(8,128)(2,1)} %param.12, f32[8,64,128]{2,1,0:T(8,128)S(1)} %constant_dynamic-update-slice_fusion, f32[8,128]{1,0:T(8,128)S(1)} %slice_multiply_fusion.11, ...), kind=kOutput, calls=%fused_computation.16 | convolution fusion | flops 538116096 | bytes 12328992 | tf_op jit(solution)/shard_map/lrk,lpk->rp/dot_general | solution.py:160
  114.3 15.8 %fusion.12 = bf16[4096,64]{0,1:T(8,128)(2,1)} fusion(bf16[4096,64]{1,0:T(8,128)(2,1)S(1)} %fusion.15, s32[4096]{0:T(1024)S(1)} %bitcast.59), kind=kOutput, calls=%fused_computation.11 | convolution fusion | flops 2164523008 | bytes 1064960 | tf_op jit(solution)/shard_map/dot_general | solution.py:164
  (29 shorter events, 0.2 us)
Async XLA Ops:
  0.0 1.3 %copy-start = (s32[2]{0:T(128)S(1)}, s32[2]{0:T(128)}, u32[]{:S(2)}) copy-start(s32[2]{0:T(128)} %param.11) | copy-start | bytes 28
  0.0 1.9 %copy-start.4 = (s32[1,4096]{1,0:T(1,128)S(1)}, s32[1,4096]{1,0:T(1,128)}, u32[]{:S(2)}) copy-start(s32[1,4096]{1,0:T(1,128)} %param.10) | copy-start | bytes 49156
  0.0 1.9 %copy-start.3 = (bf16[4096,64]{0,1:T(8,128)(2,1)S(1)}, bf16[4096,64]{0,1:T(8,128)(2,1)}, u32[]{:S(2)}) copy-start(bf16[4096,64]{0,1:T(8,128)(2,1)} %param.8) | copy-start | bytes 1572868
  1.5 15.5 %slice-start = ((s8[9437184]{0:T(1024)(128)(4,1)}), s8[1048576]{0:T(1024)(128)(4,1)S(1)}, s32[]{:S(2)}) async-start(s8[9437184]{0:T(1024)(128)(4,1)} %bitcast.51), calls=%async_computation | async-start | bytes 2097152
  2.0 15.0 %slice-start.1 = ((s8[9437184]{0:T(1024)(128)(4,1)}), s8[4194304]{0:T(1024)(128)(4,1)S(1)}, s32[]{:S(2)}) async-start(s8[9437184]{0:T(1024)(128)(4,1)} %bitcast.51), calls=%async_computation.1 | async-start | bytes 8388608
  2.0 15.0 %slice-start.2 = ((s8[9437184]{0:T(1024)(128)(4,1)}), s8[4194304]{0:T(1024)(128)(4,1)S(1)}, s32[]{:S(2)}) async-start(s8[9437184]{0:T(1024)(128)(4,1)} %bitcast.51), calls=%async_computation.2 | async-start | bytes 8388608
  16.9 6.4 %copy-start.1 = (bf16[4096,64]{1,0:T(8,128)(2,1)}, bf16[4096,64]{1,0:T(8,128)(2,1)S(1)}, u32[]{:S(2)}) copy-start(bf16[4096,64]{1,0:T(8,128)(2,1)S(1)} %get-tuple-element.9.vec_ref) | copy-start | bytes 1572868
  18.6 27.3 %collective-permute-start = (f32[8,64,128]{2,1,0:T(8,128)S(1)}, f32[8,64,128]{2,1,0:T(8,128)}, u32[]{:S(2)}, u32[]{:S(2)}) collective-permute-start(f32[8,64,128]{2,1,0:T(8,128)S(1)} %fusion.16), channel_id=1, source_target_pairs={{0,1},{1,0},{2,3},{3,2},{4,5},{5,4},{6,7},{7,6},{8,9},{9,8},{10,11... | collective-permute-start | bytes 786440 | tf_op jit(solution)/shard_map/ppermute | solution.py:21
  22.7 0.7 copy-start.2
  46.9 8.6 %collective-permute-start.1 = (f32[7,64,128]{2,1,0:T(8,128)S(1)}, f32[7,64,128]{2,1,0:T(8,128)S(1)}, u32[]{:S(2)}, u32[]{:S(2)}) collective-permute-start(f32[7,64,128]{2,1,0:T(8,128)S(1)} %slice_add_fusion), channel_id=1, source_target_pairs={{0,2},{1,3},{2,0},{3,1},{4,6},{5,7},{6,4},{7,5},{8,10},{9,11},{10,... | collective-permute-start | bytes 688136 | tf_op jit(solution)/shard_map/ppermute | solution.py:21
  55.5 12.9 %collective-permute-start.2 = (f32[6,64,128]{2,1,0:T(8,128)S(1)}, f32[6,64,128]{2,1,0:T(8,128)S(1)}, u32[]{:S(2)}, u32[]{:S(2)}) collective-permute-start(f32[6,64,128]{2,1,0:T(8,128)S(1)} %slice_add_fusion.1), channel_id=1, source_target_pairs={{0,4},{1,5},{2,6},{3,7},{4,0},{5,1},{6,2},{7,3},{8,12},{9,13},{10,... | collective-permute-start | bytes 589832 | tf_op jit(solution)/shard_map/ppermute | solution.py:21
  68.4 12.8 %collective-permute-start.3 = (f32[5,64,128]{2,1,0:T(8,128)S(1)}, f32[5,64,128]{2,1,0:T(8,128)S(1)}, u32[]{:S(2)}, u32[]{:S(2)}) collective-permute-start(f32[5,64,128]{2,1,0:T(8,128)S(1)} %slice_add_fusion.2), channel_id=1, source_target_pairs={{0,8},{1,9},{2,10},{3,11},{4,12},{5,13},{6,14},{7,15},{8,0},{9,1},... | collective-permute-start | bytes 491528 | tf_op jit(solution)/shard_map/ppermute | solution.py:21
  81.2 6.3 %collective-permute-start.4 = (f32[4,64,128]{2,1,0:T(8,128)S(1)}, f32[4,64,128]{2,1,0:T(8,128)S(1)}, u32[]{:S(2)}, u32[]{:S(2)}) collective-permute-start(f32[4,64,128]{2,1,0:T(8,128)S(1)} %slice_add_fusion.3), channel_id=1, source_target_pairs={{0,16},{1,17},{2,18},{3,19},{4,20},{5,21},{6,22},{7,23},{8,24},{9,... | collective-permute-start | bytes 393224 | tf_op jit(solution)/shard_map/ppermute | solution.py:21
  87.6 6.2 %collective-permute-start.5 = (f32[3,64,128]{2,1,0:T(8,128)S(1)}, f32[3,64,128]{2,1,0:T(8,128)S(1)}, u32[]{:S(2)}, u32[]{:S(2)}) collective-permute-start(f32[3,64,128]{2,1,0:T(8,128)S(1)} %slice_add_fusion.4), channel_id=1, source_target_pairs={{0,32},{1,33},{2,34},{3,35},{4,36},{5,37},{6,38},{7,39},{8,40},{9,... | collective-permute-start | bytes 294920 | tf_op jit(solution)/shard_map/ppermute | solution.py:21
  93.8 7.0 %collective-permute-start.6 = (f32[2,64,128]{2,1,0:T(8,128)S(1)}, f32[2,64,128]{2,1,0:T(8,128)S(1)}, u32[]{:S(2)}, u32[]{:S(2)}) collective-permute-start(f32[2,64,128]{2,1,0:T(8,128)S(1)} %slice_add_fusion.5), channel_id=1, source_target_pairs={{0,64},{1,65},{2,66},{3,67},{4,68},{5,69},{6,70},{7,71},{8,72},{9,... | collective-permute-start | bytes 196616 | tf_op jit(solution)/shard_map/ppermute | solution.py:21
  100.8 8.1 %collective-permute-start.7 = (f32[1,64,128]{2,1,0:T(8,128)S(1)}, f32[1,64,128]{2,1,0:T(8,128)S(1)}, u32[]{:S(2)}, u32[]{:S(2)}) collective-permute-start(f32[1,64,128]{2,1,0:T(8,128)S(1)} %get-tuple-element.18), channel_id=1, source_target_pairs={{0,128},{1,129},{2,130},{3,131},{4,132},{5,133},{6,134},{7,135},{8... | collective-permute-start | bytes 98312 | tf_op jit(solution)/shard_map/ppermute | solution.py:21
  104.4 4.6 %copy-start.5 = (f32[8]{0:T(128)S(1)}, f32[8]{0:T(128)}, u32[]{:S(2)}) copy-start(f32[8]{0:T(128)} %constant.38.clone) | copy-start | bytes 100

commit v2 on v1

--- a/solution.py
+++ b/solution.py
@@ -50,7 +50,9 @@
 
 def dense_kernel(lhs_ref, rhs_ref, vec_ref, gate_ref, acc_ref, out_ref):
     del gate_ref, acc_ref
-    squared = jnp.dot(lhs_ref[...], rhs_ref[...], preferred_element_type=jnp.float32)
+    squared = lax.dot_general(
+        lhs_ref[...], rhs_ref[...], (((1,), (1,)), ((), ())), preferred_element_type=jnp.float32
+    )
     scaled = root_three * jnp.sqrt(jnp.maximum(squared, 0.0))
     kernel = ((1.0 + scaled) * jnp.exp(-scaled)).astype(jnp.bfloat16)
     out_ref[...] = jnp.dot(kernel, vec_ref[...], preferred_element_type=jnp.float32)
@@ -64,7 +66,7 @@
         grid=(rows // BLOCK,),
         in_specs=[
             pl.BlockSpec((BLOCK, FEATURES), lambda i: (first + i, 0)),
-            pl.BlockSpec((FEATURES, LEAF), lambda i: (0, leaf)),
+            pl.BlockSpec((LEAF, FEATURES), lambda i: (leaf, 0)),
             pl.BlockSpec((LEAF, PANEL), lambda i: (leaf, 0)),
             pl.BlockSpec(memory_space=pl.ANY),
             pl.BlockSpec(memory_space=pl.ANY),
@@ -102,7 +104,7 @@
     ones = lhs[:, 6 * DIM + 3 : 6 * DIM + 6]
     rhs = jnp.concatenate(
         [high, middle, high, middle, low, high, ones, norm_parts, lhs[:, 6 * DIM + 6 :]], axis=1
-    ).T
+    )
     slot_limit = jnp.repeat(live_counts, LEAF)
     within = jnp.arange(per_device, dtype=jnp.int32) % LEAF
     live_rows = (within < slot_limit)[:, None]

time: 132 us -> 133 us (level)
    dot_general x1, local copies, waits for them, and re-layouts: 0.6 us -> 3.18 us  [body(): jnp.einsum('nrk,npk->nrp', basis_nodes, weights, preferred_element_type=j...]
    transpose x1 -> x0, local copies, waits for them, and re-layouts: 2.34 us -> none  [body(): rhs = jnp.concatenate([high, middle, high, middle, low, high, ones, norm_...]
  transfers between devices with their start and end apart: 8 -> 8, of which waited for: 2 -> 2; matrix products, arithmetic and copies ran while one was open for 21% -> 21% of each run, Pallas kernels for 28% -> 29%
where the time goes in v2:
time: 133 us; the launch traced here: 131 us
  Pallas kernels  37.8 us (28%)
  matrix products  36.7 us (28%)
  local copies, waits for them, and re-layouts  24.9 us (19%)
  starting transfers between devices  18.3 us (14%)
  other arithmetic  7.18 us (5%)
  waiting for transfers between devices  6.2 us (5%)
    pallas_call x8, Pallas kernels, dense_rows(): pl.pallas_call(dense_kernel, grid=(rows // BLOCK,), in_specs=[pl.BlockSpe...  37.8 us
    ppermute x8, starting transfers between devices, swapped(): lax.ppermute(x, axis, [(i, i ^ 1 << bit) for i in range(lax.axis_size(axi...  18.3 us
    dot_general x1, matrix products, body(): lax.dot_general(onehot, result, (((0,), (0,)), ((), ())), preferred_eleme...  15.8 us
    dot_general x1, matrix products, body(): lax.dot_general(onehot, jnp.concatenate([vectors, lhs_features], axis=1),...  12 us
    concatenate x1, local copies, waits for them, and re-layouts, body(): jnp.concatenate([high, middle, high, middle, low, high, ones, norm_parts,...  10.4 us
    ppermute x8, waiting for transfers between devices, swapped(): lax.ppermute(x, axis, [(i, i ^ 1 << bit) for i in range(lax.axis_size(axi...  6.2 us
    dot_general x1, matrix products, body(): jnp.einsum('lrk,lpk->rp', level_bases[local_levels:], weights, preferred_...  5.37 us
    squeeze x7, local copies, waits for them, and re-layouts, body(): gate = received[0, :8]  4.83 us
  transfers between devices with their start and end apart: 8, of which 2 were waited for; matrix products, arithmetic and copies ran while one was open for 21% of the time, Pallas kernels for 29%

profile of v2, /device:TPU:6, one launch (start us, length us, event | category | flops | bytes accessed | tf_op | source)
XLA Modules:
  0.0 131.3 jit_solution(14174122829965824327)
XLA Ops:
  0.0 0.0 copy-start
  0.0 1.1 fusion.28
  1.1 0.2 fusion.31
  1.3 0.0 copy-done
  1.3 0.1 broadcast_bitcast_fusion
  1.5 0.0 slice-start
  1.5 0.5 concatenate.9
  1.9 0.0 copy-done.5
  1.9 0.0 copy-done.4
  2.0 0.0 slice-start.1
  2.0 0.0 slice-start.2
  2.0 12.0 %fusion.11 = bf16[4096,128]{1,0:T(8,128)(2,1)S(1)} fusion(s32[4096]{0:T(1024)S(1)} %bitcast.56, bf16[4096,64]{0,1:T(8,128)(2,1)S(1)} %bitcast.54, bf16[4096,64]{0,1:T(8,128)(2,1)S(1)} %copy-done.4), kind=kOutput, calls=%fused_computation.10 | convolution fusion | flops 4314365952 | bytes 2113536 | tf_op jit(solution)/shard_map/dot_general | solution.py:91
  14.0 2.9 %slice_select_fusion = (bf16[4096,64]{1,0:T(8,128)(2,1)S(1)}, bf16[4096,64]{1,0:T(8,128)(2,1)}) fusion(bf16[4096,128]{1,0:T(8,128)(2,1)S(1)} %fusion.11, pred[4096]{0:T(1024)(128)(4,1)S(1)} %fusion.32), kind=kLoop, calls=%fused_computation.18 | loop fusion | flops 262144 | bytes 2101248 | tf_op jit(solution)/shard_map/jit(_where)/select_n | solution.py:111
  17.0 0.0 slice-done
  17.0 0.0 slice-done.1
  17.0 1.6 %fusion.16 = f32[8,64,128]{2,1,0:T(8,128)S(1)} fusion(bf16[9,4096,128]{2,1,0:T(8,128)(2,1)S(1)} %bitcast.51, bf16[4096,64]{1,0:T(8,128)(2,1)S(1)} %get-tuple-element.9.vec_ref), kind=kOutput, calls=%fused_computation.17 | convolution fusion | flops 536870912 | bytes 9699328 | tf_op jit(solution)/shard_map/rp,lrk->lpk/dot_general | solution.py:113
  18.6 0.3 collective-permute-start
  18.9 1.9 %slice_multiply_fusion = (bf16[4096,8]{1,0:T(8,128)(2,1)}, bf16[4096,8]{1,0:T(8,128)(2,1)S(1)}, bf16[4096,8]{1,0:T(8,128)(2,1)S(1)}) fusion(bf16[4096,128]{1,0:T(8,128)(2,1)S(1)} %fusion.11), kind=kLoop, calls=%fused_computation.19 | loop fusion | flops 98304 | bytes 393216 | tf_op jit(solution)/shard_map/mul | solution.py:102
  20.7 2.0 %fusion.45 = (bf16[4096,3]{1,0:T(8,128)(2,1)}, bf16[4096,3]{1,0:T(8,128)(2,1)}) fusion(bf16[4096,128]{1,0:T(8,128)(2,1)S(1)} %fusion.11), kind=kLoop, calls=%fused_computation.91 | loop fusion | bytes 98304 | tf_op jit(solution)/shard_map/slice | solution.py:103
  22.7 0.1 slice.195
  22.8 0.6 copy-done.3
  23.4 0.5 fusion.46
  23.9 1.4 %convolution_bitcast_fusion = f32[2,2048,64]{1,2,0:T(8,128)} fusion(bf16[2,64,128]{2,1,0:T(8,128)(2,1)S(1)} %multiply_convert_fusion.4, bf16[2,2048,128]{2,1,0:T(8,128)(2,1)S(1)} %bitcast.53), kind=kOutput, calls=%fused_computation.12 | convolution fusion | flops 67108864 | bytes 2129920 | tf_op jit(solution)/shard_map/nrk,npk->nrp/dot_general | solution.py:150
  25.4 0.4 slice.221
  25.7 3.2 %copy.18 = f32[2,2048,64]{2,1,0:T(8,128)} copy(f32[2,2048,64]{1,2,0:T(8,128)} %convolution_bitcast_fusion) | data formatting | bytes 2097152 | tf_op jit(solution)/shard_map/nrk,npk->nrp/dot_general | solution.py:150
  28.9 10.4 %concatenate.11.rhs_ref = bf16[4096,64]{1,0:T(8,128)(2,1)} concatenate(bf16[4096,8]{1,0:T(8,128)(2,1)S(1)} %get-tuple-element.15, bf16[4096,8]{1,0:T(8,128)(2,1)S(1)} %get-tuple-element.14, bf16[4096,8]{1,0:T(8,128)(2,1)S(1)} %get-tuple-element.15, bf16[4096,8]{1,0:T(8,128)(2,1)S(1)} %get-tuple-element.14, bf16[4096,8]{1,0:T(8,128)(2,1)} %get-tuple-element.13, ...), dimensions={1} | concatenate | bytes 1048576 | tf_op jit(solution)/shard_map/concatenate | solution.py:105
  39.3 0.6 broadcast_in_dim.40.gate_ref
  39.9 1.4 %broadcast_5_acc_ref.2.acc_ref = f32[4096,64]{1,0:T(8,128)} broadcast(f32[]{:T(128)} %constant.35.clone.1), dimensions={} | broadcast | bytes 1048580 | tf_op jit(solution)/shard_map/broadcast.5.acc_ref
  41.4 4.7 %shard_map.82.acc_ref = f32[4096,64]{1,0:T(8,128)} custom-call(bf16[4096,64]{1,0:T(8,128)(2,1)} %get-tuple-element.10.lhs_ref, bf16[4096,64]{1,0:T(8,128)(2,1)} %concatenate.11.rhs_ref, bf16[4096,64]{1,0:T(8,128)(2,1)} %copy-done.1, f32[8,128]{1,0:T(8,128)} %broadcast_in_dim.40.gate_ref, ...), custom_call_target="tpu_custom_call", output_to_operand_aliasing={{}: (4, {})} | custom-call | tf_op jit(solution)/shard_map/pallas_call | solution.py:64
  46.1 0.0 collective-permute-done
  46.1 1.0 slice_add_fusion
  47.1 2.0 %collective-permute-start.1 = (f32[7,64,128]{2,1,0:T(8,128)S(1)}, f32[7,64,128]{2,1,0:T(8,128)S(1)}, u32[]{:S(2)}, u32[]{:S(2)}) collective-permute-start(f32[7,64,128]{2,1,0:T(8,128)S(1)} %slice_add_fusion), channel_id=1, source_target_pairs={{0,2},{1,3},{2,0},{3,1},{4,6},{5,7},{6,4},{7,5},{8,10},{9,11},{10,... | collective-permute-start | bytes 688136 | tf_op jit(solution)/shard_map/ppermute | solution.py:21
  49.1 1.3 slice_bitcast_fusion.gate_ref
  50.4 4.7 %shard_map.83.acc_ref = f32[4096,64]{1,0:T(8,128)} custom-call(bf16[4096,64]{1,0:T(8,128)(2,1)} %get-tuple-element.10.lhs_ref, bf16[4096,64]{1,0:T(8,128)(2,1)} %concatenate.11.rhs_ref, bf16[4096,64]{1,0:T(8,128)(2,1)} %copy-done.1, f32[8,128]{1,0:T(8,128)} %slice_bitcast_fusion.gate_ref, f32[4096,64]{1,0:T(8,128)} %shard_map.82.acc_ref), custom_call_target="tpu_custom_call", output_to_operand_aliasing={{}: (4, {})} | custom-call | tf_op jit(solution)/shard_map/pallas_call | solution.py:64
  55.1 0.8 slice_dynamic-update-slice_fusion.6
  55.8 0.0 collective-permute-done.1
  55.8 3.3 %collective-permute-start.2 = (f32[6,64,128]{2,1,0:T(8,128)S(1)}, f32[6,64,128]{2,1,0:T(8,128)S(1)}, u32[]{:S(2)}, u32[]{:S(2)}) collective-permute-start(f32[6,64,128]{2,1,0:T(8,128)S(1)} %slice_add_fusion.1), channel_id=1, source_target_pairs={{0,4},{1,5},{2,6},{3,7},{4,0},{5,1},{6,2},{7,3},{8,12},{9,13},{10,... | collective-permute-start | bytes 589832 | tf_op jit(solution)/shard_map/ppermute | solution.py:21
  59.2 0.6 slice_bitcast_fusion.1.gate_ref
  59.8 4.7 %shard_map.84.acc_ref = f32[4096,64]{1,0:T(8,128)} custom-call(bf16[4096,64]{1,0:T(8,128)(2,1)} %get-tuple-element.10.lhs_ref, bf16[4096,64]{1,0:T(8,128)(2,1)} %concatenate.11.rhs_ref, bf16[4096,64]{1,0:T(8,128)(2,1)} %copy-done.1, f32[8,128]{1,0:T(8,128)} %slice_bitcast_fusion.1.gate_ref, f32[4096,64]{1,0:T(8,128)} %shard_map.83.acc_ref), custom_call_target="tpu_custom_call", output_to_operand_aliasing={{}: (4, {})} | custom-call | tf_op jit(solution)/shard_map/pallas_call | solution.py:64
  64.5 4.2 %collective-permute-done.2 = f32[6,64,128]{2,1,0:T(8,128)S(1)} collective-permute-done((f32[6,64,128]{2,1,0:T(8,128)S(1)}, f32[6,64,128]{2,1,0:T(8,128)S(1)}, u32[]{:S(2)}, u32[]{:S(2)}) %collective-permute-start.2) | collective-permute-done | bytes 196640 | tf_op jit(solution)/shard_map/ppermute | solution.py:21
  68.7 5.7 %collective-permute-start.3 = (f32[5,64,128]{2,1,0:T(8,128)S(1)}, f32[5,64,128]{2,1,0:T(8,128)S(1)}, u32[]{:S(2)}, u32[]{:S(2)}) collective-permute-start(f32[5,64,128]{2,1,0:T(8,128)S(1)} %slice_add_fusion.2), channel_id=1, source_target_pairs={{0,8},{1,9},{2,10},{3,11},{4,12},{5,13},{6,14},{7,15},{8,0},{9,1},... | collective-permute-start | bytes 491528 | tf_op jit(solution)/shard_map/ppermute | solution.py:21
  74.5 0.6 slice_bitcast_fusion.2.gate_ref
  75.0 4.7 %shard_map.85.acc_ref = f32[4096,64]{1,0:T(8,128)} custom-call(bf16[4096,64]{1,0:T(8,128)(2,1)} %get-tuple-element.10.lhs_ref, bf16[4096,64]{1,0:T(8,128)(2,1)} %concatenate.11.rhs_ref, bf16[4096,64]{1,0:T(8,128)(2,1)} %copy-done.1, f32[8,128]{1,0:T(8,128)} %slice_bitcast_fusion.2.gate_ref, f32[4096,64]{1,0:T(8,128)} %shard_map.84.acc_ref), custom_call_target="tpu_custom_call", output_to_operand_aliasing={{}: (4, {})} | custom-call | tf_op jit(solution)/shard_map/pallas_call | solution.py:64
  79.8 1.9 %collective-permute-done.3 = f32[5,64,128]{2,1,0:T(8,128)S(1)} collective-permute-done((f32[5,64,128]{2,1,0:T(8,128)S(1)}, f32[5,64,128]{2,1,0:T(8,128)S(1)}, u32[]{:S(2)}, u32[]{:S(2)}) %collective-permute-start.3) | collective-permute-done | bytes 163872 | tf_op jit(solution)/shard_map/ppermute | solution.py:21
  81.7 1.1 collective-permute-start.4
  82.9 0.6 slice_bitcast_fusion.3.gate_ref
  83.5 4.7 %shard_map.86.acc_ref = f32[4096,64]{1,0:T(8,128)} custom-call(bf16[4096,64]{1,0:T(8,128)(2,1)} %get-tuple-element.10.lhs_ref, bf16[4096,64]{1,0:T(8,128)(2,1)} %concatenate.11.rhs_ref, bf16[4096,64]{1,0:T(8,128)(2,1)} %copy-done.1, f32[8,128]{1,0:T(8,128)} %slice_bitcast_fusion.3.gate_ref, f32[4096,64]{1,0:T(8,128)} %shard_map.85.acc_ref), custom_call_target="tpu_custom_call", output_to_operand_aliasing={{}: (4, {})} | custom-call | tf_op jit(solution)/shard_map/pallas_call | solution.py:64
  88.2 0.0 collective-permute-done.4
  88.2 0.8 collective-permute-start.5
  89.0 0.6 slice_bitcast_fusion.4.gate_ref
  89.6 4.7 %shard_map.87.acc_ref = f32[4096,64]{1,0:T(8,128)} custom-call(bf16[4096,64]{1,0:T(8,128)(2,1)} %get-tuple-element.10.lhs_ref, bf16[4096,64]{1,0:T(8,128)(2,1)} %concatenate.11.rhs_ref, bf16[4096,64]{1,0:T(8,128)(2,1)} %copy-done.1, f32[8,128]{1,0:T(8,128)} %slice_bitcast_fusion.4.gate_ref, f32[4096,64]{1,0:T(8,128)} %shard_map.86.acc_ref), custom_call_target="tpu_custom_call", output_to_operand_aliasing={{}: (4, {})} | custom-call | tf_op jit(solution)/shard_map/pallas_call | solution.py:64
  94.4 0.0 collective-permute-done.5
  94.4 2.0 %collective-permute-start.6 = (f32[2,64,128]{2,1,0:T(8,128)S(1)}, f32[2,64,128]{2,1,0:T(8,128)S(1)}, u32[]{:S(2)}, u32[]{:S(2)}) collective-permute-start(f32[2,64,128]{2,1,0:T(8,128)S(1)} %slice_add_fusion.5), channel_id=1, source_target_pairs={{0,64},{1,65},{2,66},{3,67},{4,68},{5,69},{6,70},{7,71},{8,72},{9,... | collective-permute-start | bytes 196616 | tf_op jit(solution)/shard_map/ppermute | solution.py:21
  96.4 0.6 slice_bitcast_fusion.5.gate_ref
  97.0 4.7 %shard_map.88.acc_ref = f32[4096,64]{1,0:T(8,128)} custom-call(bf16[4096,64]{1,0:T(8,128)(2,1)} %get-tuple-element.10.lhs_ref, bf16[4096,64]{1,0:T(8,128)(2,1)} %concatenate.11.rhs_ref, bf16[4096,64]{1,0:T(8,128)(2,1)} %copy-done.1, f32[8,128]{1,0:T(8,128)} %slice_bitcast_fusion.5.gate_ref, f32[4096,64]{1,0:T(8,128)} %shard_map.87.acc_ref), custom_call_target="tpu_custom_call", output_to_operand_aliasing={{}: (4, {})} | custom-call | tf_op jit(solution)/shard_map/pallas_call | solution.py:64
  101.7 0.0 collective-permute-done.6
  101.7 3.0 %collective-permute-start.7 = (f32[1,64,128]{2,1,0:T(8,128)S(1)}, f32[1,64,128]{2,1,0:T(8,128)S(1)}, u32[]{:S(2)}, u32[]{:S(2)}) collective-permute-start(f32[1,64,128]{2,1,0:T(8,128)S(1)} %get-tuple-element.18), channel_id=1, source_target_pairs={{0,128},{1,129},{2,130},{3,131},{4,132},{5,133},{6,134},{7,135},{8... | collective-permute-start | bytes 98312 | tf_op jit(solution)/shard_map/ppermute | solution.py:21
  104.7 0.6 slice_bitcast_fusion.6.gate_ref
  105.3 4.8 %shard_map.89 = f32[4096,64]{1,0:T(8,128)} custom-call(bf16[4096,64]{1,0:T(8,128)(2,1)} %get-tuple-element.10.lhs_ref, bf16[4096,64]{1,0:T(8,128)(2,1)} %concatenate.11.rhs_ref, bf16[4096,64]{1,0:T(8,128)(2,1)} %copy-done.1, f32[8,128]{1,0:T(8,128)} %slice_bitcast_fusion.6.gate_ref, f32[4096,64]{1,0:T(8,128)} %shard_map.88.acc_ref), custom_call_target="tpu_custom_call", output_to_operand_aliasing={{}: (4, {})} | custom-call | tf_op jit(solution)/shard_map/pallas_call | solution.py:64
  110.1 0.0 collective-permute-done.7
  110.1 0.0 copy-done.2
  110.1 0.0 copy-done.6
  110.2 5.4 %fusion.15 = bf16[4096,64]{1,0:T(8,128)(2,1)S(1)} fusion(f32[4096,64]{1,0:T(8,128)} %shard_map.89, f32[2,2048,64]{2,1,0:T(8,128)S(1)} %copy-done.2, pred[4096]{0:T(1024)(128)(4,1)S(1)} %fusion.32, bf16[9,4096,128]{2,1,0:T(8,128)(2,1)} %param.12, f32[8,64,128]{2,1,0:T(8,128)S(1)} %constant_dynamic-update-slice_fusion, ...), kind=kOutput, calls=%fused_computation.16 | convolution fusion | flops 538116096 | bytes 12328992 | tf_op jit(solution)/shard_map/lrk,lpk->rp/dot_general | solution.py:162
  115.5 15.8 %fusion.12 = bf16[4096,64]{0,1:T(8,128)(2,1)} fusion(bf16[4096,64]{1,0:T(8,128)(2,1)S(1)} %fusion.15, s32[4096]{0:T(1024)S(1)} %bitcast.57), kind=kOutput, calls=%fused_computation.11 | convolution fusion | flops 2164523008 | bytes 1064960 | tf_op jit(solution)/shard_map/dot_general | solution.py:166
  (30 shorter events, 0.2 us)
Async XLA Ops:
  0.0 1.3 %copy-start = (s32[2]{0:T(128)S(1)}, s32[2]{0:T(128)}, u32[]{:S(2)}) copy-start(s32[2]{0:T(128)} %param.11) | copy-start | bytes 28
  0.0 1.9 %copy-start.5 = (s32[1,4096]{1,0:T(1,128)S(1)}, s32[1,4096]{1,0:T(1,128)}, u32[]{:S(2)}) copy-start(s32[1,4096]{1,0:T(1,128)} %param.10) | copy-start | bytes 49156
  0.0 1.9 %copy-start.4 = (bf16[4096,64]{0,1:T(8,128)(2,1)S(1)}, bf16[4096,64]{0,1:T(8,128)(2,1)}, u32[]{:S(2)}) copy-start(bf16[4096,64]{0,1:T(8,128)(2,1)} %param.8) | copy-start | bytes 1572868
  1.5 15.5 %slice-start = ((s8[9437184]{0:T(1024)(128)(4,1)}), s8[1048576]{0:T(1024)(128)(4,1)S(1)}, s32[]{:S(2)}) async-start(s8[9437184]{0:T(1024)(128)(4,1)} %bitcast.50), calls=%async_computation | async-start | bytes 2097152
  2.0 15.0 %slice-start.1 = ((s8[9437184]{0:T(1024)(128)(4,1)}), s8[4194304]{0:T(1024)(128)(4,1)S(1)}, s32[]{:S(2)}) async-start(s8[9437184]{0:T(1024)(128)(4,1)} %bitcast.50), calls=%async_computation.1 | async-start | bytes 8388608
  2.0 15.0 %slice-start.2 = ((s8[9437184]{0:T(1024)(128)(4,1)}), s8[4194304]{0:T(1024)(128)(4,1)S(1)}, s32[]{:S(2)}) async-start(s8[9437184]{0:T(1024)(128)(4,1)} %bitcast.50), calls=%async_computation.2 | async-start | bytes 8388608
  17.0 6.5 %copy-start.1 = (bf16[4096,64]{1,0:T(8,128)(2,1)}, bf16[4096,64]{1,0:T(8,128)(2,1)S(1)}, u32[]{:S(2)}) copy-start(bf16[4096,64]{1,0:T(8,128)(2,1)S(1)} %get-tuple-element.9.vec_ref) | copy-start | bytes 1572868
  18.6 27.5 %collective-permute-start = (f32[8,64,128]{2,1,0:T(8,128)S(1)}, f32[8,64,128]{2,1,0:T(8,128)}, u32[]{:S(2)}, u32[]{:S(2)}) collective-permute-start(f32[8,64,128]{2,1,0:T(8,128)S(1)} %fusion.16), channel_id=1, source_target_pairs={{0,1},{1,0},{2,3},{3,2},{4,5},{5,4},{6,7},{7,6},{8,9},{9,8},{10,11... | collective-permute-start | bytes 786440 | tf_op jit(solution)/shard_map/ppermute | solution.py:21
  22.7 0.7 copy-start.3
  47.1 8.8 %collective-permute-start.1 = (f32[7,64,128]{2,1,0:T(8,128)S(1)}, f32[7,64,128]{2,1,0:T(8,128)S(1)}, u32[]{:S(2)}, u32[]{:S(2)}) collective-permute-start(f32[7,64,128]{2,1,0:T(8,128)S(1)} %slice_add_fusion), channel_id=1, source_target_pairs={{0,2},{1,3},{2,0},{3,1},{4,6},{5,7},{6,4},{7,5},{8,10},{9,11},{10,... | collective-permute-start | bytes 688136 | tf_op jit(solution)/shard_map/ppermute | solution.py:21
  55.8 12.8 %collective-permute-start.2 = (f32[6,64,128]{2,1,0:T(8,128)S(1)}, f32[6,64,128]{2,1,0:T(8,128)S(1)}, u32[]{:S(2)}, u32[]{:S(2)}) collective-permute-start(f32[6,64,128]{2,1,0:T(8,128)S(1)} %slice_add_fusion.1), channel_id=1, source_target_pairs={{0,4},{1,5},{2,6},{3,7},{4,0},{5,1},{6,2},{7,3},{8,12},{9,13},{10,... | collective-permute-start | bytes 589832 | tf_op jit(solution)/shard_map/ppermute | solution.py:21
  68.7 13.0 %collective-permute-start.3 = (f32[5,64,128]{2,1,0:T(8,128)S(1)}, f32[5,64,128]{2,1,0:T(8,128)S(1)}, u32[]{:S(2)}, u32[]{:S(2)}) collective-permute-start(f32[5,64,128]{2,1,0:T(8,128)S(1)} %slice_add_fusion.2), channel_id=1, source_target_pairs={{0,8},{1,9},{2,10},{3,11},{4,12},{5,13},{6,14},{7,15},{8,0},{9,1},... | collective-permute-start | bytes 491528 | tf_op jit(solution)/shard_map/ppermute | solution.py:21
  81.7 6.5 %collective-permute-start.4 = (f32[4,64,128]{2,1,0:T(8,128)S(1)}, f32[4,64,128]{2,1,0:T(8,128)S(1)}, u32[]{:S(2)}, u32[]{:S(2)}) collective-permute-start(f32[4,64,128]{2,1,0:T(8,128)S(1)} %slice_add_fusion.3), channel_id=1, source_target_pairs={{0,16},{1,17},{2,18},{3,19},{4,20},{5,21},{6,22},{7,23},{8,24},{9,... | collective-permute-start | bytes 393224 | tf_op jit(solution)/shard_map/ppermute | solution.py:21
  88.2 6.2 %collective-permute-start.5 = (f32[3,64,128]{2,1,0:T(8,128)S(1)}, f32[3,64,128]{2,1,0:T(8,128)S(1)}, u32[]{:S(2)}, u32[]{:S(2)}) collective-permute-start(f32[3,64,128]{2,1,0:T(8,128)S(1)} %slice_add_fusion.4), channel_id=1, source_target_pairs={{0,32},{1,33},{2,34},{3,35},{4,36},{5,37},{6,38},{7,39},{8,40},{9,... | collective-permute-start | bytes 294920 | tf_op jit(solution)/shard_map/ppermute | solution.py:21
  94.4 7.3 %collective-permute-start.6 = (f32[2,64,128]{2,1,0:T(8,128)S(1)}, f32[2,64,128]{2,1,0:T(8,128)S(1)}, u32[]{:S(2)}, u32[]{:S(2)}) collective-permute-start(f32[2,64,128]{2,1,0:T(8,128)S(1)} %slice_add_fusion.5), channel_id=1, source_target_pairs={{0,64},{1,65},{2,66},{3,67},{4,68},{5,69},{6,70},{7,71},{8,72},{9,... | collective-permute-start | bytes 196616 | tf_op jit(solution)/shard_map/ppermute | solution.py:21
  101.7 8.4 %collective-permute-start.7 = (f32[1,64,128]{2,1,0:T(8,128)S(1)}, f32[1,64,128]{2,1,0:T(8,128)S(1)}, u32[]{:S(2)}, u32[]{:S(2)}) collective-permute-start(f32[1,64,128]{2,1,0:T(8,128)S(1)} %get-tuple-element.18), channel_id=1, source_target_pairs={{0,128},{1,129},{2,130},{3,131},{4,132},{5,133},{6,134},{7,135},{8... | collective-permute-start | bytes 98312 | tf_op jit(solution)/shard_map/ppermute | solution.py:21
  105.3 4.9 %copy-start.2 = (f32[2,2048,64]{2,1,0:T(8,128)S(1)}, f32[2,2048,64]{2,1,0:T(8,128)}, u32[]{:S(2)}) copy-start(f32[2,2048,64]{2,1,0:T(8,128)} %copy.18) | copy-start | bytes 3145732
  105.3 4.9 %copy-start.6 = (f32[8]{0:T(128)S(1)}, f32[8]{0:T(128)}, u32[]{:S(2)}) copy-start(f32[8]{0:T(128)} %constant.38.clone) | copy-start | bytes 100

commit v3 on v2

--- a/solution.py
+++ b/solution.py
@@ -48,25 +48,29 @@
     return lhs.T, rhs
 
 
-def dense_kernel(lhs_ref, rhs_ref, vec_ref, gate_ref, acc_ref, out_ref):
+def dense_kernel(rows_ref, leaf_ref, vec_ref, gate_ref, acc_ref, out_ref):
     del gate_ref, acc_ref
     squared = lax.dot_general(
-        lhs_ref[...], rhs_ref[...], (((1,), (1,)), ((), ())), preferred_element_type=jnp.float32
+        rows_ref[:, :FEATURES],
+        leaf_ref[:, FEATURES : 2 * FEATURES],
+        (((1,), (1,)), ((), ())),
+        preferred_element_type=jnp.float32,
     )
     scaled = root_three * jnp.sqrt(jnp.maximum(squared, 0.0))
     kernel = ((1.0 + scaled) * jnp.exp(-scaled)).astype(jnp.bfloat16)
     out_ref[...] = jnp.dot(kernel, vec_ref[...], preferred_element_type=jnp.float32)
 
 
-def dense_rows(acc, lhs, rhs, vec, gate, row_start, rows):
+def dense_rows(acc, table, vec, gate, row_start, rows):
     leaf = row_start // LEAF
     first = row_start // BLOCK
+    width = table.shape[1]
     return pl.pallas_call(
         dense_kernel,
         grid=(rows // BLOCK,),
         in_specs=[
-            pl.BlockSpec((BLOCK, FEATURES), lambda i: (first + i, 0)),
-            pl.BlockSpec((LEAF, FEATURES), lambda i: (leaf, 0)),
+            pl.BlockSpec((BLOCK, width), lambda i: (first + i, 0)),
+            pl.BlockSpec((LEAF, width), lambda i: (leaf, 0)),
             pl.BlockSpec((LEAF, PANEL), lambda i: (leaf, 0)),
             pl.BlockSpec(memory_space=pl.ANY),
             pl.BlockSpec(memory_space=pl.ANY),
@@ -74,7 +78,7 @@
         out_specs=pl.BlockSpec((BLOCK, PANEL), lambda i: (first + i, 0)),
         out_shape=jax.ShapeDtypeStruct(acc.shape, jnp.float32),
         input_output_aliases={4: 0},
-    )(lhs, rhs, vec, gate, acc)
+    )(table, table, vec, gate, acc)
 
 
 def body(vectors, contexts, tree_order, live_counts, level_bases, coupling, length_scale):
@@ -87,24 +91,14 @@
     onehot = (slot_order[:, None] == jnp.arange(per_device, dtype=jnp.int32)[None, :]).astype(
         jnp.bfloat16
     )
-    lhs_features, _ = gram_features(contexts / length_scale[:, None])
-    gathered = lax.dot_general(
+    lhs_features, rhs_features = gram_features(contexts / length_scale[:, None])
+    table = lax.dot_general(
         onehot,
-        jnp.concatenate([vectors, lhs_features], axis=1),
+        jnp.concatenate([lhs_features, rhs_features.T, vectors], axis=1),
         (((1,), (0,)), ((), ())),
         preferred_element_type=jnp.float32,
     ).astype(jnp.bfloat16)
-    ordered = gathered[:, :PANEL]
-    lhs = gathered[:, PANEL:]
-    half = jnp.asarray(-0.5, jnp.bfloat16)
-    high = lhs[:, 0:DIM] * half
-    middle = lhs[:, 2 * DIM : 3 * DIM] * half
-    low = lhs[:, 5 * DIM : 6 * DIM] * half
-    norm_parts = lhs[:, 6 * DIM : 6 * DIM + 3]
-    ones = lhs[:, 6 * DIM + 3 : 6 * DIM + 6]
-    rhs = jnp.concatenate(
-        [high, middle, high, middle, low, high, ones, norm_parts, lhs[:, 6 * DIM + 6 :]], axis=1
-    )
+    ordered = table[:, 2 * FEATURES :]
     slot_limit = jnp.repeat(live_counts, LEAF)
     within = jnp.arange(per_device, dtype=jnp.int32) % LEAF
     live_rows = (within < slot_limit)[:, None]
@@ -124,13 +118,13 @@
         received = swapped(stack, "leaf", bit_index)
         upto = (bit_index + 1) * len(chunk_starts) // device_levels
         for row_start in chunk_starts[done:upto]:
-            accumulated = dense_rows(accumulated, lhs, rhs, masked, gate, row_start, block_rows)
+            accumulated = dense_rows(accumulated, table, masked, gate, row_start, block_rows)
         done = upto
         finished.append(received[0])
         stack = stack[1:] + received[1:]
         gate = received[0, :8]
     for row_start in chunk_starts[done:]:
-        accumulated = dense_rows(accumulated, lhs, rhs, masked, gate, row_start, block_rows)
+        accumulated = dense_rows(accumulated, table, masked, gate, row_start, block_rows)
     sibling_totals = jnp.stack(finished)
 
 

time: 133 us -> 116 us (0.87)
  local copies, waits for them, and re-layouts: 24.9 us -> 9.71 us
  other arithmetic: 7.18 us -> 4.54 us
  Pallas kernels: 37.8 us -> 40.4 us
  waiting for transfers between devices: 6.2 us -> 4.7 us
    concatenate x1, local copies, waits for them, and re-layouts: 10.4 us -> 0.46 us  [gram_features(): jnp.concatenate([high, middle, high, middle, low, high, ones, norm_parts,...]
    dot_general x1, local copies, waits for them, and re-layouts: 3.18 us -> 0.6 us  [body(): jnp.einsum('nrk,npk->nrp', basis_nodes, weights, preferred_element_type=j...]
    pallas_call x8, Pallas kernels: 37.8 us -> 40.4 us  [dense_rows(): pl.pallas_call(dense_kernel, grid=(rows // BLOCK,), in_specs=[pl.BlockSpe...]
    slice x2 -> x0, local copies, waits for them, and re-layouts: 2.35 us -> none  [the longest x1 1.99 us: body(): norm_parts = lhs[:, 6 * DIM:6 * DIM + 3]]
    mul x1 -> x0, other arithmetic: 1.86 us -> none  [body(): low = lhs[:, 5 * DIM:6 * DIM] * half]
    ppermute x8, waiting for transfers between devices: 6.2 us -> 4.7 us  [swapped(): lax.ppermute(x, axis, [(i, i ^ 1 << bit) for i in range(lax.axis_size(axi...]
  transfers between devices with their start and end apart: 8 -> 8, of which waited for: 2 -> 2; matrix products, arithmetic and copies ran while one was open for 21% -> 8% of each run, Pallas kernels for 29% -> 35%
where the time goes in v3:
time: 116 us; the launch traced here: 115 us
  Pallas kernels  40.4 us (35%)
  matrix products  36.3 us (31%)
  starting transfers between devices  18.7 us (16%)
  local copies, waits for them, and re-layouts  9.71 us (8%)
  waiting for transfers between devices  4.7 us (4%)
  other arithmetic  4.54 us (4%)
    pallas_call x8, Pallas kernels, dense_rows(): pl.pallas_call(dense_kernel, grid=(rows // BLOCK,), in_specs=[pl.BlockSpe...  40.4 us
    ppermute x8, starting transfers between devices, swapped(): lax.ppermute(x, axis, [(i, i ^ 1 << bit) for i in range(lax.axis_size(axi...  18.7 us
    dot_general x1, matrix products, body(): lax.dot_general(onehot, result, (((0,), (0,)), ((), ())), preferred_eleme...  15.8 us
    dot_general x1, matrix products, body(): lax.dot_general(onehot, jnp.concatenate([lhs_features, rhs_features.T, ve...  12.5 us
    dot_general x1, matrix products, body(): jnp.einsum('lrk,lpk->rp', level_bases[local_levels:], weights, preferred_...  5.37 us
    squeeze x7, local copies, waits for them, and re-layouts, body(): gate = received[0, :8]  4.82 us
    ppermute x8, waiting for transfers between devices, swapped(): lax.ppermute(x, axis, [(i, i ^ 1 << bit) for i in range(lax.axis_size(axi...  4.7 us
  transfers between devices with their start and end apart: 8, of which 2 were waited for; matrix products, arithmetic and copies ran while one was open for 8% of the time, Pallas kernels for 35%

profile of v3, /device:TPU:6, one launch (start us, length us, event | category | flops | bytes accessed | tf_op | source)
XLA Modules:
  0.0 114.5 jit_solution(4429879945341715665)
XLA Ops:
  0.0 0.0 copy-start
  0.0 1.1 broadcast_multiply_fusion
  1.1 0.2 fusion.30
  1.3 0.0 copy-done
  1.3 0.1 broadcast_bitcast_fusion
  1.5 0.5 concatenate.12
  1.9 0.0 slice-start
  1.9 0.5 concatenate.11
  2.4 0.0 copy-done.5
  2.4 0.0 copy-done.4
  2.4 0.0 slice-start.1
  2.4 0.0 slice-start.2
  2.4 12.5 %fusion.8.rows_ref.leaf_ref = bf16[4096,192]{1,0:T(8,128)(2,1)S(1)} fusion(s32[4096]{0:T(1024)S(1)} %bitcast.58, bf16[4096,64]{0,1:T(8,128)(2,1)S(1)} %copy-done.4, bf16[4096,64]{0,1:T(8,128)(2,1)S(1)} %bitcast.55, bf16[4096,64]{0,1:T(8,128)(2,1)S(1)} %bitcast.56), kind=kOutput, calls=%fused_computation.9 | convolution fusion | flops 6464733184 | bytes 3162112 | tf_op jit(solution)/shard_map/dot_general | solution.py:95
  15.0 0.0 copy-start.1
  15.0 2.2 %slice_select_fusion.vec_ref = bf16[4096,64]{1,0:T(8,128)(2,1)S(1)} fusion(bf16[4096,192]{1,0:T(8,128)(2,1)S(1)} %fusion.8.rows_ref.leaf_ref, pred[4096]{0:T(1024)(128)(4,1)S(1)} %fusion.31), kind=kLoop, calls=%fused_computation.23 | loop fusion | flops 262144 | bytes 1052672 | tf_op jit(solution)/shard_map/jit(_where)/select_n | solution.py:105
  17.2 0.0 slice-done
  17.2 0.0 slice-done.1
  17.2 0.0 slice-done.2
  17.2 0.0 copy-start.2
  17.2 1.6 %fusion.21 = f32[8,64,128]{2,1,0:T(8,128)S(1)} fusion(bf16[9,4096,128]{2,1,0:T(8,128)(2,1)S(1)} %bitcast.52, bf16[4096,64]{1,0:T(8,128)(2,1)S(1)} %slice_select_fusion.vec_ref), kind=kOutput, calls=%fused_computation.22 | convolution fusion | flops 536870912 | bytes 9699328 | tf_op jit(solution)/shard_map/rp,lrk->lpk/dot_general | solution.py:107
  18.8 0.0 copy-start.3
  18.8 0.3 collective-permute-start
  19.1 0.1 slice.161
  19.2 0.3 copy-done.3
  19.5 0.5 fusion.45
  20.0 0.5 convolution_bitcast_fusion
  20.5 0.6 copy.18
  21.1 0.6 broadcast_in_dim.40.gate_ref
  21.7 1.4 %broadcast_4_acc_ref.2.acc_ref = f32[4096,64]{1,0:T(8,128)} broadcast(f32[]{:T(128)} %constant.33.clone.1), dimensions={} | broadcast | bytes 1048580 | tf_op jit(solution)/shard_map/broadcast.4.acc_ref
  23.2 5.0 %shard_map.82.acc_ref = f32[4096,64]{1,0:T(8,128)} custom-call(bf16[4096,192]{1,0:T(8,128)(2,1)} %copy-done.1, bf16[4096,192]{1,0:T(8,128)(2,1)} %copy-done.1, bf16[4096,64]{1,0:T(8,128)(2,1)} %copy-done.2, f32[8,128]{1,0:T(8,128)} %broadcast_in_dim.40.gate_ref, f32[4096,64]{1,0:T(8,128)} %broadcast_4_acc_ref.2.acc_ref), custom_call_target="tpu_custom_call", output_to_operand_aliasing={{}: (4, {})} | custom-call | tf_op jit(solution)/shard_map/pallas_call | solution.py:68
  28.2 0.0 collective-permute-done
  28.2 1.0 slice_add_fusion
  29.2 2.0 %collective-permute-start.1 = (f32[7,64,128]{2,1,0:T(8,128)S(1)}, f32[7,64,128]{2,1,0:T(8,128)S(1)}, u32[]{:S(2)}, u32[]{:S(2)}) collective-permute-start(f32[7,64,128]{2,1,0:T(8,128)S(1)} %slice_add_fusion), channel_id=1, source_target_pairs={{0,2},{1,3},{2,0},{3,1},{4,6},{5,7},{6,4},{7,5},{8,10},{9,11},{10,... | collective-permute-start | bytes 688136 | tf_op jit(solution)/shard_map/ppermute | solution.py:21
  31.2 1.3 %slice_bitcast_fusion.gate_ref = f32[8,128]{1,0:T(8,128)} fusion(f32[8,64,128]{2,1,0:T(8,128)} %collective-permute-done), kind=kLoop, calls=%fused_computation.80 | loop fusion | bytes 8192 | tf_op jit(solution)/shard_map/squeeze | solution.py:125
  32.5 5.1 %shard_map.83.acc_ref = f32[4096,64]{1,0:T(8,128)} custom-call(bf16[4096,192]{1,0:T(8,128)(2,1)} %copy-done.1, bf16[4096,192]{1,0:T(8,128)(2,1)} %copy-done.1, bf16[4096,64]{1,0:T(8,128)(2,1)} %copy-done.2, f32[8,128]{1,0:T(8,128)} %slice_bitcast_fusion.gate_ref, f32[4096,64]{1,0:T(8,128)} %shard_map.82.acc_ref), custom_call_target="tpu_custom_call", output_to_operand_aliasing={{}: (4, {})} | custom-call | tf_op jit(solution)/shard_map/pallas_call | solution.py:68
  37.5 0.8 slice_dynamic-update-slice_fusion.6
  38.3 0.0 collective-permute-done.1
  38.3 3.4 %collective-permute-start.2 = (f32[6,64,128]{2,1,0:T(8,128)S(1)}, f32[6,64,128]{2,1,0:T(8,128)S(1)}, u32[]{:S(2)}, u32[]{:S(2)}) collective-permute-start(f32[6,64,128]{2,1,0:T(8,128)S(1)} %slice_add_fusion.1), channel_id=1, source_target_pairs={{0,4},{1,5},{2,6},{3,7},{4,0},{5,1},{6,2},{7,3},{8,12},{9,13},{10,... | collective-permute-start | bytes 589832 | tf_op jit(solution)/shard_map/ppermute | solution.py:21
  41.7 0.6 slice_bitcast_fusion.1.gate_ref
  42.3 5.0 %shard_map.84.acc_ref = f32[4096,64]{1,0:T(8,128)} custom-call(bf16[4096,192]{1,0:T(8,128)(2,1)} %copy-done.1, bf16[4096,192]{1,0:T(8,128)(2,1)} %copy-done.1, bf16[4096,64]{1,0:T(8,128)(2,1)} %copy-done.2, f32[8,128]{1,0:T(8,128)} %slice_bitcast_fusion.1.gate_ref, f32[4096,64]{1,0:T(8,128)} %shard_map.83.acc_ref), custom_call_target="tpu_custom_call", output_to_operand_aliasing={{}: (4, {})} | custom-call | tf_op jit(solution)/shard_map/pallas_call | solution.py:68
  47.3 3.3 %collective-permute-done.2 = f32[6,64,128]{2,1,0:T(8,128)S(1)} collective-permute-done((f32[6,64,128]{2,1,0:T(8,128)S(1)}, f32[6,64,128]{2,1,0:T(8,128)S(1)}, u32[]{:S(2)}, u32[]{:S(2)}) %collective-permute-start.2) | collective-permute-done | bytes 196640 | tf_op jit(solution)/shard_map/ppermute | solution.py:21
  50.6 6.0 %collective-permute-start.3 = (f32[5,64,128]{2,1,0:T(8,128)S(1)}, f32[5,64,128]{2,1,0:T(8,128)S(1)}, u32[]{:S(2)}, u32[]{:S(2)}) collective-permute-start(f32[5,64,128]{2,1,0:T(8,128)S(1)} %slice_add_fusion.2), channel_id=1, source_target_pairs={{0,8},{1,9},{2,10},{3,11},{4,12},{5,13},{6,14},{7,15},{8,0},{9,1},... | collective-permute-start | bytes 491528 | tf_op jit(solution)/shard_map/ppermute | solution.py:21
  56.7 0.6 slice_bitcast_fusion.2.gate_ref
  57.3 5.1 %shard_map.85.acc_ref = f32[4096,64]{1,0:T(8,128)} custom-call(bf16[4096,192]{1,0:T(8,128)(2,1)} %copy-done.1, bf16[4096,192]{1,0:T(8,128)(2,1)} %copy-done.1, bf16[4096,64]{1,0:T(8,128)(2,1)} %copy-done.2, f32[8,128]{1,0:T(8,128)} %slice_bitcast_fusion.2.gate_ref, f32[4096,64]{1,0:T(8,128)} %shard_map.84.acc_ref), custom_call_target="tpu_custom_call", output_to_operand_aliasing={{}: (4, {})} | custom-call | tf_op jit(solution)/shard_map/pallas_call | solution.py:68
  62.3 1.4 %collective-permute-done.3 = f32[5,64,128]{2,1,0:T(8,128)S(1)} collective-permute-done((f32[5,64,128]{2,1,0:T(8,128)S(1)}, f32[5,64,128]{2,1,0:T(8,128)S(1)}, u32[]{:S(2)}, u32[]{:S(2)}) %collective-permute-start.3) | collective-permute-done | bytes 163872 | tf_op jit(solution)/shard_map/ppermute | solution.py:21
  63.8 0.9 collective-permute-start.4
  64.7 0.6 slice_bitcast_fusion.3.gate_ref
  65.3 5.0 %shard_map.86.acc_ref = f32[4096,64]{1,0:T(8,128)} custom-call(bf16[4096,192]{1,0:T(8,128)(2,1)} %copy-done.1, bf16[4096,192]{1,0:T(8,128)(2,1)} %copy-done.1, bf16[4096,64]{1,0:T(8,128)(2,1)} %copy-done.2, f32[8,128]{1,0:T(8,128)} %slice_bitcast_fusion.3.gate_ref, f32[4096,64]{1,0:T(8,128)} %shard_map.85.acc_ref), custom_call_target="tpu_custom_call", output_to_operand_aliasing={{}: (4, {})} | custom-call | tf_op jit(solution)/shard_map/pallas_call | solution.py:68
  70.3 0.0 collective-permute-done.4
  70.3 1.2 %collective-permute-start.5 = (f32[3,64,128]{2,1,0:T(8,128)S(1)}, f32[3,64,128]{2,1,0:T(8,128)S(1)}, u32[]{:S(2)}, u32[]{:S(2)}) collective-permute-start(f32[3,64,128]{2,1,0:T(8,128)S(1)} %slice_add_fusion.4), channel_id=1, source_target_pairs={{0,32},{1,33},{2,34},{3,35},{4,36},{5,37},{6,38},{7,39},{8,40},{9,... | collective-permute-start | bytes 294920 | tf_op jit(solution)/shard_map/ppermute | solution.py:21
  71.5 0.6 slice_bitcast_fusion.4.gate_ref
  72.1 5.0 %shard_map.87.acc_ref = f32[4096,64]{1,0:T(8,128)} custom-call(bf16[4096,192]{1,0:T(8,128)(2,1)} %copy-done.1, bf16[4096,192]{1,0:T(8,128)(2,1)} %copy-done.1, bf16[4096,64]{1,0:T(8,128)(2,1)} %copy-done.2, f32[8,128]{1,0:T(8,128)} %slice_bitcast_fusion.4.gate_ref, f32[4096,64]{1,0:T(8,128)} %shard_map.86.acc_ref), custom_call_target="tpu_custom_call", output_to_operand_aliasing={{}: (4, {})} | custom-call | tf_op jit(solution)/shard_map/pallas_call | solution.py:68
  77.2 0.0 collective-permute-done.5
  77.2 1.9 %collective-permute-start.6 = (f32[2,64,128]{2,1,0:T(8,128)S(1)}, f32[2,64,128]{2,1,0:T(8,128)S(1)}, u32[]{:S(2)}, u32[]{:S(2)}) collective-permute-start(f32[2,64,128]{2,1,0:T(8,128)S(1)} %slice_add_fusion.5), channel_id=1, source_target_pairs={{0,64},{1,65},{2,66},{3,67},{4,68},{5,69},{6,70},{7,71},{8,72},{9,... | collective-permute-start | bytes 196616 | tf_op jit(solution)/shard_map/ppermute | solution.py:21
  79.1 0.6 slice_bitcast_fusion.5.gate_ref
  79.7 5.0 %shard_map.88.acc_ref = f32[4096,64]{1,0:T(8,128)} custom-call(bf16[4096,192]{1,0:T(8,128)(2,1)} %copy-done.1, bf16[4096,192]{1,0:T(8,128)(2,1)} %copy-done.1, bf16[4096,64]{1,0:T(8,128)(2,1)} %copy-done.2, f32[8,128]{1,0:T(8,128)} %slice_bitcast_fusion.5.gate_ref, f32[4096,64]{1,0:T(8,128)} %shard_map.87.acc_ref), custom_call_target="tpu_custom_call", output_to_operand_aliasing={{}: (4, {})} | custom-call | tf_op jit(solution)/shard_map/pallas_call | solution.py:68
  84.7 0.0 collective-permute-done.6
  84.7 3.0 %collective-permute-start.7 = (f32[1,64,128]{2,1,0:T(8,128)S(1)}, f32[1,64,128]{2,1,0:T(8,128)S(1)}, u32[]{:S(2)}, u32[]{:S(2)}) collective-permute-start(f32[1,64,128]{2,1,0:T(8,128)S(1)} %get-tuple-element.16), channel_id=1, source_target_pairs={{0,128},{1,129},{2,130},{3,131},{4,132},{5,133},{6,134},{7,135},{8... | collective-permute-start | bytes 98312 | tf_op jit(solution)/shard_map/ppermute | solution.py:21
  87.7 0.6 slice_bitcast_fusion.6.gate_ref
  88.3 5.0 %shard_map.89 = f32[4096,64]{1,0:T(8,128)} custom-call(bf16[4096,192]{1,0:T(8,128)(2,1)} %copy-done.1, bf16[4096,192]{1,0:T(8,128)(2,1)} %copy-done.1, bf16[4096,64]{1,0:T(8,128)(2,1)} %copy-done.2, f32[8,128]{1,0:T(8,128)} %slice_bitcast_fusion.6.gate_ref, f32[4096,64]{1,0:T(8,128)} %shard_map.88.acc_ref), custom_call_target="tpu_custom_call", output_to_operand_aliasing={{}: (4, {})} | custom-call | tf_op jit(solution)/shard_map/pallas_call | solution.py:68
  93.4 0.0 collective-permute-done.7
  93.4 0.0 copy-done.6
  93.4 5.4 %fusion.15 = bf16[4096,64]{1,0:T(8,128)(2,1)S(1)} fusion(f32[4096,64]{1,0:T(8,128)} %shard_map.89, f32[2,2048,64]{2,1,0:T(8,128)S(1)} %copy.18, pred[4096]{0:T(1024)(128)(4,1)S(1)} %fusion.31, bf16[9,4096,128]{2,1,0:T(8,128)(2,1)} %param.12, f32[8,64,128]{2,1,0:T(8,128)S(1)} %constant_dynamic-update-slice_fusion, f32[8,128]{1,0:T(8,128)S(1)} %slice_multiply_fusion.8, ...), kind=kOutput, calls=%fused_computation.16 | convolution fusion | flops 538116096 | bytes 12328992 | tf_op jit(solution)/shard_map/lrk,lpk->rp/dot_general | solution.py:156
  98.8 15.8 %fusion.12 = bf16[4096,64]{0,1:T(8,128)(2,1)} fusion(bf16[4096,64]{1,0:T(8,128)(2,1)S(1)} %fusion.15, s32[4096]{0:T(1024)S(1)} %bitcast.59), kind=kOutput, calls=%fused_computation.11 | convolution fusion | flops 2164523008 | bytes 1064960 | tf_op jit(solution)/shard_map/dot_general | solution.py:160
  (27 shorter events, 0.2 us)
Async XLA Ops:
  0.0 1.3 %copy-start = (s32[2]{0:T(128)S(1)}, s32[2]{0:T(128)}, u32[]{:S(2)}) copy-start(s32[2]{0:T(128)} %param.11) | copy-start | bytes 28
  0.0 2.4 %copy-start.5 = (s32[1,4096]{1,0:T(1,128)S(1)}, s32[1,4096]{1,0:T(1,128)}, u32[]{:S(2)}) copy-start(s32[1,4096]{1,0:T(1,128)} %param.10) | copy-start | bytes 49156
  0.0 2.4 %copy-start.4 = (bf16[4096,64]{0,1:T(8,128)(2,1)S(1)}, bf16[4096,64]{0,1:T(8,128)(2,1)}, u32[]{:S(2)}) copy-start(bf16[4096,64]{0,1:T(8,128)(2,1)} %param.8) | copy-start | bytes 1572868
  1.9 15.2 %slice-start = ((s8[9437184]{0:T(1024)(128)(4,1)}), s8[1048576]{0:T(1024)(128)(4,1)S(1)}, s32[]{:S(2)}) async-start(s8[9437184]{0:T(1024)(128)(4,1)} %bitcast.51), calls=%async_computation | async-start | bytes 2097152
  2.4 14.8 %slice-start.1 = ((s8[9437184]{0:T(1024)(128)(4,1)}), s8[4194304]{0:T(1024)(128)(4,1)S(1)}, s32[]{:S(2)}) async-start(s8[9437184]{0:T(1024)(128)(4,1)} %bitcast.51), calls=%async_computation.1 | async-start | bytes 8388608
  2.4 14.7 %slice-start.2 = ((s8[9437184]{0:T(1024)(128)(4,1)}), s8[4194304]{0:T(1024)(128)(4,1)S(1)}, s32[]{:S(2)}) async-start(s8[9437184]{0:T(1024)(128)(4,1)} %bitcast.51), calls=%async_computation.2 | async-start | bytes 8388608
  15.0 3.8 %copy-start.1 = (bf16[4096,192]{1,0:T(8,128)(2,1)}, bf16[4096,192]{1,0:T(8,128)(2,1)S(1)}, u32[]{:S(2)}) copy-start(bf16[4096,192]{1,0:T(8,128)(2,1)S(1)} %fusion.8.rows_ref.leaf_ref) | copy-start | bytes 4718596
  17.2 2.3 %copy-start.2 = (bf16[4096,64]{1,0:T(8,128)(2,1)}, bf16[4096,64]{1,0:T(8,128)(2,1)S(1)}, u32[]{:S(2)}) copy-start(bf16[4096,64]{1,0:T(8,128)(2,1)S(1)} %slice_select_fusion.vec_ref) | copy-start | bytes 1572868
  18.8 0.7 copy-start.3
  18.8 9.4 %collective-permute-start = (f32[8,64,128]{2,1,0:T(8,128)S(1)}, f32[8,64,128]{2,1,0:T(8,128)}, u32[]{:S(2)}, u32[]{:S(2)}) collective-permute-start(f32[8,64,128]{2,1,0:T(8,128)S(1)} %fusion.21), channel_id=1, source_target_pairs={{0,1},{1,0},{2,3},{3,2},{4,5},{5,4},{6,7},{7,6},{8,9},{9,8},{10,11... | collective-permute-start | bytes 786440 | tf_op jit(solution)/shard_map/ppermute | solution.py:21
  29.2 9.1 %collective-permute-start.1 = (f32[7,64,128]{2,1,0:T(8,128)S(1)}, f32[7,64,128]{2,1,0:T(8,128)S(1)}, u32[]{:S(2)}, u32[]{:S(2)}) collective-permute-start(f32[7,64,128]{2,1,0:T(8,128)S(1)} %slice_add_fusion), channel_id=1, source_target_pairs={{0,2},{1,3},{2,0},{3,1},{4,6},{5,7},{6,4},{7,5},{8,10},{9,11},{10,... | collective-permute-start | bytes 688136 | tf_op jit(solution)/shard_map/ppermute | solution.py:21
  38.3 12.3 %collective-permute-start.2 = (f32[6,64,128]{2,1,0:T(8,128)S(1)}, f32[6,64,128]{2,1,0:T(8,128)S(1)}, u32[]{:S(2)}, u32[]{:S(2)}) collective-permute-start(f32[6,64,128]{2,1,0:T(8,128)S(1)} %slice_add_fusion.1), channel_id=1, source_target_pairs={{0,4},{1,5},{2,6},{3,7},{4,0},{5,1},{6,2},{7,3},{8,12},{9,13},{10,... | collective-permute-start | bytes 589832 | tf_op jit(solution)/shard_map/ppermute | solution.py:21
  50.6 13.1 %collective-permute-start.3 = (f32[5,64,128]{2,1,0:T(8,128)S(1)}, f32[5,64,128]{2,1,0:T(8,128)S(1)}, u32[]{:S(2)}, u32[]{:S(2)}) collective-permute-start(f32[5,64,128]{2,1,0:T(8,128)S(1)} %slice_add_fusion.2), channel_id=1, source_target_pairs={{0,8},{1,9},{2,10},{3,11},{4,12},{5,13},{6,14},{7,15},{8,0},{9,1},... | collective-permute-start | bytes 491528 | tf_op jit(solution)/shard_map/ppermute | solution.py:21
  63.8 6.5 %collective-permute-start.4 = (f32[4,64,128]{2,1,0:T(8,128)S(1)}, f32[4,64,128]{2,1,0:T(8,128)S(1)}, u32[]{:S(2)}, u32[]{:S(2)}) collective-permute-start(f32[4,64,128]{2,1,0:T(8,128)S(1)} %slice_add_fusion.3), channel_id=1, source_target_pairs={{0,16},{1,17},{2,18},{3,19},{4,20},{5,21},{6,22},{7,23},{8,24},{9,... | collective-permute-start | bytes 393224 | tf_op jit(solution)/shard_map/ppermute | solution.py:21
  70.3 6.8 %collective-permute-start.5 = (f32[3,64,128]{2,1,0:T(8,128)S(1)}, f32[3,64,128]{2,1,0:T(8,128)S(1)}, u32[]{:S(2)}, u32[]{:S(2)}) collective-permute-start(f32[3,64,128]{2,1,0:T(8,128)S(1)} %slice_add_fusion.4), channel_id=1, source_target_pairs={{0,32},{1,33},{2,34},{3,35},{4,36},{5,37},{6,38},{7,39},{8,40},{9,... | collective-permute-start | bytes 294920 | tf_op jit(solution)/shard_map/ppermute | solution.py:21
  77.2 7.5 %collective-permute-start.6 = (f32[2,64,128]{2,1,0:T(8,128)S(1)}, f32[2,64,128]{2,1,0:T(8,128)S(1)}, u32[]{:S(2)}, u32[]{:S(2)}) collective-permute-start(f32[2,64,128]{2,1,0:T(8,128)S(1)} %slice_add_fusion.5), channel_id=1, source_target_pairs={{0,64},{1,65},{2,66},{3,67},{4,68},{5,69},{6,70},{7,71},{8,72},{9,... | collective-permute-start | bytes 196616 | tf_op jit(solution)/shard_map/ppermute | solution.py:21
  84.7 8.6 %collective-permute-start.7 = (f32[1,64,128]{2,1,0:T(8,128)S(1)}, f32[1,64,128]{2,1,0:T(8,128)S(1)}, u32[]{:S(2)}, u32[]{:S(2)}) collective-permute-start(f32[1,64,128]{2,1,0:T(8,128)S(1)} %get-tuple-element.16), channel_id=1, source_target_pairs={{0,128},{1,129},{2,130},{3,131},{4,132},{5,133},{6,134},{7,135},{8... | collective-permute-start | bytes 98312 | tf_op jit(solution)/shard_map/ppermute | solution.py:21
  88.3 5.1 %copy-start.6 = (f32[8]{0:T(128)S(1)}, f32[8]{0:T(128)}, u32[]{:S(2)}) copy-start(f32[8]{0:T(128)} %constant.36.clone) | copy-start | bytes 100

commit v4 on v3

--- a/solution.py
+++ b/solution.py
@@ -62,7 +62,7 @@
 
 
 def dense_rows(acc, table, vec, gate, row_start, rows):
-    leaf = row_start // LEAF
+    per_leaf = LEAF // BLOCK
     first = row_start // BLOCK
     width = table.shape[1]
     return pl.pallas_call(
@@ -70,8 +70,8 @@
         grid=(rows // BLOCK,),
         in_specs=[
             pl.BlockSpec((BLOCK, width), lambda i: (first + i, 0)),
-            pl.BlockSpec((LEAF, width), lambda i: (leaf, 0)),
-            pl.BlockSpec((LEAF, PANEL), lambda i: (leaf, 0)),
+            pl.BlockSpec((LEAF, width), lambda i: ((first + i) // per_leaf, 0)),
+            pl.BlockSpec((LEAF, PANEL), lambda i: ((first + i) // per_leaf, 0)),
             pl.BlockSpec(memory_space=pl.ANY),
             pl.BlockSpec(memory_space=pl.ANY),
         ],
@@ -107,7 +107,7 @@
     partials = jnp.einsum(
         "rp,lrk->lpk", masked, level_bases[local_levels:], preferred_element_type=jnp.float32
     )
-    block_rows = min(512, LEAF)
+    block_rows = per_device
     chunk_starts = list(range(0, per_device, block_rows))
     accumulated = jnp.zeros((per_device, PANEL), jnp.float32)
     stack = partials
@@ -116,7 +116,7 @@
     done = 0
     for bit_index in range(device_levels):
         received = swapped(stack, "leaf", bit_index)
-        upto = (bit_index + 1) * len(chunk_starts) // device_levels
+        upto = -(-(bit_index + 1) * len(chunk_starts) // device_levels)
         for row_start in chunk_starts[done:upto]:
             accumulated = dense_rows(accumulated, table, masked, gate, row_start, block_rows)
         done = upto

time: 116 us -> 127 us (1.095)
  waiting for transfers between devices: 4.7 us -> 33.1 us
  Pallas kernels: 40.4 us -> 26.3 us
  local copies, waits for them, and re-layouts: 9.71 us -> 4.56 us
  other arithmetic: 4.54 us -> 6.33 us
    ppermute x8, waiting for transfers between devices: 4.7 us -> 33.1 us  [swapped(): lax.ppermute(x, axis, [(i, i ^ 1 << bit) for i in range(lax.axis_size(axi...]
    pallas_call x8 -> x1, Pallas kernels: 40.4 us -> 26.3 us  [dense_rows(): pl.pallas_call(dense_kernel, grid=(rows // BLOCK,), in_specs=[pl.BlockSpe...]
    squeeze x7 -> x0, local copies, waits for them, and re-layouts: 4.82 us -> none  [body(): gate = received[0, :8]]
    add x0 -> x1, other arithmetic: none -> 1.79 us  [body(): accumulated + jnp.einsum('nrk,npk->nrp', basis_nodes, weights, preferred_...]
  transfers between devices with their start and end apart: 8 -> 8, of which waited for: 2 -> 7; matrix products, arithmetic and copies ran while one was open for 8% -> 5% of each run, Pallas kernels for 35% -> 21%
where the time goes in v4:
time: 127 us; the launch traced here: 126 us
  matrix products  35.8 us (28%)
  waiting for transfers between devices  33.1 us (26%)
  Pallas kernels  26.3 us (21%)
  starting transfers between devices  19.8 us (16%)
  other arithmetic  6.33 us (5%)
  local copies, waits for them, and re-layouts  4.56 us (4%)
    ppermute x8, waiting for transfers between devices, swapped(): lax.ppermute(x, axis, [(i, i ^ 1 << bit) for i in range(lax.axis_size(axi...  33.1 us
    pallas_call x1, Pallas kernels, dense_rows(): pl.pallas_call(dense_kernel, grid=(rows // BLOCK,), in_specs=[pl.BlockSpe...  26.3 us
    ppermute x8, starting transfers between devices, swapped(): lax.ppermute(x, axis, [(i, i ^ 1 << bit) for i in range(lax.axis_size(axi...  19.8 us
    dot_general x1, matrix products, body(): lax.dot_general(onehot, result, (((0,), (0,)), ((), ())), preferred_eleme...  15.8 us
    dot_general x1, matrix products, body(): lax.dot_general(onehot, jnp.concatenate([lhs_features, rhs_features.T, ve...  12.5 us
    dot_general x1, matrix products, body(): jnp.einsum('lrk,lpk->rp', level_bases[local_levels:], weights, preferred_...  4.88 us
  transfers between devices with their start and end apart: 8, of which 7 were waited for; matrix products, arithmetic and copies ran while one was open for 5% of the time, Pallas kernels for 21%

profile of v4, /device:TPU:6, one launch (start us, length us, event | category | flops | bytes accessed | tf_op | source)
XLA Modules:
  0.0 126.1 jit_solution(12197439666986534450)
XLA Ops:
  0.0 0.0 copy-start
  0.0 0.0 copy-start.5
  0.0 0.0 copy-start.4
  0.0 1.1 broadcast_multiply_fusion
  1.1 0.2 fusion.34
  1.3 0.0 copy-done
  1.3 0.1 broadcast_bitcast_fusion
  1.5 0.5 concatenate.12
  1.9 0.0 slice-start
  1.9 0.5 concatenate.11
  2.4 0.0 copy-done.5
  2.4 0.0 copy-done.4
  2.4 0.0 slice-start.1
  2.4 0.0 slice-start.2
  2.4 12.5 %fusion.8.rows_ref.leaf_ref = bf16[4096,192]{1,0:T(8,128)(2,1)S(1)} fusion(s32[4096]{0:T(1024)S(1)} %bitcast.42, bf16[4096,64]{0,1:T(8,128)(2,1)S(1)} %copy-done.4, bf16[4096,64]{0,1:T(8,128)(2,1)S(1)} %bitcast.39, bf16[4096,64]{0,1:T(8,128)(2,1)S(1)} %bitcast.40), kind=kOutput, calls=%fused_computation.9 | convolution fusion | flops 6464733184 | bytes 3162112 | tf_op jit(solution)/shard_map/dot_general | solution.py:95
  15.0 0.0 copy-start.2
  15.0 2.2 %slice_select_fusion.vec_ref = bf16[4096,64]{1,0:T(8,128)(2,1)S(1)} fusion(bf16[4096,192]{1,0:T(8,128)(2,1)S(1)} %fusion.8.rows_ref.leaf_ref, pred[4096]{0:T(1024)(128)(4,1)S(1)} %fusion.35), kind=kLoop, calls=%fused_computation.23 | loop fusion | flops 262144 | bytes 1052672 | tf_op jit(solution)/shard_map/jit(_where)/select_n | solution.py:105
  17.2 0.0 slice-done
  17.2 0.0 slice-done.1
  17.2 0.0 slice-done.2
  17.2 0.0 copy-start.1
  17.2 0.0 copy-start.3
  17.2 1.6 %fusion.27 = f32[8,64,128]{2,1,0:T(8,128)S(1)} fusion(bf16[9,4096,128]{2,1,0:T(8,128)(2,1)S(1)} %bitcast.35, bf16[4096,64]{1,0:T(8,128)(2,1)S(1)} %slice_select_fusion.vec_ref), kind=kOutput, calls=%fused_computation.22 | convolution fusion | flops 536870912 | bytes 9699328 | tf_op jit(solution)/shard_map/rp,lrk->lpk/dot_general | solution.py:107
  18.8 0.0 copy-done.2
  18.8 0.3 collective-permute-start
  19.1 0.1 slice.120
  19.2 0.0 copy-done.3
  19.2 0.0 copy-done.1
  19.2 0.5 fusion.49
  19.7 0.5 convolution_bitcast_fusion
  20.2 0.6 copy.11
  20.8 0.6 broadcast_in_dim.40.gate_ref
  21.4 1.4 %broadcast_4_acc_ref.2.acc_ref = f32[4096,64]{1,0:T(8,128)} broadcast(f32[]{:T(128)} %constant.33.clone.1), dimensions={} | broadcast | bytes 1048580 | tf_op jit(solution)/shard_map/broadcast.4.acc_ref
  22.9 26.3 %shard_map.82 = f32[4096,64]{1,0:T(8,128)} custom-call(bf16[4096,192]{1,0:T(8,128)(2,1)} %copy-done.2, bf16[4096,192]{1,0:T(8,128)(2,1)} %copy-done.2, bf16[4096,64]{1,0:T(8,128)(2,1)} %copy-done.1, f32[8,128]{1,0:T(8,128)} %broadcast_in_dim.40.gate_ref, f32[4096,64]{1,0:T(8,128)} %broadcast_4_acc_ref.2.acc_ref), custom_call_target="tpu_custom_call", output_to_operand_aliasing={{}: (4, {})} | custom-call | tf_op jit(solution)/shard_map/pallas_call | solution.py:68
  49.1 0.0 collective-permute-done
  49.1 1.0 slice_add_fusion
  50.1 0.0 copy-start.6
  50.1 1.9 %collective-permute-start.1 = (f32[7,64,128]{2,1,0:T(8,128)S(1)}, f32[7,64,128]{2,1,0:T(8,128)S(1)}, u32[]{:S(2)}, u32[]{:S(2)}) collective-permute-start(f32[7,64,128]{2,1,0:T(8,128)S(1)} %slice_add_fusion), channel_id=1, source_target_pairs={{0,2},{1,3},{2,0},{3,1},{4,6},{5,7},{6,4},{7,5},{8,10},{9,11},{10,... | collective-permute-start | bytes 688136 | tf_op jit(solution)/shard_map/ppermute | solution.py:21
  52.1 1.8 %bitcast_add_fusion = f32[4096,64]{1,0:T(8,128)S(1)} fusion(f32[4096,64]{1,0:T(8,128)} %shard_map.82, f32[2,2048,64]{2,1,0:T(8,128)S(1)} %copy.11), kind=kLoop, calls=%fused_computation.16 | loop fusion | flops 262144 | bytes 3145728 | tf_op jit(solution)/shard_map/add | solution.py:144
  53.9 0.8 slice_dynamic-update-slice_fusion.6
  54.6 3.7 %collective-permute-done.1 = f32[7,64,128]{2,1,0:T(8,128)S(1)} collective-permute-done((f32[7,64,128]{2,1,0:T(8,128)S(1)}, f32[7,64,128]{2,1,0:T(8,128)S(1)}, u32[]{:S(2)}, u32[]{:S(2)}) %collective-permute-start.1) | collective-permute-done | bytes 229408 | tf_op jit(solution)/shard_map/ppermute | solution.py:21
  58.4 3.4 %collective-permute-start.2 = (f32[6,64,128]{2,1,0:T(8,128)S(1)}, f32[6,64,128]{2,1,0:T(8,128)S(1)}, u32[]{:S(2)}, u32[]{:S(2)}) collective-permute-start(f32[6,64,128]{2,1,0:T(8,128)S(1)} %slice_add_fusion.1), channel_id=1, source_target_pairs={{0,4},{1,5},{2,6},{3,7},{4,0},{5,1},{6,2},{7,3},{8,12},{9,13},{10,... | collective-permute-start | bytes 589832 | tf_op jit(solution)/shard_map/ppermute | solution.py:21
  61.7 9.0 %collective-permute-done.2 = f32[6,64,128]{2,1,0:T(8,128)S(1)} collective-permute-done((f32[6,64,128]{2,1,0:T(8,128)S(1)}, f32[6,64,128]{2,1,0:T(8,128)S(1)}, u32[]{:S(2)}, u32[]{:S(2)}) %collective-permute-start.2) | collective-permute-done | bytes 196640 | tf_op jit(solution)/shard_map/ppermute | solution.py:21
  70.7 6.4 %collective-permute-start.3 = (f32[5,64,128]{2,1,0:T(8,128)S(1)}, f32[5,64,128]{2,1,0:T(8,128)S(1)}, u32[]{:S(2)}, u32[]{:S(2)}) collective-permute-start(f32[5,64,128]{2,1,0:T(8,128)S(1)} %slice_add_fusion.2), channel_id=1, source_target_pairs={{0,8},{1,9},{2,10},{3,11},{4,12},{5,13},{6,14},{7,15},{8,0},{9,1},... | collective-permute-start | bytes 491528 | tf_op jit(solution)/shard_map/ppermute | solution.py:21
  77.1 7.0 %collective-permute-done.3 = f32[5,64,128]{2,1,0:T(8,128)S(1)} collective-permute-done((f32[5,64,128]{2,1,0:T(8,128)S(1)}, f32[5,64,128]{2,1,0:T(8,128)S(1)}, u32[]{:S(2)}, u32[]{:S(2)}) %collective-permute-start.3) | collective-permute-done | bytes 163872 | tf_op jit(solution)/shard_map/ppermute | solution.py:21
  84.1 0.8 collective-permute-start.4
  84.9 4.3 %collective-permute-done.4 = f32[4,64,128]{2,1,0:T(8,128)S(1)} collective-permute-done((f32[4,64,128]{2,1,0:T(8,128)S(1)}, f32[4,64,128]{2,1,0:T(8,128)S(1)}, u32[]{:S(2)}, u32[]{:S(2)}) %collective-permute-start.4) | collective-permute-done | bytes 131104 | tf_op jit(solution)/shard_map/ppermute | solution.py:21
  89.2 1.4 %collective-permute-start.5 = (f32[3,64,128]{2,1,0:T(8,128)S(1)}, f32[3,64,128]{2,1,0:T(8,128)S(1)}, u32[]{:S(2)}, u32[]{:S(2)}) collective-permute-start(f32[3,64,128]{2,1,0:T(8,128)S(1)} %slice_add_fusion.4), channel_id=1, source_target_pairs={{0,32},{1,33},{2,34},{3,35},{4,36},{5,37},{6,38},{7,39},{8,40},{9,... | collective-permute-start | bytes 294920 | tf_op jit(solution)/shard_map/ppermute | solution.py:21
  90.6 4.8 %collective-permute-done.5 = f32[3,64,128]{2,1,0:T(8,128)S(1)} collective-permute-done((f32[3,64,128]{2,1,0:T(8,128)S(1)}, f32[3,64,128]{2,1,0:T(8,128)S(1)}, u32[]{:S(2)}, u32[]{:S(2)}) %collective-permute-start.5) | collective-permute-done | bytes 98336 | tf_op jit(solution)/shard_map/ppermute | solution.py:21
  95.4 2.3 %collective-permute-start.6 = (f32[2,64,128]{2,1,0:T(8,128)S(1)}, f32[2,64,128]{2,1,0:T(8,128)S(1)}, u32[]{:S(2)}, u32[]{:S(2)}) collective-permute-start(f32[2,64,128]{2,1,0:T(8,128)S(1)} %slice_add_fusion.5), channel_id=1, source_target_pairs={{0,64},{1,65},{2,66},{3,67},{4,68},{5,69},{6,70},{7,71},{8,72},{9,... | collective-permute-start | bytes 196616 | tf_op jit(solution)/shard_map/ppermute | solution.py:21
  97.7 2.2 %collective-permute-done.6 = f32[2,64,128]{2,1,0:T(8,128)S(1)} collective-permute-done((f32[2,64,128]{2,1,0:T(8,128)S(1)}, f32[2,64,128]{2,1,0:T(8,128)S(1)}, u32[]{:S(2)}, u32[]{:S(2)}) %collective-permute-start.6) | collective-permute-done | bytes 65568 | tf_op jit(solution)/shard_map/ppermute | solution.py:21
  99.9 3.4 %collective-permute-start.7 = (f32[1,64,128]{2,1,0:T(8,128)S(1)}, f32[1,64,128]{2,1,0:T(8,128)S(1)}, u32[]{:S(2)}, u32[]{:S(2)}) collective-permute-start(f32[1,64,128]{2,1,0:T(8,128)S(1)} %get-tuple-element.16), channel_id=1, source_target_pairs={{0,128},{1,129},{2,130},{3,131},{4,132},{5,133},{6,134},{7,135},{8... | collective-permute-start | bytes 98312 | tf_op jit(solution)/shard_map/ppermute | solution.py:21
  103.4 2.1 %collective-permute-done.7 = f32[1,64,128]{2,1,0:T(8,128)S(1)} collective-permute-done((f32[1,64,128]{2,1,0:T(8,128)S(1)}, f32[1,64,128]{2,1,0:T(8,128)S(1)}, u32[]{:S(2)}, u32[]{:S(2)}) %collective-permute-start.7) | collective-permute-done | bytes 32800 | tf_op jit(solution)/shard_map/ppermute | solution.py:21
  105.4 0.0 copy-done.6
  105.5 4.9 %fusion.18 = bf16[4096,64]{1,0:T(8,128)(2,1)S(1)} fusion(f32[4096,64]{1,0:T(8,128)S(1)} %bitcast_add_fusion, bf16[9,4096,128]{2,1,0:T(8,128)(2,1)} %param.12, pred[4096]{0:T(1024)(128)(4,1)S(1)} %fusion.35, f32[8,64,128]{2,1,0:T(8,128)S(1)} %constant_dynamic-update-slice_fusion, f32[8,128]{1,0:T(8,128)S(1)} %slice_multiply_fusion.8, f32[8]{0:T(128)S(1)} %copy-done.6), kind=kOutput, calls=%fused_computation.13 | convolution fusion | flops 537853952 | bytes 10231840 | tf_op jit(solution)/shard_map/lrk,lpk->rp/dot_general | solution.py:156
  110.3 15.8 %fusion.21 = bf16[4096,64]{0,1:T(8,128)(2,1)} fusion(bf16[4096,64]{1,0:T(8,128)(2,1)S(1)} %fusion.18, s32[4096]{0:T(1024)S(1)} %bitcast.43), kind=kOutput, calls=%fused_computation.14 | convolution fusion | flops 2164523008 | bytes 1064960 | tf_op jit(solution)/shard_map/dot_general | solution.py:160
  (22 shorter events, 0.2 us)
Async XLA Ops:
  0.0 1.3 %copy-start = (s32[2]{0:T(128)S(1)}, s32[2]{0:T(128)}, u32[]{:S(2)}) copy-start(s32[2]{0:T(128)} %param.11) | copy-start | bytes 28
  0.0 2.4 %copy-start.5 = (s32[1,4096]{1,0:T(1,128)S(1)}, s32[1,4096]{1,0:T(1,128)}, u32[]{:S(2)}) copy-start(s32[1,4096]{1,0:T(1,128)} %param.10) | copy-start | bytes 49156
  0.0 2.4 %copy-start.4 = (bf16[4096,64]{0,1:T(8,128)(2,1)S(1)}, bf16[4096,64]{0,1:T(8,128)(2,1)}, u32[]{:S(2)}) copy-start(bf16[4096,64]{0,1:T(8,128)(2,1)} %param.8) | copy-start | bytes 1572868
  1.9 15.2 %slice-start = ((s8[9437184]{0:T(1024)(128)(4,1)}), s8[1048576]{0:T(1024)(128)(4,1)S(1)}, s32[]{:S(2)}) async-start(s8[9437184]{0:T(1024)(128)(4,1)} %bitcast.34), calls=%async_computation | async-start | bytes 2097152
  2.4 14.8 %slice-start.1 = ((s8[9437184]{0:T(1024)(128)(4,1)}), s8[4194304]{0:T(1024)(128)(4,1)S(1)}, s32[]{:S(2)}) async-start(s8[9437184]{0:T(1024)(128)(4,1)} %bitcast.34), calls=%async_computation.1 | async-start | bytes 8388608
  2.4 14.7 %slice-start.2 = ((s8[9437184]{0:T(1024)(128)(4,1)}), s8[4194304]{0:T(1024)(128)(4,1)S(1)}, s32[]{:S(2)}) async-start(s8[9437184]{0:T(1024)(128)(4,1)} %bitcast.34), calls=%async_computation.2 | async-start | bytes 8388608
  15.0 3.8 %copy-start.2 = (bf16[4096,192]{1,0:T(8,128)(2,1)}, bf16[4096,192]{1,0:T(8,128)(2,1)S(1)}, u32[]{:S(2)}) copy-start(bf16[4096,192]{1,0:T(8,128)(2,1)S(1)} %fusion.8.rows_ref.leaf_ref) | copy-start | bytes 4718596
  17.2 2.0 %copy-start.1 = (bf16[4096,64]{1,0:T(8,128)(2,1)}, bf16[4096,64]{1,0:T(8,128)(2,1)S(1)}, u32[]{:S(2)}) copy-start(bf16[4096,64]{1,0:T(8,128)(2,1)S(1)} %slice_select_fusion.vec_ref) | copy-start | bytes 1572868
  17.2 2.0 %copy-start.3 = (f32[9,128]{1,0:T(8,128)S(1)}, f32[9,128]{1,0:T(8,128)}, u32[]{:S(2)}) copy-start(f32[9,128]{1,0:T(8,128)} %param.13) | copy-start | bytes 13828
  18.8 30.3 %collective-permute-start = (f32[8,64,128]{2,1,0:T(8,128)S(1)}, f32[8,64,128]{2,1,0:T(8,128)}, u32[]{:S(2)}, u32[]{:S(2)}) collective-permute-start(f32[8,64,128]{2,1,0:T(8,128)S(1)} %fusion.27), channel_id=1, source_target_pairs={{0,1},{1,0},{2,3},{3,2},{4,5},{5,4},{6,7},{7,6},{8,9},{9,8},{10,11... | collective-permute-start | bytes 786440 | tf_op jit(solution)/shard_map/ppermute | solution.py:21
  50.1 55.3 %copy-start.6 = (f32[8]{0:T(128)S(1)}, f32[8]{0:T(128)}, u32[]{:S(2)}) copy-start(f32[8]{0:T(128)} %constant.36.clone) | copy-start | bytes 100
  50.1 8.2 %collective-permute-start.1 = (f32[7,64,128]{2,1,0:T(8,128)S(1)}, f32[7,64,128]{2,1,0:T(8,128)S(1)}, u32[]{:S(2)}, u32[]{:S(2)}) collective-permute-start(f32[7,64,128]{2,1,0:T(8,128)S(1)} %slice_add_fusion), channel_id=1, source_target_pairs={{0,2},{1,3},{2,0},{3,1},{4,6},{5,7},{6,4},{7,5},{8,10},{9,11},{10,... | collective-permute-start | bytes 688136 | tf_op jit(solution)/shard_map/ppermute | solution.py:21
  58.4 12.4 %collective-permute-start.2 = (f32[6,64,128]{2,1,0:T(8,128)S(1)}, f32[6,64,128]{2,1,0:T(8,128)S(1)}, u32[]{:S(2)}, u32[]{:S(2)}) collective-permute-start(f32[6,64,128]{2,1,0:T(8,128)S(1)} %slice_add_fusion.1), channel_id=1, source_target_pairs={{0,4},{1,5},{2,6},{3,7},{4,0},{5,1},{6,2},{7,3},{8,12},{9,13},{10,... | collective-permute-start | bytes 589832 | tf_op jit(solution)/shard_map/ppermute | solution.py:21
  70.7 13.4 %collective-permute-start.3 = (f32[5,64,128]{2,1,0:T(8,128)S(1)}, f32[5,64,128]{2,1,0:T(8,128)S(1)}, u32[]{:S(2)}, u32[]{:S(2)}) collective-permute-start(f32[5,64,128]{2,1,0:T(8,128)S(1)} %slice_add_fusion.2), channel_id=1, source_target_pairs={{0,8},{1,9},{2,10},{3,11},{4,12},{5,13},{6,14},{7,15},{8,0},{9,1},... | collective-permute-start | bytes 491528 | tf_op jit(solution)/shard_map/ppermute | solution.py:21
  84.1 5.1 %collective-permute-start.4 = (f32[4,64,128]{2,1,0:T(8,128)S(1)}, f32[4,64,128]{2,1,0:T(8,128)S(1)}, u32[]{:S(2)}, u32[]{:S(2)}) collective-permute-start(f32[4,64,128]{2,1,0:T(8,128)S(1)} %slice_add_fusion.3), channel_id=1, source_target_pairs={{0,16},{1,17},{2,18},{3,19},{4,20},{5,21},{6,22},{7,23},{8,24},{9,... | collective-permute-start | bytes 393224 | tf_op jit(solution)/shard_map/ppermute | solution.py:21
  89.2 6.2 %collective-permute-start.5 = (f32[3,64,128]{2,1,0:T(8,128)S(1)}, f32[3,64,128]{2,1,0:T(8,128)S(1)}, u32[]{:S(2)}, u32[]{:S(2)}) collective-permute-start(f32[3,64,128]{2,1,0:T(8,128)S(1)} %slice_add_fusion.4), channel_id=1, source_target_pairs={{0,32},{1,33},{2,34},{3,35},{4,36},{5,37},{6,38},{7,39},{8,40},{9,... | collective-permute-start | bytes 294920 | tf_op jit(solution)/shard_map/ppermute | solution.py:21
  95.4 4.5 %collective-permute-start.6 = (f32[2,64,128]{2,1,0:T(8,128)S(1)}, f32[2,64,128]{2,1,0:T(8,128)S(1)}, u32[]{:S(2)}, u32[]{:S(2)}) collective-permute-start(f32[2,64,128]{2,1,0:T(8,128)S(1)} %slice_add_fusion.5), channel_id=1, source_target_pairs={{0,64},{1,65},{2,66},{3,67},{4,68},{5,69},{6,70},{7,71},{8,72},{9,... | collective-permute-start | bytes 196616 | tf_op jit(solution)/shard_map/ppermute | solution.py:21
  99.9 5.5 %collective-permute-start.7 = (f32[1,64,128]{2,1,0:T(8,128)S(1)}, f32[1,64,128]{2,1,0:T(8,128)S(1)}, u32[]{:S(2)}, u32[]{:S(2)}) collective-permute-start(f32[1,64,128]{2,1,0:T(8,128)S(1)} %get-tuple-element.16), channel_id=1, source_target_pairs={{0,128},{1,129},{2,130},{3,131},{4,132},{5,133},{6,134},{7,135},{8... | collective-permute-start | bytes 98312 | tf_op jit(solution)/shard_map/ppermute | solution.py:21

commit v5 on v3

--- a/solution.py
+++ b/solution.py
@@ -157,9 +157,10 @@
         "lrk,lpk->rp", level_bases[local_levels:], weights, preferred_element_type=jnp.float32
     )
     result = jnp.where(live_rows, accumulated, jnp.zeros_like(accumulated)).astype(jnp.bfloat16)
-    return lax.dot_general(
-        onehot, result, (((0,), (0,)), ((), ())), preferred_element_type=jnp.float32
-    ).astype(jnp.bfloat16)
+    inverse = (jnp.arange(per_device, dtype=jnp.int32)[:, None] == slot_order[None, :]).astype(
+        jnp.bfloat16
+    )
+    return jnp.dot(inverse, result, preferred_element_type=jnp.float32).astype(jnp.bfloat16)
 
 
 def solution(mesh):

time: 116 us -> 115 us (level)
  matrix products: 36.3 us -> 35 us
    dot_general x1, matrix products: 15.8 us -> 14.6 us  [body(): jnp.dot(inverse, result, preferred_element_type=jnp.float32)]
  transfers between devices with their start and end apart: 8 -> 8, of which waited for: 2 -> 2; matrix products, arithmetic and copies ran while one was open for 8% -> 8% of each run, Pallas kernels for 35% -> 36%
where the time goes in v5:
time: 115 us; the launch traced here: 113 us
  Pallas kernels  40.4 us (35%)
  matrix products  35 us (30%)
  starting transfers between devices  18.7 us (16%)
  local copies, waits for them, and re-layouts  9.71 us (8%)
  waiting for transfers between devices  4.7 us (4%)
  other arithmetic  4.54 us (4%)
    pallas_call x8, Pallas kernels, dense_rows(): pl.pallas_call(dense_kernel, grid=(rows // BLOCK,), in_specs=[pl.BlockSpe...  40.4 us
    ppermute x8, starting transfers between devices, swapped(): lax.ppermute(x, axis, [(i, i ^ 1 << bit) for i in range(lax.axis_size(axi...  18.7 us
    dot_general x1, matrix products, body(): jnp.dot(inverse, result, preferred_element_type=jnp.float32)  14.6 us
    dot_general x1, matrix products, body(): lax.dot_general(onehot, jnp.concatenate([lhs_features, rhs_features.T, ve...  12.5 us
    dot_general x1, matrix products, body(): jnp.einsum('lrk,lpk->rp', level_bases[local_levels:], weights, preferred_...  5.37 us
    squeeze x7, local copies, waits for them, and re-layouts, body(): gate = received[0, :8]  4.82 us
    ppermute x8, waiting for transfers between devices, swapped(): lax.ppermute(x, axis, [(i, i ^ 1 << bit) for i in range(lax.axis_size(axi...  4.7 us
  transfers between devices with their start and end apart: 8, of which 2 were waited for; matrix products, arithmetic and copies ran while one was open for 8% of the time, Pallas kernels for 36%

profile of v5, /device:TPU:6, one launch (start us, length us, event | category | flops | bytes accessed | tf_op | source)
XLA Modules:
  0.0 113.3 jit_solution(18108273917379269302)
XLA Ops:
  0.0 0.0 copy-start
  0.0 1.1 broadcast_multiply_fusion
  1.1 0.2 fusion.30
  1.3 0.0 copy-done
  1.3 0.1 broadcast_bitcast_fusion
  1.5 0.5 concatenate.12
  1.9 0.0 slice-start
  1.9 0.5 concatenate.11
  2.4 0.0 copy-done.5
  2.4 0.0 copy-done.4
  2.4 0.0 slice-start.1
  2.4 0.0 slice-start.2
  2.4 12.5 %fusion.8.rows_ref.leaf_ref = bf16[4096,192]{1,0:T(8,128)(2,1)S(1)} fusion(s32[4096]{0:T(1024)S(1)} %bitcast.58, bf16[4096,64]{0,1:T(8,128)(2,1)S(1)} %copy-done.4, bf16[4096,64]{0,1:T(8,128)(2,1)S(1)} %bitcast.55, bf16[4096,64]{0,1:T(8,128)(2,1)S(1)} %bitcast.56), kind=kOutput, calls=%fused_computation.10 | convolution fusion | flops 6464733184 | bytes 3162112 | tf_op jit(solution)/shard_map/dot_general | solution.py:95
  15.0 0.0 copy-start.1
  15.0 2.2 %slice_select_fusion.vec_ref = bf16[4096,64]{1,0:T(8,128)(2,1)S(1)} fusion(bf16[4096,192]{1,0:T(8,128)(2,1)S(1)} %fusion.8.rows_ref.leaf_ref, pred[4096]{0:T(1024)(128)(4,1)S(1)} %fusion.31), kind=kLoop, calls=%fused_computation.24 | loop fusion | flops 262144 | bytes 1052672 | tf_op jit(solution)/shard_map/jit(_where)/select_n | solution.py:105
  17.2 0.0 slice-done
  17.2 0.0 slice-done.1
  17.2 0.0 slice-done.2
  17.2 0.0 copy-start.2
  17.2 1.6 %fusion.21 = f32[8,64,128]{2,1,0:T(8,128)S(1)} fusion(bf16[9,4096,128]{2,1,0:T(8,128)(2,1)S(1)} %bitcast.52, bf16[4096,64]{1,0:T(8,128)(2,1)S(1)} %slice_select_fusion.vec_ref), kind=kOutput, calls=%fused_computation.23 | convolution fusion | flops 536870912 | bytes 9699328 | tf_op jit(solution)/shard_map/rp,lrk->lpk/dot_general | solution.py:107
  18.8 0.0 copy-done.1
  18.8 0.0 copy-start.3
  18.8 0.3 collective-permute-start
  19.1 0.1 slice.161
  19.2 0.3 copy-done.3
  19.5 0.5 fusion.45
  20.0 0.5 convolution_bitcast_fusion
  20.5 0.6 copy.18
  21.1 0.6 broadcast_in_dim.41.gate_ref
  21.7 1.4 %broadcast_4_acc_ref.2.acc_ref = f32[4096,64]{1,0:T(8,128)} broadcast(f32[]{:T(128)} %constant.33.clone.1), dimensions={} | broadcast | bytes 1048580 | tf_op jit(solution)/shard_map/broadcast.4.acc_ref
  23.2 5.0 %shard_map.82.acc_ref = f32[4096,64]{1,0:T(8,128)} custom-call(bf16[4096,192]{1,0:T(8,128)(2,1)} %copy-done.1, bf16[4096,192]{1,0:T(8,128)(2,1)} %copy-done.1, bf16[4096,64]{1,0:T(8,128)(2,1)} %copy-done.2, f32[8,128]{1,0:T(8,128)} %broadcast_in_dim.41.gate_ref, f32[4096,64]{1,0:T(8,128)} %broadcast_4_acc_ref.2.acc_ref), custom_call_target="tpu_custom_call", output_to_operand_aliasing={{}: (4, {})} | custom-call | tf_op jit(solution)/shard_map/pallas_call | solution.py:68
  28.2 0.0 collective-permute-done
  28.2 1.0 slice_add_fusion
  29.2 2.0 %collective-permute-start.1 = (f32[7,64,128]{2,1,0:T(8,128)S(1)}, f32[7,64,128]{2,1,0:T(8,128)S(1)}, u32[]{:S(2)}, u32[]{:S(2)}) collective-permute-start(f32[7,64,128]{2,1,0:T(8,128)S(1)} %slice_add_fusion), channel_id=1, source_target_pairs={{0,2},{1,3},{2,0},{3,1},{4,6},{5,7},{6,4},{7,5},{8,10},{9,11},{10,... | collective-permute-start | bytes 688136 | tf_op jit(solution)/shard_map/ppermute | solution.py:21
  31.2 1.3 %slice_bitcast_fusion.gate_ref = f32[8,128]{1,0:T(8,128)} fusion(f32[8,64,128]{2,1,0:T(8,128)} %collective-permute-done), kind=kLoop, calls=%fused_computation.81 | loop fusion | bytes 8192 | tf_op jit(solution)/shard_map/squeeze | solution.py:125
  32.5 5.1 %shard_map.83.acc_ref = f32[4096,64]{1,0:T(8,128)} custom-call(bf16[4096,192]{1,0:T(8,128)(2,1)} %copy-done.1, bf16[4096,192]{1,0:T(8,128)(2,1)} %copy-done.1, bf16[4096,64]{1,0:T(8,128)(2,1)} %copy-done.2, f32[8,128]{1,0:T(8,128)} %slice_bitcast_fusion.gate_ref, f32[4096,64]{1,0:T(8,128)} %shard_map.82.acc_ref), custom_call_target="tpu_custom_call", output_to_operand_aliasing={{}: (4, {})} | custom-call | tf_op jit(solution)/shard_map/pallas_call | solution.py:68
  37.5 0.8 slice_dynamic-update-slice_fusion.6
  38.3 0.0 collective-permute-done.1
  38.3 3.4 %collective-permute-start.2 = (f32[6,64,128]{2,1,0:T(8,128)S(1)}, f32[6,64,128]{2,1,0:T(8,128)S(1)}, u32[]{:S(2)}, u32[]{:S(2)}) collective-permute-start(f32[6,64,128]{2,1,0:T(8,128)S(1)} %slice_add_fusion.1), channel_id=1, source_target_pairs={{0,4},{1,5},{2,6},{3,7},{4,0},{5,1},{6,2},{7,3},{8,12},{9,13},{10,... | collective-permute-start | bytes 589832 | tf_op jit(solution)/shard_map/ppermute | solution.py:21
  41.7 0.6 slice_bitcast_fusion.1.gate_ref
  42.3 5.0 %shard_map.84.acc_ref = f32[4096,64]{1,0:T(8,128)} custom-call(bf16[4096,192]{1,0:T(8,128)(2,1)} %copy-done.1, bf16[4096,192]{1,0:T(8,128)(2,1)} %copy-done.1, bf16[4096,64]{1,0:T(8,128)(2,1)} %copy-done.2, f32[8,128]{1,0:T(8,128)} %slice_bitcast_fusion.1.gate_ref, f32[4096,64]{1,0:T(8,128)} %shard_map.83.acc_ref), custom_call_target="tpu_custom_call", output_to_operand_aliasing={{}: (4, {})} | custom-call | tf_op jit(solution)/shard_map/pallas_call | solution.py:68
  47.3 3.3 %collective-permute-done.2 = f32[6,64,128]{2,1,0:T(8,128)S(1)} collective-permute-done((f32[6,64,128]{2,1,0:T(8,128)S(1)}, f32[6,64,128]{2,1,0:T(8,128)S(1)}, u32[]{:S(2)}, u32[]{:S(2)}) %collective-permute-start.2) | collective-permute-done | bytes 196640 | tf_op jit(solution)/shard_map/ppermute | solution.py:21
  50.6 6.0 %collective-permute-start.3 = (f32[5,64,128]{2,1,0:T(8,128)S(1)}, f32[5,64,128]{2,1,0:T(8,128)S(1)}, u32[]{:S(2)}, u32[]{:S(2)}) collective-permute-start(f32[5,64,128]{2,1,0:T(8,128)S(1)} %slice_add_fusion.2), channel_id=1, source_target_pairs={{0,8},{1,9},{2,10},{3,11},{4,12},{5,13},{6,14},{7,15},{8,0},{9,1},... | collective-permute-start | bytes 491528 | tf_op jit(solution)/shard_map/ppermute | solution.py:21
  56.7 0.6 slice_bitcast_fusion.2.gate_ref
  57.3 5.1 %shard_map.85.acc_ref = f32[4096,64]{1,0:T(8,128)} custom-call(bf16[4096,192]{1,0:T(8,128)(2,1)} %copy-done.1, bf16[4096,192]{1,0:T(8,128)(2,1)} %copy-done.1, bf16[4096,64]{1,0:T(8,128)(2,1)} %copy-done.2, f32[8,128]{1,0:T(8,128)} %slice_bitcast_fusion.2.gate_ref, f32[4096,64]{1,0:T(8,128)} %shard_map.84.acc_ref), custom_call_target="tpu_custom_call", output_to_operand_aliasing={{}: (4, {})} | custom-call | tf_op jit(solution)/shard_map/pallas_call | solution.py:68
  62.3 1.4 %collective-permute-done.3 = f32[5,64,128]{2,1,0:T(8,128)S(1)} collective-permute-done((f32[5,64,128]{2,1,0:T(8,128)S(1)}, f32[5,64,128]{2,1,0:T(8,128)S(1)}, u32[]{:S(2)}, u32[]{:S(2)}) %collective-permute-start.3) | collective-permute-done | bytes 163872 | tf_op jit(solution)/shard_map/ppermute | solution.py:21
  63.8 0.9 collective-permute-start.4
  64.7 0.6 slice_bitcast_fusion.3.gate_ref
  65.3 5.0 %shard_map.86.acc_ref = f32[4096,64]{1,0:T(8,128)} custom-call(bf16[4096,192]{1,0:T(8,128)(2,1)} %copy-done.1, bf16[4096,192]{1,0:T(8,128)(2,1)} %copy-done.1, bf16[4096,64]{1,0:T(8,128)(2,1)} %copy-done.2, f32[8,128]{1,0:T(8,128)} %slice_bitcast_fusion.3.gate_ref, f32[4096,64]{1,0:T(8,128)} %shard_map.85.acc_ref), custom_call_target="tpu_custom_call", output_to_operand_aliasing={{}: (4, {})} | custom-call | tf_op jit(solution)/shard_map/pallas_call | solution.py:68
  70.3 0.0 collective-permute-done.4
  70.3 1.2 %collective-permute-start.5 = (f32[3,64,128]{2,1,0:T(8,128)S(1)}, f32[3,64,128]{2,1,0:T(8,128)S(1)}, u32[]{:S(2)}, u32[]{:S(2)}) collective-permute-start(f32[3,64,128]{2,1,0:T(8,128)S(1)} %slice_add_fusion.4), channel_id=1, source_target_pairs={{0,32},{1,33},{2,34},{3,35},{4,36},{5,37},{6,38},{7,39},{8,40},{9,... | collective-permute-start | bytes 294920 | tf_op jit(solution)/shard_map/ppermute | solution.py:21
  71.5 0.6 slice_bitcast_fusion.4.gate_ref
  72.1 5.0 %shard_map.87.acc_ref = f32[4096,64]{1,0:T(8,128)} custom-call(bf16[4096,192]{1,0:T(8,128)(2,1)} %copy-done.1, bf16[4096,192]{1,0:T(8,128)(2,1)} %copy-done.1, bf16[4096,64]{1,0:T(8,128)(2,1)} %copy-done.2, f32[8,128]{1,0:T(8,128)} %slice_bitcast_fusion.4.gate_ref, f32[4096,64]{1,0:T(8,128)} %shard_map.86.acc_ref), custom_call_target="tpu_custom_call", output_to_operand_aliasing={{}: (4, {})} | custom-call | tf_op jit(solution)/shard_map/pallas_call | solution.py:68
  77.2 0.0 collective-permute-done.5
  77.2 1.9 %collective-permute-start.6 = (f32[2,64,128]{2,1,0:T(8,128)S(1)}, f32[2,64,128]{2,1,0:T(8,128)S(1)}, u32[]{:S(2)}, u32[]{:S(2)}) collective-permute-start(f32[2,64,128]{2,1,0:T(8,128)S(1)} %slice_add_fusion.5), channel_id=1, source_target_pairs={{0,64},{1,65},{2,66},{3,67},{4,68},{5,69},{6,70},{7,71},{8,72},{9,... | collective-permute-start | bytes 196616 | tf_op jit(solution)/shard_map/ppermute | solution.py:21
  79.1 0.6 slice_bitcast_fusion.5.gate_ref
  79.7 5.0 %shard_map.88.acc_ref = f32[4096,64]{1,0:T(8,128)} custom-call(bf16[4096,192]{1,0:T(8,128)(2,1)} %copy-done.1, bf16[4096,192]{1,0:T(8,128)(2,1)} %copy-done.1, bf16[4096,64]{1,0:T(8,128)(2,1)} %copy-done.2, f32[8,128]{1,0:T(8,128)} %slice_bitcast_fusion.5.gate_ref, f32[4096,64]{1,0:T(8,128)} %shard_map.87.acc_ref), custom_call_target="tpu_custom_call", output_to_operand_aliasing={{}: (4, {})} | custom-call | tf_op jit(solution)/shard_map/pallas_call | solution.py:68
  84.7 0.0 collective-permute-done.6
  84.7 3.0 %collective-permute-start.7 = (f32[1,64,128]{2,1,0:T(8,128)S(1)}, f32[1,64,128]{2,1,0:T(8,128)S(1)}, u32[]{:S(2)}, u32[]{:S(2)}) collective-permute-start(f32[1,64,128]{2,1,0:T(8,128)S(1)} %get-tuple-element.16), channel_id=1, source_target_pairs={{0,128},{1,129},{2,130},{3,131},{4,132},{5,133},{6,134},{7,135},{8... | collective-permute-start | bytes 98312 | tf_op jit(solution)/shard_map/ppermute | solution.py:21
  87.7 0.6 slice_bitcast_fusion.6.gate_ref
  88.3 5.0 %shard_map.89 = f32[4096,64]{1,0:T(8,128)} custom-call(bf16[4096,192]{1,0:T(8,128)(2,1)} %copy-done.1, bf16[4096,192]{1,0:T(8,128)(2,1)} %copy-done.1, bf16[4096,64]{1,0:T(8,128)(2,1)} %copy-done.2, f32[8,128]{1,0:T(8,128)} %slice_bitcast_fusion.6.gate_ref, f32[4096,64]{1,0:T(8,128)} %shard_map.88.acc_ref), custom_call_target="tpu_custom_call", output_to_operand_aliasing={{}: (4, {})} | custom-call | tf_op jit(solution)/shard_map/pallas_call | solution.py:68
  93.4 0.0 collective-permute-done.7
  93.4 5.4 %fusion.15 = bf16[4096,64]{1,0:T(8,128)(2,1)S(1)} fusion(f32[4096,64]{1,0:T(8,128)} %shard_map.89, f32[2,2048,64]{2,1,0:T(8,128)S(1)} %copy.18, pred[4096]{0:T(1024)(128)(4,1)S(1)} %fusion.31, bf16[9,4096,128]{2,1,0:T(8,128)(2,1)} %param.12, f32[8,64,128]{2,1,0:T(8,128)S(1)} %constant_dynamic-update-slice_fusion, f32[8,128]{1,0:T(8,128)S(1)} %slice_multiply_fusion.8, ...), kind=kOutput, calls=%fused_computation.17 | convolution fusion | flops 538116096 | bytes 12328992 | tf_op jit(solution)/shard_map/lrk,lpk->rp/dot_general | solution.py:156
  98.8 14.6 %fusion.12 = bf16[4096,64]{0,1:T(8,128)(2,1)} fusion(bf16[4096,64]{1,0:T(8,128)(2,1)S(1)} %fusion.15, s32[4096]{0:T(1024)S(1)} %bitcast.59), kind=kOutput, calls=%fused_computation.12 | convolution fusion | flops 2164523008 | bytes 1064960 | tf_op jit(solution)/shard_map/dot_general | solution.py:163
  (27 shorter events, 0.2 us)
Async XLA Ops:
  0.0 1.3 %copy-start = (s32[2]{0:T(128)S(1)}, s32[2]{0:T(128)}, u32[]{:S(2)}) copy-start(s32[2]{0:T(128)} %param.11) | copy-start | bytes 28
  0.0 2.4 %copy-start.5 = (s32[1,4096]{1,0:T(1,128)S(1)}, s32[1,4096]{1,0:T(1,128)}, u32[]{:S(2)}) copy-start(s32[1,4096]{1,0:T(1,128)} %param.10) | copy-start | bytes 49156
  0.0 2.4 %copy-start.4 = (bf16[4096,64]{0,1:T(8,128)(2,1)S(1)}, bf16[4096,64]{0,1:T(8,128)(2,1)}, u32[]{:S(2)}) copy-start(bf16[4096,64]{0,1:T(8,128)(2,1)} %param.8) | copy-start | bytes 1572868
  1.9 15.2 %slice-start = ((s8[9437184]{0:T(1024)(128)(4,1)}), s8[1048576]{0:T(1024)(128)(4,1)S(1)}, s32[]{:S(2)}) async-start(s8[9437184]{0:T(1024)(128)(4,1)} %bitcast.51), calls=%async_computation | async-start | bytes 2097152
  2.4 14.8 %slice-start.1 = ((s8[9437184]{0:T(1024)(128)(4,1)}), s8[4194304]{0:T(1024)(128)(4,1)S(1)}, s32[]{:S(2)}) async-start(s8[9437184]{0:T(1024)(128)(4,1)} %bitcast.51), calls=%async_computation.1 | async-start | bytes 8388608
  2.4 14.7 %slice-start.2 = ((s8[9437184]{0:T(1024)(128)(4,1)}), s8[4194304]{0:T(1024)(128)(4,1)S(1)}, s32[]{:S(2)}) async-start(s8[9437184]{0:T(1024)(128)(4,1)} %bitcast.51), calls=%async_computation.2 | async-start | bytes 8388608
  15.0 3.8 %copy-start.1 = (bf16[4096,192]{1,0:T(8,128)(2,1)}, bf16[4096,192]{1,0:T(8,128)(2,1)S(1)}, u32[]{:S(2)}) copy-start(bf16[4096,192]{1,0:T(8,128)(2,1)S(1)} %fusion.8.rows_ref.leaf_ref) | copy-start | bytes 4718596
  17.2 2.3 %copy-start.2 = (bf16[4096,64]{1,0:T(8,128)(2,1)}, bf16[4096,64]{1,0:T(8,128)(2,1)S(1)}, u32[]{:S(2)}) copy-start(bf16[4096,64]{1,0:T(8,128)(2,1)S(1)} %slice_select_fusion.vec_ref) | copy-start | bytes 1572868
  18.8 0.7 copy-start.3
  18.8 9.4 %collective-permute-start = (f32[8,64,128]{2,1,0:T(8,128)S(1)}, f32[8,64,128]{2,1,0:T(8,128)}, u32[]{:S(2)}, u32[]{:S(2)}) collective-permute-start(f32[8,64,128]{2,1,0:T(8,128)S(1)} %fusion.21), channel_id=1, source_target_pairs={{0,1},{1,0},{2,3},{3,2},{4,5},{5,4},{6,7},{7,6},{8,9},{9,8},{10,11... | collective-permute-start | bytes 786440 | tf_op jit(solution)/shard_map/ppermute | solution.py:21
  29.2 9.1 %collective-permute-start.1 = (f32[7,64,128]{2,1,0:T(8,128)S(1)}, f32[7,64,128]{2,1,0:T(8,128)S(1)}, u32[]{:S(2)}, u32[]{:S(2)}) collective-permute-start(f32[7,64,128]{2,1,0:T(8,128)S(1)} %slice_add_fusion), channel_id=1, source_target_pairs={{0,2},{1,3},{2,0},{3,1},{4,6},{5,7},{6,4},{7,5},{8,10},{9,11},{10,... | collective-permute-start | bytes 688136 | tf_op jit(solution)/shard_map/ppermute | solution.py:21
  38.3 12.3 %collective-permute-start.2 = (f32[6,64,128]{2,1,0:T(8,128)S(1)}, f32[6,64,128]{2,1,0:T(8,128)S(1)}, u32[]{:S(2)}, u32[]{:S(2)}) collective-permute-start(f32[6,64,128]{2,1,0:T(8,128)S(1)} %slice_add_fusion.1), channel_id=1, source_target_pairs={{0,4},{1,5},{2,6},{3,7},{4,0},{5,1},{6,2},{7,3},{8,12},{9,13},{10,... | collective-permute-start | bytes 589832 | tf_op jit(solution)/shard_map/ppermute | solution.py:21
  50.6 13.1 %collective-permute-start.3 = (f32[5,64,128]{2,1,0:T(8,128)S(1)}, f32[5,64,128]{2,1,0:T(8,128)S(1)}, u32[]{:S(2)}, u32[]{:S(2)}) collective-permute-start(f32[5,64,128]{2,1,0:T(8,128)S(1)} %slice_add_fusion.2), channel_id=1, source_target_pairs={{0,8},{1,9},{2,10},{3,11},{4,12},{5,13},{6,14},{7,15},{8,0},{9,1},... | collective-permute-start | bytes 491528 | tf_op jit(solution)/shard_map/ppermute | solution.py:21
  63.8 6.5 %collective-permute-start.4 = (f32[4,64,128]{2,1,0:T(8,128)S(1)}, f32[4,64,128]{2,1,0:T(8,128)S(1)}, u32[]{:S(2)}, u32[]{:S(2)}) collective-permute-start(f32[4,64,128]{2,1,0:T(8,128)S(1)} %slice_add_fusion.3), channel_id=1, source_target_pairs={{0,16},{1,17},{2,18},{3,19},{4,20},{5,21},{6,22},{7,23},{8,24},{9,... | collective-permute-start | bytes 393224 | tf_op jit(solution)/shard_map/ppermute | solution.py:21
  70.3 6.8 %collective-permute-start.5 = (f32[3,64,128]{2,1,0:T(8,128)S(1)}, f32[3,64,128]{2,1,0:T(8,128)S(1)}, u32[]{:S(2)}, u32[]{:S(2)}) collective-permute-start(f32[3,64,128]{2,1,0:T(8,128)S(1)} %slice_add_fusion.4), channel_id=1, source_target_pairs={{0,32},{1,33},{2,34},{3,35},{4,36},{5,37},{6,38},{7,39},{8,40},{9,... | collective-permute-start | bytes 294920 | tf_op jit(solution)/shard_map/ppermute | solution.py:21
  77.2 7.5 %collective-permute-start.6 = (f32[2,64,128]{2,1,0:T(8,128)S(1)}, f32[2,64,128]{2,1,0:T(8,128)S(1)}, u32[]{:S(2)}, u32[]{:S(2)}) collective-permute-start(f32[2,64,128]{2,1,0:T(8,128)S(1)} %slice_add_fusion.5), channel_id=1, source_target_pairs={{0,64},{1,65},{2,66},{3,67},{4,68},{5,69},{6,70},{7,71},{8,72},{9,... | collective-permute-start | bytes 196616 | tf_op jit(solution)/shard_map/ppermute | solution.py:21
  84.7 8.6 %collective-permute-start.7 = (f32[1,64,128]{2,1,0:T(8,128)S(1)}, f32[1,64,128]{2,1,0:T(8,128)S(1)}, u32[]{:S(2)}, u32[]{:S(2)}) collective-permute-start(f32[1,64,128]{2,1,0:T(8,128)S(1)} %get-tuple-element.16), channel_id=1, source_target_pairs={{0,128},{1,129},{2,130},{3,131},{4,132},{5,133},{6,134},{7,135},{8... | collective-permute-start | bytes 98312 | tf_op jit(solution)/shard_map/ppermute | solution.py:21
  88.3 5.1 %copy-start.6 = (f32[8]{0:T(128)S(1)}, f32[8]{0:T(128)}, u32[]{:S(2)}) copy-start(f32[8]{0:T(128)} %constant.36.clone) | copy-start | bytes 100

commit v6 on v5

--- a/solution.py
+++ b/solution.py
@@ -64,7 +64,7 @@
 def dense_rows(acc, table, vec, gate, row_start, rows):
     leaf = row_start // LEAF
     first = row_start // BLOCK
-    width = table.shape[1]
+    width = 2 * FEATURES
     return pl.pallas_call(
         dense_kernel,
         grid=(rows // BLOCK,),

time: 115 us -> 114 us (level)
  Pallas kernels: 40.4 us -> 38.8 us
    pallas_call x8, Pallas kernels: 40.4 us -> 38.8 us  [dense_rows(): pl.pallas_call(dense_kernel, grid=(rows // BLOCK,), in_specs=[pl.BlockSpe...]
  transfers between devices with their start and end apart: 8 -> 8, of which waited for: 2 -> 2; matrix products, arithmetic and copies ran while one was open for 8% -> 8% of each run, Pallas kernels for 36% -> 35%
where the time goes in v6:
time: 114 us; the launch traced here: 112 us
  Pallas kernels  38.8 us (34%)
  matrix products  35 us (31%)
  starting transfers between devices  18.7 us (16%)
  local copies, waits for them, and re-layouts  9.71 us (9%)
  waiting for transfers between devices  5.08 us (4%)
  other arithmetic  4.54 us (4%)
    pallas_call x8, Pallas kernels, dense_rows(): pl.pallas_call(dense_kernel, grid=(rows // BLOCK,), in_specs=[pl.BlockSpe...  38.8 us
    ppermute x8, starting transfers between devices, swapped(): lax.ppermute(x, axis, [(i, i ^ 1 << bit) for i in range(lax.axis_size(axi...  18.7 us
    dot_general x1, matrix products, body(): jnp.dot(inverse, result, preferred_element_type=jnp.float32)  14.6 us
    dot_general x1, matrix products, body(): lax.dot_general(onehot, jnp.concatenate([lhs_features, rhs_features.T, ve...  12.5 us
    dot_general x1, matrix products, body(): jnp.einsum('lrk,lpk->rp', level_bases[local_levels:], weights, preferred_...  5.37 us
    ppermute x8, waiting for transfers between devices, swapped(): lax.ppermute(x, axis, [(i, i ^ 1 << bit) for i in range(lax.axis_size(axi...  5.08 us
    squeeze x7, local copies, waits for them, and re-layouts, body(): gate = received[0, :8]  4.82 us
  transfers between devices with their start and end apart: 8, of which 2 were waited for; matrix products, arithmetic and copies ran while one was open for 8% of the time, Pallas kernels for 35%

profile of v6, /device:TPU:6, one launch (start us, length us, event | category | flops | bytes accessed | tf_op | source)
XLA Modules:
  0.0 112.1 jit_solution(1370089638390362218)
XLA Ops:
  0.0 0.0 copy-start
  0.0 1.1 broadcast_multiply_fusion
  1.1 0.2 fusion.30
  1.3 0.0 copy-done
  1.3 0.1 broadcast_bitcast_fusion
  1.5 0.5 concatenate.12
  1.9 0.0 slice-start
  1.9 0.5 concatenate.11
  2.4 0.0 copy-done.5
  2.4 0.0 copy-done.4
  2.4 0.0 slice-start.1
  2.4 0.0 slice-start.2
  2.4 12.5 %fusion.8.rows_ref.leaf_ref = bf16[4096,192]{1,0:T(8,128)(2,1)S(1)} fusion(s32[4096]{0:T(1024)S(1)} %bitcast.58, bf16[4096,64]{0,1:T(8,128)(2,1)S(1)} %copy-done.4, bf16[4096,64]{0,1:T(8,128)(2,1)S(1)} %bitcast.55, bf16[4096,64]{0,1:T(8,128)(2,1)S(1)} %bitcast.56), kind=kOutput, calls=%fused_computation.10 | convolution fusion | flops 6464733184 | bytes 3162112 | tf_op jit(solution)/shard_map/dot_general | solution.py:95
  15.0 0.0 copy-start.1
  15.0 2.2 %slice_select_fusion.vec_ref = bf16[4096,64]{1,0:T(8,128)(2,1)S(1)} fusion(bf16[4096,192]{1,0:T(8,128)(2,1)S(1)} %fusion.8.rows_ref.leaf_ref, pred[4096]{0:T(1024)(128)(4,1)S(1)} %fusion.31), kind=kLoop, calls=%fused_computation.24 | loop fusion | flops 262144 | bytes 1052672 | tf_op jit(solution)/shard_map/jit(_where)/select_n | solution.py:105
  17.2 0.0 slice-done
  17.2 0.0 slice-done.1
  17.2 0.0 slice-done.2
  17.2 0.0 copy-start.2
  17.2 1.6 %fusion.21 = f32[8,64,128]{2,1,0:T(8,128)S(1)} fusion(bf16[9,4096,128]{2,1,0:T(8,128)(2,1)S(1)} %bitcast.52, bf16[4096,64]{1,0:T(8,128)(2,1)S(1)} %slice_select_fusion.vec_ref), kind=kOutput, calls=%fused_computation.23 | convolution fusion | flops 536870912 | bytes 9699328 | tf_op jit(solution)/shard_map/rp,lrk->lpk/dot_general | solution.py:107
  18.8 0.0 copy-done.1
  18.8 0.0 copy-start.3
  18.8 0.3 collective-permute-start
  19.1 0.1 slice.161
  19.2 0.3 copy-done.3
  19.5 0.5 fusion.45
  20.0 0.5 convolution_bitcast_fusion
  20.5 0.6 copy.18
  21.1 0.6 broadcast_in_dim.41.gate_ref
  21.7 1.4 %broadcast_4_acc_ref.2.acc_ref = f32[4096,64]{1,0:T(8,128)} broadcast(f32[]{:T(128)} %constant.33.clone.1), dimensions={} | broadcast | bytes 1048580 | tf_op jit(solution)/shard_map/broadcast.4.acc_ref
  23.2 4.8 %shard_map.82.acc_ref = f32[4096,64]{1,0:T(8,128)} custom-call(bf16[4096,192]{1,0:T(8,128)(2,1)} %copy-done.1, bf16[4096,192]{1,0:T(8,128)(2,1)} %copy-done.1, bf16[4096,64]{1,0:T(8,128)(2,1)} %copy-done.2, f32[8,128]{1,0:T(8,128)} %broadcast_in_dim.41.gate_ref, f32[4096,64]{1,0:T(8,128)} %broadcast_4_acc_ref.2.acc_ref), custom_call_target="tpu_custom_call", output_to_operand_aliasing={{}: (4, {})} | custom-call | tf_op jit(solution)/shard_map/pallas_call | solution.py:68
  28.0 0.0 collective-permute-done
  28.0 1.0 slice_add_fusion
  29.0 2.0 %collective-permute-start.1 = (f32[7,64,128]{2,1,0:T(8,128)S(1)}, f32[7,64,128]{2,1,0:T(8,128)S(1)}, u32[]{:S(2)}, u32[]{:S(2)}) collective-permute-start(f32[7,64,128]{2,1,0:T(8,128)S(1)} %slice_add_fusion), channel_id=1, source_target_pairs={{0,2},{1,3},{2,0},{3,1},{4,6},{5,7},{6,4},{7,5},{8,10},{9,11},{10,... | collective-permute-start | bytes 688136 | tf_op jit(solution)/shard_map/ppermute | solution.py:21
  31.0 1.3 %slice_bitcast_fusion.gate_ref = f32[8,128]{1,0:T(8,128)} fusion(f32[8,64,128]{2,1,0:T(8,128)} %collective-permute-done), kind=kLoop, calls=%fused_computation.81 | loop fusion | bytes 8192 | tf_op jit(solution)/shard_map/squeeze | solution.py:125
  32.3 4.9 %shard_map.83.acc_ref = f32[4096,64]{1,0:T(8,128)} custom-call(bf16[4096,192]{1,0:T(8,128)(2,1)} %copy-done.1, bf16[4096,192]{1,0:T(8,128)(2,1)} %copy-done.1, bf16[4096,64]{1,0:T(8,128)(2,1)} %copy-done.2, f32[8,128]{1,0:T(8,128)} %slice_bitcast_fusion.gate_ref, f32[4096,64]{1,0:T(8,128)} %shard_map.82.acc_ref), custom_call_target="tpu_custom_call", output_to_operand_aliasing={{}: (4, {})} | custom-call | tf_op jit(solution)/shard_map/pallas_call | solution.py:68
  37.1 0.8 slice_dynamic-update-slice_fusion.6
  37.9 0.0 collective-permute-done.1
  37.9 3.4 %collective-permute-start.2 = (f32[6,64,128]{2,1,0:T(8,128)S(1)}, f32[6,64,128]{2,1,0:T(8,128)S(1)}, u32[]{:S(2)}, u32[]{:S(2)}) collective-permute-start(f32[6,64,128]{2,1,0:T(8,128)S(1)} %slice_add_fusion.1), channel_id=1, source_target_pairs={{0,4},{1,5},{2,6},{3,7},{4,0},{5,1},{6,2},{7,3},{8,12},{9,13},{10,... | collective-permute-start | bytes 589832 | tf_op jit(solution)/shard_map/ppermute | solution.py:21
  41.3 0.6 slice_bitcast_fusion.1.gate_ref
  41.9 4.8 %shard_map.84.acc_ref = f32[4096,64]{1,0:T(8,128)} custom-call(bf16[4096,192]{1,0:T(8,128)(2,1)} %copy-done.1, bf16[4096,192]{1,0:T(8,128)(2,1)} %copy-done.1, bf16[4096,64]{1,0:T(8,128)(2,1)} %copy-done.2, f32[8,128]{1,0:T(8,128)} %slice_bitcast_fusion.1.gate_ref, f32[4096,64]{1,0:T(8,128)} %shard_map.83.acc_ref), custom_call_target="tpu_custom_call", output_to_operand_aliasing={{}: (4, {})} | custom-call | tf_op jit(solution)/shard_map/pallas_call | solution.py:68
  46.7 3.5 %collective-permute-done.2 = f32[6,64,128]{2,1,0:T(8,128)S(1)} collective-permute-done((f32[6,64,128]{2,1,0:T(8,128)S(1)}, f32[6,64,128]{2,1,0:T(8,128)S(1)}, u32[]{:S(2)}, u32[]{:S(2)}) %collective-permute-start.2) | collective-permute-done | bytes 196640 | tf_op jit(solution)/shard_map/ppermute | solution.py:21
  50.2 6.1 %collective-permute-start.3 = (f32[5,64,128]{2,1,0:T(8,128)S(1)}, f32[5,64,128]{2,1,0:T(8,128)S(1)}, u32[]{:S(2)}, u32[]{:S(2)}) collective-permute-start(f32[5,64,128]{2,1,0:T(8,128)S(1)} %slice_add_fusion.2), channel_id=1, source_target_pairs={{0,8},{1,9},{2,10},{3,11},{4,12},{5,13},{6,14},{7,15},{8,0},{9,1},... | collective-permute-start | bytes 491528 | tf_op jit(solution)/shard_map/ppermute | solution.py:21
  56.3 0.6 slice_bitcast_fusion.2.gate_ref
  56.9 4.9 %shard_map.85.acc_ref = f32[4096,64]{1,0:T(8,128)} custom-call(bf16[4096,192]{1,0:T(8,128)(2,1)} %copy-done.1, bf16[4096,192]{1,0:T(8,128)(2,1)} %copy-done.1, bf16[4096,64]{1,0:T(8,128)(2,1)} %copy-done.2, f32[8,128]{1,0:T(8,128)} %slice_bitcast_fusion.2.gate_ref, f32[4096,64]{1,0:T(8,128)} %shard_map.84.acc_ref), custom_call_target="tpu_custom_call", output_to_operand_aliasing={{}: (4, {})} | custom-call | tf_op jit(solution)/shard_map/pallas_call | solution.py:68
  61.7 1.6 %collective-permute-done.3 = f32[5,64,128]{2,1,0:T(8,128)S(1)} collective-permute-done((f32[5,64,128]{2,1,0:T(8,128)S(1)}, f32[5,64,128]{2,1,0:T(8,128)S(1)}, u32[]{:S(2)}, u32[]{:S(2)}) %collective-permute-start.3) | collective-permute-done | bytes 163872 | tf_op jit(solution)/shard_map/ppermute | solution.py:21
  63.4 0.9 collective-permute-start.4
  64.3 0.6 slice_bitcast_fusion.3.gate_ref
  64.9 4.8 %shard_map.86.acc_ref = f32[4096,64]{1,0:T(8,128)} custom-call(bf16[4096,192]{1,0:T(8,128)(2,1)} %copy-done.1, bf16[4096,192]{1,0:T(8,128)(2,1)} %copy-done.1, bf16[4096,64]{1,0:T(8,128)(2,1)} %copy-done.2, f32[8,128]{1,0:T(8,128)} %slice_bitcast_fusion.3.gate_ref, f32[4096,64]{1,0:T(8,128)} %shard_map.85.acc_ref), custom_call_target="tpu_custom_call", output_to_operand_aliasing={{}: (4, {})} | custom-call | tf_op jit(solution)/shard_map/pallas_call | solution.py:68
  69.7 0.0 collective-permute-done.4
  69.7 1.2 %collective-permute-start.5 = (f32[3,64,128]{2,1,0:T(8,128)S(1)}, f32[3,64,128]{2,1,0:T(8,128)S(1)}, u32[]{:S(2)}, u32[]{:S(2)}) collective-permute-start(f32[3,64,128]{2,1,0:T(8,128)S(1)} %slice_add_fusion.4), channel_id=1, source_target_pairs={{0,32},{1,33},{2,34},{3,35},{4,36},{5,37},{6,38},{7,39},{8,40},{9,... | collective-permute-start | bytes 294920 | tf_op jit(solution)/shard_map/ppermute | solution.py:21
  71.0 0.6 slice_bitcast_fusion.4.gate_ref
  71.5 4.8 %shard_map.87.acc_ref = f32[4096,64]{1,0:T(8,128)} custom-call(bf16[4096,192]{1,0:T(8,128)(2,1)} %copy-done.1, bf16[4096,192]{1,0:T(8,128)(2,1)} %copy-done.1, bf16[4096,64]{1,0:T(8,128)(2,1)} %copy-done.2, f32[8,128]{1,0:T(8,128)} %slice_bitcast_fusion.4.gate_ref, f32[4096,64]{1,0:T(8,128)} %shard_map.86.acc_ref), custom_call_target="tpu_custom_call", output_to_operand_aliasing={{}: (4, {})} | custom-call | tf_op jit(solution)/shard_map/pallas_call | solution.py:68
  76.4 0.0 collective-permute-done.5
  76.4 1.9 %collective-permute-start.6 = (f32[2,64,128]{2,1,0:T(8,128)S(1)}, f32[2,64,128]{2,1,0:T(8,128)S(1)}, u32[]{:S(2)}, u32[]{:S(2)}) collective-permute-start(f32[2,64,128]{2,1,0:T(8,128)S(1)} %slice_add_fusion.5), channel_id=1, source_target_pairs={{0,64},{1,65},{2,66},{3,67},{4,68},{5,69},{6,70},{7,71},{8,72},{9,... | collective-permute-start | bytes 196616 | tf_op jit(solution)/shard_map/ppermute | solution.py:21
  78.3 0.6 slice_bitcast_fusion.5.gate_ref
  78.9 4.8 %shard_map.88.acc_ref = f32[4096,64]{1,0:T(8,128)} custom-call(bf16[4096,192]{1,0:T(8,128)(2,1)} %copy-done.1, bf16[4096,192]{1,0:T(8,128)(2,1)} %copy-done.1, bf16[4096,64]{1,0:T(8,128)(2,1)} %copy-done.2, f32[8,128]{1,0:T(8,128)} %slice_bitcast_fusion.5.gate_ref, f32[4096,64]{1,0:T(8,128)} %shard_map.87.acc_ref), custom_call_target="tpu_custom_call", output_to_operand_aliasing={{}: (4, {})} | custom-call | tf_op jit(solution)/shard_map/pallas_call | solution.py:68
  83.7 0.0 collective-permute-done.6
  83.7 3.0 %collective-permute-start.7 = (f32[1,64,128]{2,1,0:T(8,128)S(1)}, f32[1,64,128]{2,1,0:T(8,128)S(1)}, u32[]{:S(2)}, u32[]{:S(2)}) collective-permute-start(f32[1,64,128]{2,1,0:T(8,128)S(1)} %get-tuple-element.16), channel_id=1, source_target_pairs={{0,128},{1,129},{2,130},{3,131},{4,132},{5,133},{6,134},{7,135},{8... | collective-permute-start | bytes 98312 | tf_op jit(solution)/shard_map/ppermute | solution.py:21
  86.7 0.6 slice_bitcast_fusion.6.gate_ref
  87.3 4.9 %shard_map.89 = f32[4096,64]{1,0:T(8,128)} custom-call(bf16[4096,192]{1,0:T(8,128)(2,1)} %copy-done.1, bf16[4096,192]{1,0:T(8,128)(2,1)} %copy-done.1, bf16[4096,64]{1,0:T(8,128)(2,1)} %copy-done.2, f32[8,128]{1,0:T(8,128)} %slice_bitcast_fusion.6.gate_ref, f32[4096,64]{1,0:T(8,128)} %shard_map.88.acc_ref), custom_call_target="tpu_custom_call", output_to_operand_aliasing={{}: (4, {})} | custom-call | tf_op jit(solution)/shard_map/pallas_call | solution.py:68
  92.2 0.0 collective-permute-done.7
  92.2 5.4 %fusion.15 = bf16[4096,64]{1,0:T(8,128)(2,1)S(1)} fusion(f32[4096,64]{1,0:T(8,128)} %shard_map.89, f32[2,2048,64]{2,1,0:T(8,128)S(1)} %copy.18, pred[4096]{0:T(1024)(128)(4,1)S(1)} %fusion.31, bf16[9,4096,128]{2,1,0:T(8,128)(2,1)} %param.12, f32[8,64,128]{2,1,0:T(8,128)S(1)} %constant_dynamic-update-slice_fusion, f32[8,128]{1,0:T(8,128)S(1)} %slice_multiply_fusion.8, ...), kind=kOutput, calls=%fused_computation.17 | convolution fusion | flops 538116096 | bytes 12328992 | tf_op jit(solution)/shard_map/lrk,lpk->rp/dot_general | solution.py:156
  97.6 14.6 %fusion.12 = bf16[4096,64]{0,1:T(8,128)(2,1)} fusion(bf16[4096,64]{1,0:T(8,128)(2,1)S(1)} %fusion.15, s32[4096]{0:T(1024)S(1)} %bitcast.59), kind=kOutput, calls=%fused_computation.12 | convolution fusion | flops 2164523008 | bytes 1064960 | tf_op jit(solution)/shard_map/dot_general | solution.py:163
  (27 shorter events, 0.2 us)
Async XLA Ops:
  0.0 1.3 %copy-start = (s32[2]{0:T(128)S(1)}, s32[2]{0:T(128)}, u32[]{:S(2)}) copy-start(s32[2]{0:T(128)} %param.11) | copy-start | bytes 28
  0.0 2.4 %copy-start.5 = (s32[1,4096]{1,0:T(1,128)S(1)}, s32[1,4096]{1,0:T(1,128)}, u32[]{:S(2)}) copy-start(s32[1,4096]{1,0:T(1,128)} %param.10) | copy-start | bytes 49156
  0.0 2.4 %copy-start.4 = (bf16[4096,64]{0,1:T(8,128)(2,1)S(1)}, bf16[4096,64]{0,1:T(8,128)(2,1)}, u32[]{:S(2)}) copy-start(bf16[4096,64]{0,1:T(8,128)(2,1)} %param.8) | copy-start | bytes 1572868
  1.9 15.2 %slice-start = ((s8[9437184]{0:T(1024)(128)(4,1)}), s8[1048576]{0:T(1024)(128)(4,1)S(1)}, s32[]{:S(2)}) async-start(s8[9437184]{0:T(1024)(128)(4,1)} %bitcast.51), calls=%async_computation | async-start | bytes 2097152
  2.4 14.8 %slice-start.1 = ((s8[9437184]{0:T(1024)(128)(4,1)}), s8[4194304]{0:T(1024)(128)(4,1)S(1)}, s32[]{:S(2)}) async-start(s8[9437184]{0:T(1024)(128)(4,1)} %bitcast.51), calls=%async_computation.1 | async-start | bytes 8388608
  2.4 14.7 %slice-start.2 = ((s8[9437184]{0:T(1024)(128)(4,1)}), s8[4194304]{0:T(1024)(128)(4,1)S(1)}, s32[]{:S(2)}) async-start(s8[9437184]{0:T(1024)(128)(4,1)} %bitcast.51), calls=%async_computation.2 | async-start | bytes 8388608
  15.0 3.8 %copy-start.1 = (bf16[4096,192]{1,0:T(8,128)(2,1)}, bf16[4096,192]{1,0:T(8,128)(2,1)S(1)}, u32[]{:S(2)}) copy-start(bf16[4096,192]{1,0:T(8,128)(2,1)S(1)} %fusion.8.rows_ref.leaf_ref) | copy-start | bytes 4718596
  17.2 2.3 %copy-start.2 = (bf16[4096,64]{1,0:T(8,128)(2,1)}, bf16[4096,64]{1,0:T(8,128)(2,1)S(1)}, u32[]{:S(2)}) copy-start(bf16[4096,64]{1,0:T(8,128)(2,1)S(1)} %slice_select_fusion.vec_ref) | copy-start | bytes 1572868
  18.8 0.7 copy-start.3
  18.8 9.2 %collective-permute-start = (f32[8,64,128]{2,1,0:T(8,128)S(1)}, f32[8,64,128]{2,1,0:T(8,128)}, u32[]{:S(2)}, u32[]{:S(2)}) collective-permute-start(f32[8,64,128]{2,1,0:T(8,128)S(1)} %fusion.21), channel_id=1, source_target_pairs={{0,1},{1,0},{2,3},{3,2},{4,5},{5,4},{6,7},{7,6},{8,9},{9,8},{10,11... | collective-permute-start | bytes 786440 | tf_op jit(solution)/shard_map/ppermute | solution.py:21
  29.0 8.9 %collective-permute-start.1 = (f32[7,64,128]{2,1,0:T(8,128)S(1)}, f32[7,64,128]{2,1,0:T(8,128)S(1)}, u32[]{:S(2)}, u32[]{:S(2)}) collective-permute-start(f32[7,64,128]{2,1,0:T(8,128)S(1)} %slice_add_fusion), channel_id=1, source_target_pairs={{0,2},{1,3},{2,0},{3,1},{4,6},{5,7},{6,4},{7,5},{8,10},{9,11},{10,... | collective-permute-start | bytes 688136 | tf_op jit(solution)/shard_map/ppermute | solution.py:21
  37.9 12.3 %collective-permute-start.2 = (f32[6,64,128]{2,1,0:T(8,128)S(1)}, f32[6,64,128]{2,1,0:T(8,128)S(1)}, u32[]{:S(2)}, u32[]{:S(2)}) collective-permute-start(f32[6,64,128]{2,1,0:T(8,128)S(1)} %slice_add_fusion.1), channel_id=1, source_target_pairs={{0,4},{1,5},{2,6},{3,7},{4,0},{5,1},{6,2},{7,3},{8,12},{9,13},{10,... | collective-permute-start | bytes 589832 | tf_op jit(solution)/shard_map/ppermute | solution.py:21
  50.2 13.1 %collective-permute-start.3 = (f32[5,64,128]{2,1,0:T(8,128)S(1)}, f32[5,64,128]{2,1,0:T(8,128)S(1)}, u32[]{:S(2)}, u32[]{:S(2)}) collective-permute-start(f32[5,64,128]{2,1,0:T(8,128)S(1)} %slice_add_fusion.2), channel_id=1, source_target_pairs={{0,8},{1,9},{2,10},{3,11},{4,12},{5,13},{6,14},{7,15},{8,0},{9,1},... | collective-permute-start | bytes 491528 | tf_op jit(solution)/shard_map/ppermute | solution.py:21
  63.4 6.4 %collective-permute-start.4 = (f32[4,64,128]{2,1,0:T(8,128)S(1)}, f32[4,64,128]{2,1,0:T(8,128)S(1)}, u32[]{:S(2)}, u32[]{:S(2)}) collective-permute-start(f32[4,64,128]{2,1,0:T(8,128)S(1)} %slice_add_fusion.3), channel_id=1, source_target_pairs={{0,16},{1,17},{2,18},{3,19},{4,20},{5,21},{6,22},{7,23},{8,24},{9,... | collective-permute-start | bytes 393224 | tf_op jit(solution)/shard_map/ppermute | solution.py:21
  69.7 6.6 %collective-permute-start.5 = (f32[3,64,128]{2,1,0:T(8,128)S(1)}, f32[3,64,128]{2,1,0:T(8,128)S(1)}, u32[]{:S(2)}, u32[]{:S(2)}) collective-permute-start(f32[3,64,128]{2,1,0:T(8,128)S(1)} %slice_add_fusion.4), channel_id=1, source_target_pairs={{0,32},{1,33},{2,34},{3,35},{4,36},{5,37},{6,38},{7,39},{8,40},{9,... | collective-permute-start | bytes 294920 | tf_op jit(solution)/shard_map/ppermute | solution.py:21
  76.4 7.3 %collective-permute-start.6 = (f32[2,64,128]{2,1,0:T(8,128)S(1)}, f32[2,64,128]{2,1,0:T(8,128)S(1)}, u32[]{:S(2)}, u32[]{:S(2)}) collective-permute-start(f32[2,64,128]{2,1,0:T(8,128)S(1)} %slice_add_fusion.5), channel_id=1, source_target_pairs={{0,64},{1,65},{2,66},{3,67},{4,68},{5,69},{6,70},{7,71},{8,72},{9,... | collective-permute-start | bytes 196616 | tf_op jit(solution)/shard_map/ppermute | solution.py:21
  83.7 8.4 %collective-permute-start.7 = (f32[1,64,128]{2,1,0:T(8,128)S(1)}, f32[1,64,128]{2,1,0:T(8,128)S(1)}, u32[]{:S(2)}, u32[]{:S(2)}) collective-permute-start(f32[1,64,128]{2,1,0:T(8,128)S(1)} %get-tuple-element.16), channel_id=1, source_target_pairs={{0,128},{1,129},{2,130},{3,131},{4,132},{5,133},{6,134},{7,135},{8... | collective-permute-start | bytes 98312 | tf_op jit(solution)/shard_map/ppermute | solution.py:21
  87.3 4.9 %copy-start.6 = (f32[8]{0:T(128)S(1)}, f32[8]{0:T(128)}, u32[]{:S(2)}) copy-start(f32[8]{0:T(128)} %constant.36.clone) | copy-start | bytes 100

commit v7 on v6

--- a/solution.py
+++ b/solution.py
@@ -48,8 +48,8 @@
     return lhs.T, rhs
 
 
-def dense_kernel(rows_ref, leaf_ref, vec_ref, gate_ref, acc_ref, out_ref):
-    del gate_ref, acc_ref
+def dense_kernel(rows_ref, leaf_ref, vec_ref, gate_ref, *refs):
+    out_ref = refs[-1]
     squared = lax.dot_general(
         rows_ref[:, :FEATURES],
         leaf_ref[:, FEATURES : 2 * FEATURES],
@@ -65,20 +65,26 @@
     leaf = row_start // LEAF
     first = row_start // BLOCK
     width = 2 * FEATURES
+    in_specs = [
+        pl.BlockSpec((BLOCK, width), lambda i: (first + i, 0)),
+        pl.BlockSpec((LEAF, width), lambda i: (leaf, 0)),
+        pl.BlockSpec((LEAF, PANEL), lambda i: (leaf, 0)),
+        pl.BlockSpec(memory_space=pl.ANY),
+    ]
+    operands = [table, table, vec, gate]
+    aliases = {}
+    if acc is not None:
+        in_specs.append(pl.BlockSpec(memory_space=pl.ANY))
+        operands.append(acc)
+        aliases = {4: 0}
     return pl.pallas_call(
         dense_kernel,
         grid=(rows // BLOCK,),
-        in_specs=[
-            pl.BlockSpec((BLOCK, width), lambda i: (first + i, 0)),
-            pl.BlockSpec((LEAF, width), lambda i: (leaf, 0)),
-            pl.BlockSpec((LEAF, PANEL), lambda i: (leaf, 0)),
-            pl.BlockSpec(memory_space=pl.ANY),
-            pl.BlockSpec(memory_space=pl.ANY),
-        ],
+        in_specs=in_specs,
         out_specs=pl.BlockSpec((BLOCK, PANEL), lambda i: (first + i, 0)),
-        out_shape=jax.ShapeDtypeStruct(acc.shape, jnp.float32),
-        input_output_aliases={4: 0},
-    )(table, table, vec, gate, acc)
+        out_shape=jax.ShapeDtypeStruct((table.shape[0], PANEL), jnp.float32),
+        input_output_aliases=aliases,
+    )(*operands)
 
 
 def body(vectors, contexts, tree_order, live_counts, level_bases, coupling, length_scale):
@@ -109,7 +115,7 @@
     )
     block_rows = min(512, LEAF)
     chunk_starts = list(range(0, per_device, block_rows))
-    accumulated = jnp.zeros((per_device, PANEL), jnp.float32)
+    accumulated = None
     stack = partials
     finished = []
     gate = jnp.zeros((8, RANK), jnp.float32)

time: 114 us -> 112 us (0.982)
  local copies, waits for them, and re-layouts: 9.71 us -> 8.26 us
    another operation x1 -> x0, local copies, waits for them, and re-layouts: 1.44 us -> none
  transfers between devices with their start and end apart: 8 -> 8, of which waited for: 2 -> 2; matrix products, arithmetic and copies ran while one was open for 8% -> 7% of each run, Pallas kernels for 35% -> 35%
where the time goes in v7:
time: 112 us; the launch traced here: 111 us
  Pallas kernels  38.8 us (35%)
  matrix products  35 us (31%)
  starting transfers between devices  18.6 us (17%)
  local copies, waits for them, and re-layouts  8.26 us (7%)
  waiting for transfers between devices  5.14 us (5%)
  other arithmetic  4.54 us (4%)
    pallas_call x8, Pallas kernels, dense_rows(): pl.pallas_call(dense_kernel, grid=(rows // BLOCK,), in_specs=in_specs, ou...  38.8 us
    ppermute x8, starting transfers between devices, swapped(): lax.ppermute(x, axis, [(i, i ^ 1 << bit) for i in range(lax.axis_size(axi...  18.6 us
    dot_general x1, matrix products, body(): jnp.dot(inverse, result, preferred_element_type=jnp.float32)  14.6 us
    dot_general x1, matrix products, body(): lax.dot_general(onehot, jnp.concatenate([lhs_features, rhs_features.T, ve...  12.5 us
    dot_general x1, matrix products, body(): jnp.einsum('lrk,lpk->rp', level_bases[local_levels:], weights, preferred_...  5.37 us
    ppermute x8, waiting for transfers between devices, swapped(): lax.ppermute(x, axis, [(i, i ^ 1 << bit) for i in range(lax.axis_size(axi...  5.14 us
    squeeze x7, local copies, waits for them, and re-layouts, body(): gate = received[0, :8]  4.82 us
  transfers between devices with their start and end apart: 8, of which 2 were waited for; matrix products, arithmetic and copies ran while one was open for 7% of the time, Pallas kernels for 35%

profile of v7, /device:TPU:6, one launch (start us, length us, event | category | flops | bytes accessed | tf_op | source)
XLA Modules:
  0.0 110.7 jit_solution(13362959595899829774)
XLA Ops:
  0.0 0.0 copy-start
  0.0 1.1 broadcast_multiply_fusion
  1.1 0.2 fusion.30
  1.3 0.0 copy-done
  1.3 0.1 broadcast_bitcast_fusion
  1.5 0.5 concatenate.11
  1.9 0.0 slice-start
  1.9 0.5 concatenate.12
  2.4 0.0 copy-done.5
  2.4 0.0 copy-done.4
  2.4 0.0 slice-start.1
  2.4 0.0 slice-start.2
  2.4 12.5 %fusion.8.rows_ref.leaf_ref = bf16[4096,192]{1,0:T(8,128)(2,1)S(1)} fusion(s32[4096]{0:T(1024)S(1)} %bitcast.58, bf16[4096,64]{0,1:T(8,128)(2,1)S(1)} %copy-done.4, bf16[4096,64]{0,1:T(8,128)(2,1)S(1)} %bitcast.56, bf16[4096,64]{0,1:T(8,128)(2,1)S(1)} %bitcast.55), kind=kOutput, calls=%fused_computation.10 | convolution fusion | flops 6464733184 | bytes 3162112 | tf_op jit(solution)/shard_map/dot_general | solution.py:101
  15.0 0.0 copy-start.1
  15.0 2.2 %slice_select_fusion.vec_ref = bf16[4096,64]{1,0:T(8,128)(2,1)S(1)} fusion(bf16[4096,192]{1,0:T(8,128)(2,1)S(1)} %fusion.8.rows_ref.leaf_ref, pred[4096]{0:T(1024)(128)(4,1)S(1)} %fusion.31), kind=kLoop, calls=%fused_computation.24 | loop fusion | flops 262144 | bytes 1052672 | tf_op jit(solution)/shard_map/jit(_where)/select_n | solution.py:111
  17.2 0.0 slice-done
  17.2 0.0 slice-done.1
  17.2 0.0 slice-done.2
  17.2 0.0 copy-start.2
  17.2 1.6 %fusion.21 = f32[8,64,128]{2,1,0:T(8,128)S(1)} fusion(bf16[9,4096,128]{2,1,0:T(8,128)(2,1)S(1)} %bitcast.52, bf16[4096,64]{1,0:T(8,128)(2,1)S(1)} %slice_select_fusion.vec_ref), kind=kOutput, calls=%fused_computation.23 | convolution fusion | flops 536870912 | bytes 9699328 | tf_op jit(solution)/shard_map/rp,lrk->lpk/dot_general | solution.py:113
  18.8 0.0 copy-done.1
  18.8 0.0 copy-start.3
  18.8 0.3 collective-permute-start
  19.1 0.1 slice.161
  19.2 0.3 copy-done.3
  19.5 0.0 copy-done.2
  19.5 0.5 fusion.45
  20.0 0.5 convolution_bitcast_fusion
  20.5 0.6 broadcast_in_dim.44.gate_ref
  21.1 4.8 %shard_map.82.refs_0_ = f32[4096,64]{1,0:T(8,128)} custom-call(bf16[4096,192]{1,0:T(8,128)(2,1)} %copy-done.1, bf16[4096,192]{1,0:T(8,128)(2,1)} %copy-done.1, bf16[4096,64]{1,0:T(8,128)(2,1)} %copy-done.2, f32[8,128]{1,0:T(8,128)} %broadcast_in_dim.44.gate_ref), custom_call_target="tpu_custom_call" | custom-call | tf_op jit(solution)/shard_map/pallas_call | solution.py:80
  26.0 0.6 copy.17
  26.6 0.0 collective-permute-done
  26.6 1.0 slice_add_fusion
  27.6 2.0 %collective-permute-start.1 = (f32[7,64,128]{2,1,0:T(8,128)S(1)}, f32[7,64,128]{2,1,0:T(8,128)S(1)}, u32[]{:S(2)}, u32[]{:S(2)}) collective-permute-start(f32[7,64,128]{2,1,0:T(8,128)S(1)} %slice_add_fusion), channel_id=1, source_target_pairs={{0,2},{1,3},{2,0},{3,1},{4,6},{5,7},{6,4},{7,5},{8,10},{9,11},{10,... | collective-permute-start | bytes 688136 | tf_op jit(solution)/shard_map/ppermute | solution.py:21
  29.6 1.3 %slice_bitcast_fusion.gate_ref = f32[8,128]{1,0:T(8,128)} fusion(f32[8,64,128]{2,1,0:T(8,128)} %collective-permute-done), kind=kLoop, calls=%fused_computation.81 | loop fusion | bytes 8192 | tf_op jit(solution)/shard_map/squeeze | solution.py:131
  30.8 4.9 %shard_map.83.refs_0_ = f32[4096,64]{1,0:T(8,128)} custom-call(bf16[4096,192]{1,0:T(8,128)(2,1)} %copy-done.1, bf16[4096,192]{1,0:T(8,128)(2,1)} %copy-done.1, bf16[4096,64]{1,0:T(8,128)(2,1)} %copy-done.2, f32[8,128]{1,0:T(8,128)} %slice_bitcast_fusion.gate_ref, f32[4096,64]{1,0:T(8,128)} %shard_map.82.refs_0_), custom_call_target="tpu_custom_call", output_to_operand_aliasing={{}: (4, {})} | custom-call | tf_op jit(solution)/shard_map/pallas_call | solution.py:80
  35.7 0.8 slice_dynamic-update-slice_fusion.6
  36.5 0.0 collective-permute-done.1
  36.5 3.4 %collective-permute-start.2 = (f32[6,64,128]{2,1,0:T(8,128)S(1)}, f32[6,64,128]{2,1,0:T(8,128)S(1)}, u32[]{:S(2)}, u32[]{:S(2)}) collective-permute-start(f32[6,64,128]{2,1,0:T(8,128)S(1)} %slice_add_fusion.1), channel_id=1, source_target_pairs={{0,4},{1,5},{2,6},{3,7},{4,0},{5,1},{6,2},{7,3},{8,12},{9,13},{10,... | collective-permute-start | bytes 589832 | tf_op jit(solution)/shard_map/ppermute | solution.py:21
  39.8 0.6 slice_bitcast_fusion.1.gate_ref
  40.4 4.9 %shard_map.84.refs_0_ = f32[4096,64]{1,0:T(8,128)} custom-call(bf16[4096,192]{1,0:T(8,128)(2,1)} %copy-done.1, bf16[4096,192]{1,0:T(8,128)(2,1)} %copy-done.1, bf16[4096,64]{1,0:T(8,128)(2,1)} %copy-done.2, f32[8,128]{1,0:T(8,128)} %slice_bitcast_fusion.1.gate_ref, f32[4096,64]{1,0:T(8,128)} %shard_map.83.refs_0_), custom_call_target="tpu_custom_call", output_to_operand_aliasing={{}: (4, {})} | custom-call | tf_op jit(solution)/shard_map/pallas_call | solution.py:80
  45.3 3.5 %collective-permute-done.2 = f32[6,64,128]{2,1,0:T(8,128)S(1)} collective-permute-done((f32[6,64,128]{2,1,0:T(8,128)S(1)}, f32[6,64,128]{2,1,0:T(8,128)S(1)}, u32[]{:S(2)}, u32[]{:S(2)}) %collective-permute-start.2) | collective-permute-done | bytes 196640 | tf_op jit(solution)/shard_map/ppermute | solution.py:21
  48.8 6.0 %collective-permute-start.3 = (f32[5,64,128]{2,1,0:T(8,128)S(1)}, f32[5,64,128]{2,1,0:T(8,128)S(1)}, u32[]{:S(2)}, u32[]{:S(2)}) collective-permute-start(f32[5,64,128]{2,1,0:T(8,128)S(1)} %slice_add_fusion.2), channel_id=1, source_target_pairs={{0,8},{1,9},{2,10},{3,11},{4,12},{5,13},{6,14},{7,15},{8,0},{9,1},... | collective-permute-start | bytes 491528 | tf_op jit(solution)/shard_map/ppermute | solution.py:21
  54.8 0.6 slice_bitcast_fusion.2.gate_ref
  55.4 4.9 %shard_map.85.refs_0_ = f32[4096,64]{1,0:T(8,128)} custom-call(bf16[4096,192]{1,0:T(8,128)(2,1)} %copy-done.1, bf16[4096,192]{1,0:T(8,128)(2,1)} %copy-done.1, bf16[4096,64]{1,0:T(8,128)(2,1)} %copy-done.2, f32[8,128]{1,0:T(8,128)} %slice_bitcast_fusion.2.gate_ref, f32[4096,64]{1,0:T(8,128)} %shard_map.84.refs_0_), custom_call_target="tpu_custom_call", output_to_operand_aliasing={{}: (4, {})} | custom-call | tf_op jit(solution)/shard_map/pallas_call | solution.py:80
  60.3 1.7 %collective-permute-done.3 = f32[5,64,128]{2,1,0:T(8,128)S(1)} collective-permute-done((f32[5,64,128]{2,1,0:T(8,128)S(1)}, f32[5,64,128]{2,1,0:T(8,128)S(1)}, u32[]{:S(2)}, u32[]{:S(2)}) %collective-permute-start.3) | collective-permute-done | bytes 163872 | tf_op jit(solution)/shard_map/ppermute | solution.py:21
  62.0 0.9 collective-permute-start.4
  62.8 0.6 slice_bitcast_fusion.3.gate_ref
  63.4 4.8 %shard_map.86.refs_0_ = f32[4096,64]{1,0:T(8,128)} custom-call(bf16[4096,192]{1,0:T(8,128)(2,1)} %copy-done.1, bf16[4096,192]{1,0:T(8,128)(2,1)} %copy-done.1, bf16[4096,64]{1,0:T(8,128)(2,1)} %copy-done.2, f32[8,128]{1,0:T(8,128)} %slice_bitcast_fusion.3.gate_ref, f32[4096,64]{1,0:T(8,128)} %shard_map.85.refs_0_), custom_call_target="tpu_custom_call", output_to_operand_aliasing={{}: (4, {})} | custom-call | tf_op jit(solution)/shard_map/pallas_call | solution.py:80
  68.3 0.0 collective-permute-done.4
  68.3 1.2 %collective-permute-start.5 = (f32[3,64,128]{2,1,0:T(8,128)S(1)}, f32[3,64,128]{2,1,0:T(8,128)S(1)}, u32[]{:S(2)}, u32[]{:S(2)}) collective-permute-start(f32[3,64,128]{2,1,0:T(8,128)S(1)} %slice_add_fusion.4), channel_id=1, source_target_pairs={{0,32},{1,33},{2,34},{3,35},{4,36},{5,37},{6,38},{7,39},{8,40},{9,... | collective-permute-start | bytes 294920 | tf_op jit(solution)/shard_map/ppermute | solution.py:21
  69.5 0.6 slice_bitcast_fusion.4.gate_ref
  70.1 4.8 %shard_map.87.refs_0_ = f32[4096,64]{1,0:T(8,128)} custom-call(bf16[4096,192]{1,0:T(8,128)(2,1)} %copy-done.1, bf16[4096,192]{1,0:T(8,128)(2,1)} %copy-done.1, bf16[4096,64]{1,0:T(8,128)(2,1)} %copy-done.2, f32[8,128]{1,0:T(8,128)} %slice_bitcast_fusion.4.gate_ref, f32[4096,64]{1,0:T(8,128)} %shard_map.86.refs_0_), custom_call_target="tpu_custom_call", output_to_operand_aliasing={{}: (4, {})} | custom-call | tf_op jit(solution)/shard_map/pallas_call | solution.py:80
  74.9 0.0 collective-permute-done.5
  75.0 1.9 %collective-permute-start.6 = (f32[2,64,128]{2,1,0:T(8,128)S(1)}, f32[2,64,128]{2,1,0:T(8,128)S(1)}, u32[]{:S(2)}, u32[]{:S(2)}) collective-permute-start(f32[2,64,128]{2,1,0:T(8,128)S(1)} %slice_add_fusion.5), channel_id=1, source_target_pairs={{0,64},{1,65},{2,66},{3,67},{4,68},{5,69},{6,70},{7,71},{8,72},{9,... | collective-permute-start | bytes 196616 | tf_op jit(solution)/shard_map/ppermute | solution.py:21
  76.9 0.6 slice_bitcast_fusion.5.gate_ref
  77.5 4.8 %shard_map.88.refs_0_ = f32[4096,64]{1,0:T(8,128)} custom-call(bf16[4096,192]{1,0:T(8,128)(2,1)} %copy-done.1, bf16[4096,192]{1,0:T(8,128)(2,1)} %copy-done.1, bf16[4096,64]{1,0:T(8,128)(2,1)} %copy-done.2, f32[8,128]{1,0:T(8,128)} %slice_bitcast_fusion.5.gate_ref, f32[4096,64]{1,0:T(8,128)} %shard_map.87.refs_0_), custom_call_target="tpu_custom_call", output_to_operand_aliasing={{}: (4, {})} | custom-call | tf_op jit(solution)/shard_map/pallas_call | solution.py:80
  82.3 0.0 collective-permute-done.6
  82.3 3.0 %collective-permute-start.7 = (f32[1,64,128]{2,1,0:T(8,128)S(1)}, f32[1,64,128]{2,1,0:T(8,128)S(1)}, u32[]{:S(2)}, u32[]{:S(2)}) collective-permute-start(f32[1,64,128]{2,1,0:T(8,128)S(1)} %get-tuple-element.16), channel_id=1, source_target_pairs={{0,128},{1,129},{2,130},{3,131},{4,132},{5,133},{6,134},{7,135},{8... | collective-permute-start | bytes 98312 | tf_op jit(solution)/shard_map/ppermute | solution.py:21
  85.3 0.6 slice_bitcast_fusion.6.gate_ref
  85.9 4.9 %shard_map.89 = f32[4096,64]{1,0:T(8,128)} custom-call(bf16[4096,192]{1,0:T(8,128)(2,1)} %copy-done.1, bf16[4096,192]{1,0:T(8,128)(2,1)} %copy-done.1, bf16[4096,64]{1,0:T(8,128)(2,1)} %copy-done.2, f32[8,128]{1,0:T(8,128)} %slice_bitcast_fusion.6.gate_ref, f32[4096,64]{1,0:T(8,128)} %shard_map.88.refs_0_), custom_call_target="tpu_custom_call", output_to_operand_aliasing={{}: (4, {})} | custom-call | tf_op jit(solution)/shard_map/pallas_call | solution.py:80
  90.8 0.0 collective-permute-done.7
  90.8 5.4 %fusion.15 = bf16[4096,64]{1,0:T(8,128)(2,1)S(1)} fusion(f32[4096,64]{1,0:T(8,128)} %shard_map.89, f32[2,2048,64]{2,1,0:T(8,128)S(1)} %copy.17, pred[4096]{0:T(1024)(128)(4,1)S(1)} %fusion.31, bf16[9,4096,128]{2,1,0:T(8,128)(2,1)} %param.12, f32[8,64,128]{2,1,0:T(8,128)S(1)} %constant_dynamic-update-slice_fusion, f32[8,128]{1,0:T(8,128)S(1)} %slice_multiply_fusion.8, ...), kind=kOutput, calls=%fused_computation.17 | convolution fusion | flops 538116096 | bytes 12328992 | tf_op jit(solution)/shard_map/lrk,lpk->rp/dot_general | solution.py:162
  96.2 14.6 %fusion.12 = bf16[4096,64]{0,1:T(8,128)(2,1)} fusion(bf16[4096,64]{1,0:T(8,128)(2,1)S(1)} %fusion.15, s32[4096]{0:T(1024)S(1)} %bitcast.59), kind=kOutput, calls=%fused_computation.12 | convolution fusion | flops 2164523008 | bytes 1064960 | tf_op jit(solution)/shard_map/dot_general | solution.py:169
  (26 shorter events, 0.2 us)
Async XLA Ops:
  0.0 1.3 %copy-start = (s32[2]{0:T(128)S(1)}, s32[2]{0:T(128)}, u32[]{:S(2)}) copy-start(s32[2]{0:T(128)} %param.11) | copy-start | bytes 28
  0.0 2.4 %copy-start.5 = (s32[1,4096]{1,0:T(1,128)S(1)}, s32[1,4096]{1,0:T(1,128)}, u32[]{:S(2)}) copy-start(s32[1,4096]{1,0:T(1,128)} %param.10) | copy-start | bytes 49156
  0.0 2.4 %copy-start.4 = (bf16[4096,64]{0,1:T(8,128)(2,1)S(1)}, bf16[4096,64]{0,1:T(8,128)(2,1)}, u32[]{:S(2)}) copy-start(bf16[4096,64]{0,1:T(8,128)(2,1)} %param.8) | copy-start | bytes 1572868
  1.9 15.2 %slice-start = ((s8[9437184]{0:T(1024)(128)(4,1)}), s8[1048576]{0:T(1024)(128)(4,1)S(1)}, s32[]{:S(2)}) async-start(s8[9437184]{0:T(1024)(128)(4,1)} %bitcast.51), calls=%async_computation | async-start | bytes 2097152
  2.4 14.8 %slice-start.1 = ((s8[9437184]{0:T(1024)(128)(4,1)}), s8[4194304]{0:T(1024)(128)(4,1)S(1)}, s32[]{:S(2)}) async-start(s8[9437184]{0:T(1024)(128)(4,1)} %bitcast.51), calls=%async_computation.1 | async-start | bytes 8388608
  2.4 14.7 %slice-start.2 = ((s8[9437184]{0:T(1024)(128)(4,1)}), s8[4194304]{0:T(1024)(128)(4,1)S(1)}, s32[]{:S(2)}) async-start(s8[9437184]{0:T(1024)(128)(4,1)} %bitcast.51), calls=%async_computation.2 | async-start | bytes 8388608
  15.0 3.8 %copy-start.1 = (bf16[4096,192]{1,0:T(8,128)(2,1)}, bf16[4096,192]{1,0:T(8,128)(2,1)S(1)}, u32[]{:S(2)}) copy-start(bf16[4096,192]{1,0:T(8,128)(2,1)S(1)} %fusion.8.rows_ref.leaf_ref) | copy-start | bytes 4718596
  17.2 2.3 %copy-start.2 = (bf16[4096,64]{1,0:T(8,128)(2,1)}, bf16[4096,64]{1,0:T(8,128)(2,1)S(1)}, u32[]{:S(2)}) copy-start(bf16[4096,64]{1,0:T(8,128)(2,1)S(1)} %slice_select_fusion.vec_ref) | copy-start | bytes 1572868
  18.8 0.7 copy-start.3
  18.8 7.8 %collective-permute-start = (f32[8,64,128]{2,1,0:T(8,128)S(1)}, f32[8,64,128]{2,1,0:T(8,128)}, u32[]{:S(2)}, u32[]{:S(2)}) collective-permute-start(f32[8,64,128]{2,1,0:T(8,128)S(1)} %fusion.21), channel_id=1, source_target_pairs={{0,1},{1,0},{2,3},{3,2},{4,5},{5,4},{6,7},{7,6},{8,9},{9,8},{10,11... | collective-permute-start | bytes 786440 | tf_op jit(solution)/shard_map/ppermute | solution.py:21
  27.6 8.9 %collective-permute-start.1 = (f32[7,64,128]{2,1,0:T(8,128)S(1)}, f32[7,64,128]{2,1,0:T(8,128)S(1)}, u32[]{:S(2)}, u32[]{:S(2)}) collective-permute-start(f32[7,64,128]{2,1,0:T(8,128)S(1)} %slice_add_fusion), channel_id=1, source_target_pairs={{0,2},{1,3},{2,0},{3,1},{4,6},{5,7},{6,4},{7,5},{8,10},{9,11},{10,... | collective-permute-start | bytes 688136 | tf_op jit(solution)/shard_map/ppermute | solution.py:21
  36.5 12.3 %collective-permute-start.2 = (f32[6,64,128]{2,1,0:T(8,128)S(1)}, f32[6,64,128]{2,1,0:T(8,128)S(1)}, u32[]{:S(2)}, u32[]{:S(2)}) collective-permute-start(f32[6,64,128]{2,1,0:T(8,128)S(1)} %slice_add_fusion.1), channel_id=1, source_target_pairs={{0,4},{1,5},{2,6},{3,7},{4,0},{5,1},{6,2},{7,3},{8,12},{9,13},{10,... | collective-permute-start | bytes 589832 | tf_op jit(solution)/shard_map/ppermute | solution.py:21
  48.8 13.2 %collective-permute-start.3 = (f32[5,64,128]{2,1,0:T(8,128)S(1)}, f32[5,64,128]{2,1,0:T(8,128)S(1)}, u32[]{:S(2)}, u32[]{:S(2)}) collective-permute-start(f32[5,64,128]{2,1,0:T(8,128)S(1)} %slice_add_fusion.2), channel_id=1, source_target_pairs={{0,8},{1,9},{2,10},{3,11},{4,12},{5,13},{6,14},{7,15},{8,0},{9,1},... | collective-permute-start | bytes 491528 | tf_op jit(solution)/shard_map/ppermute | solution.py:21
  62.0 6.3 %collective-permute-start.4 = (f32[4,64,128]{2,1,0:T(8,128)S(1)}, f32[4,64,128]{2,1,0:T(8,128)S(1)}, u32[]{:S(2)}, u32[]{:S(2)}) collective-permute-start(f32[4,64,128]{2,1,0:T(8,128)S(1)} %slice_add_fusion.3), channel_id=1, source_target_pairs={{0,16},{1,17},{2,18},{3,19},{4,20},{5,21},{6,22},{7,23},{8,24},{9,... | collective-permute-start | bytes 393224 | tf_op jit(solution)/shard_map/ppermute | solution.py:21
  68.3 6.6 %collective-permute-start.5 = (f32[3,64,128]{2,1,0:T(8,128)S(1)}, f32[3,64,128]{2,1,0:T(8,128)S(1)}, u32[]{:S(2)}, u32[]{:S(2)}) collective-permute-start(f32[3,64,128]{2,1,0:T(8,128)S(1)} %slice_add_fusion.4), channel_id=1, source_target_pairs={{0,32},{1,33},{2,34},{3,35},{4,36},{5,37},{6,38},{7,39},{8,40},{9,... | collective-permute-start | bytes 294920 | tf_op jit(solution)/shard_map/ppermute | solution.py:21
  75.0 7.4 %collective-permute-start.6 = (f32[2,64,128]{2,1,0:T(8,128)S(1)}, f32[2,64,128]{2,1,0:T(8,128)S(1)}, u32[]{:S(2)}, u32[]{:S(2)}) collective-permute-start(f32[2,64,128]{2,1,0:T(8,128)S(1)} %slice_add_fusion.5), channel_id=1, source_target_pairs={{0,64},{1,65},{2,66},{3,67},{4,68},{5,69},{6,70},{7,71},{8,72},{9,... | collective-permute-start | bytes 196616 | tf_op jit(solution)/shard_map/ppermute | solution.py:21
  82.3 8.4 %collective-permute-start.7 = (f32[1,64,128]{2,1,0:T(8,128)S(1)}, f32[1,64,128]{2,1,0:T(8,128)S(1)}, u32[]{:S(2)}, u32[]{:S(2)}) collective-permute-start(f32[1,64,128]{2,1,0:T(8,128)S(1)} %get-tuple-element.16), channel_id=1, source_target_pairs={{0,128},{1,129},{2,130},{3,131},{4,132},{5,133},{6,134},{7,135},{8... | collective-permute-start | bytes 98312 | tf_op jit(solution)/shard_map/ppermute | solution.py:21
  85.9 4.9 %copy-start.6 = (f32[8]{0:T(128)S(1)}, f32[8]{0:T(128)}, u32[]{:S(2)}) copy-start(f32[8]{0:T(128)} %constant.36.clone) | copy-start | bytes 100

commit v8 on v7

--- a/solution.py
+++ b/solution.py
@@ -128,7 +128,7 @@
         done = upto
         finished.append(received[0])
         stack = stack[1:] + received[1:]
-        gate = received[0, :8]
+        gate = received
     for row_start in chunk_starts[done:]:
         accumulated = dense_rows(accumulated, table, masked, gate, row_start, block_rows)
     sibling_totals = jnp.stack(finished)

time: 112 us -> 134 us (1.20)
  waiting for transfers between devices: 5.14 us -> 33.3 us
  local copies, waits for them, and re-layouts: 8.26 us -> 2.4 us
  starting transfers between devices: 18.6 us -> 20 us
    ppermute x8, waiting for transfers between devices: 5.14 us -> 33.3 us  [swapped(): lax.ppermute(x, axis, [(i, i ^ 1 << bit) for i in range(lax.axis_size(axi...]
    squeeze x7 -> x0, local copies, waits for them, and re-layouts: 4.82 us -> none  [body(): gate = received[0, :8]]
  transfers between devices with their start and end apart: 8 -> 8, of which waited for: 2 -> 7; matrix products, arithmetic and copies ran while one was open for 7% -> 2% of each run, Pallas kernels for 35% -> 29%
where the time goes in v8:
time: 134 us
  Pallas kernels  38.9 us (29%)
  matrix products  35.3 us (26%)
  waiting for transfers between devices  33.3 us (25%)
  starting transfers between devices  20 us (15%)
  other arithmetic  3.59 us (3%)
  local copies, waits for them, and re-layouts  2.4 us (2%)
    pallas_call x8, Pallas kernels, dense_rows(): pl.pallas_call(dense_kernel, grid=(rows // BLOCK,), in_specs=in_specs, ou...  38.9 us
    ppermute x8, waiting for transfers between devices, swapped(): lax.ppermute(x, axis, [(i, i ^ 1 << bit) for i in range(lax.axis_size(axi...  33.3 us
    ppermute x8, starting transfers between devices, swapped(): lax.ppermute(x, axis, [(i, i ^ 1 << bit) for i in range(lax.axis_size(axi...  20 us
    dot_general x1, matrix products, body(): jnp.dot(inverse, result, preferred_element_type=jnp.float32)  14.6 us
    dot_general x1, matrix products, body(): lax.dot_general(onehot, jnp.concatenate([lhs_features, rhs_features.T, ve...  12.5 us
    dot_general x1, matrix products, body(): jnp.einsum('lrk,lpk->rp', level_bases[local_levels:], weights, preferred_...  5.63 us
  transfers between devices with their start and end apart: 8, of which 7 were waited for; matrix products, arithmetic and copies ran while one was open for 2% of the time, Pallas kernels for 29%

profile of v8, /device:TPU:6, one launch (start us, length us, event | category | flops | bytes accessed | tf_op | source)
XLA Modules:
  0.0 133.7 jit_solution(6752255275830139610)
XLA Ops:
  0.0 0.0 copy-start
  0.0 1.1 broadcast_multiply_fusion
  1.1 0.2 fusion.30
  1.3 0.0 copy-done
  1.3 0.1 broadcast_bitcast_fusion
  1.5 0.5 concatenate.12
  1.9 0.0 slice-start
  1.9 0.5 concatenate.11
  2.4 0.0 copy-done.14
  2.4 0.0 copy-done.13
  2.4 0.0 slice-start.1
  2.4 0.0 slice-start.2
  2.4 12.5 %fusion.8.rows_ref.leaf_ref = bf16[4096,192]{1,0:T(8,128)(2,1)S(1)} fusion(s32[4096]{0:T(1024)S(1)} %bitcast.44, bf16[4096,64]{0,1:T(8,128)(2,1)S(1)} %copy-done.13, bf16[4096,64]{0,1:T(8,128)(2,1)S(1)} %bitcast.41, bf16[4096,64]{0,1:T(8,128)(2,1)S(1)} %bitcast.42), kind=kOutput, calls=%fused_computation.10 | convolution fusion | flops 6464733184 | bytes 3162112 | tf_op jit(solution)/shard_map/dot_general | solution.py:101
  15.0 0.0 copy-start.1
  15.0 2.2 %slice_select_fusion.vec_ref = bf16[4096,64]{1,0:T(8,128)(2,1)S(1)} fusion(bf16[4096,192]{1,0:T(8,128)(2,1)S(1)} %fusion.8.rows_ref.leaf_ref, pred[4096]{0:T(1024)(128)(4,1)S(1)} %fusion.31), kind=kLoop, calls=%fused_computation.24 | loop fusion | flops 262144 | bytes 1052672 | tf_op jit(solution)/shard_map/jit(_where)/select_n | solution.py:111
  17.2 0.0 slice-done
  17.2 0.0 slice-done.1
  17.2 0.0 slice-done.2
  17.2 0.0 copy-start.2
  17.2 1.6 %fusion.21 = f32[8,64,128]{2,1,0:T(8,128)S(1)} fusion(bf16[9,4096,128]{2,1,0:T(8,128)(2,1)S(1)} %bitcast.38, bf16[4096,64]{1,0:T(8,128)(2,1)S(1)} %slice_select_fusion.vec_ref), kind=kOutput, calls=%fused_computation.23 | convolution fusion | flops 536870912 | bytes 9699328 | tf_op jit(solution)/shard_map/rp,lrk->lpk/dot_general | solution.py:113
  18.8 0.0 copy-done.1
  18.8 0.0 copy-start.12
  18.8 0.1 collective-permute-start
  18.9 0.1 slice.133
  19.0 0.0 copy-done.2
  19.0 0.5 fusion.45
  19.5 0.0 copy-done.12
  19.6 0.9 collective-permute-done.gate_ref
  20.5 2.0 %collective-permute-start.1 = (f32[7,64,128]{2,1,0:T(8,128)S(1)}, f32[7,64,128]{2,1,0:T(8,128)S(1)}, u32[]{:S(2)}, u32[]{:S(2)}) collective-permute-start(f32[7,64,128]{2,1,0:T(8,128)S(1)} %slice_add_fusion), channel_id=1, source_target_pairs={{0,2},{1,3},{2,0},{3,1},{4,6},{5,7},{6,4},{7,5},{8,10},{9,11},{10,... | collective-permute-start | bytes 688136 | tf_op jit(solution)/shard_map/ppermute | solution.py:21
  22.5 0.5 convolution_bitcast_fusion
  23.0 5.4 %collective-permute-done.1.gate_ref = f32[7,64,128]{2,1,0:T(8,128)S(1)} collective-permute-done((f32[7,64,128]{2,1,0:T(8,128)S(1)}, f32[7,64,128]{2,1,0:T(8,128)S(1)}, u32[]{:S(2)}, u32[]{:S(2)}) %collective-permute-start.1) | collective-permute-done | bytes 229408 | tf_op jit(solution)/shard_map/ppermute | solution.py:21
  28.4 3.4 %collective-permute-start.2 = (f32[6,64,128]{2,1,0:T(8,128)S(1)}, f32[6,64,128]{2,1,0:T(8,128)S(1)}, u32[]{:S(2)}, u32[]{:S(2)}) collective-permute-start(f32[6,64,128]{2,1,0:T(8,128)S(1)} %slice_add_fusion.1), channel_id=1, source_target_pairs={{0,4},{1,5},{2,6},{3,7},{4,0},{5,1},{6,2},{7,3},{8,12},{9,13},{10,... | collective-permute-start | bytes 589832 | tf_op jit(solution)/shard_map/ppermute | solution.py:21
  31.8 8.7 %collective-permute-done.2.gate_ref = f32[6,64,128]{2,1,0:T(8,128)S(1)} collective-permute-done((f32[6,64,128]{2,1,0:T(8,128)S(1)}, f32[6,64,128]{2,1,0:T(8,128)S(1)}, u32[]{:S(2)}, u32[]{:S(2)}) %collective-permute-start.2) | collective-permute-done | bytes 196640 | tf_op jit(solution)/shard_map/ppermute | solution.py:21
  40.5 6.5 %collective-permute-start.3 = (f32[5,64,128]{2,1,0:T(8,128)S(1)}, f32[5,64,128]{2,1,0:T(8,128)S(1)}, u32[]{:S(2)}, u32[]{:S(2)}) collective-permute-start(f32[5,64,128]{2,1,0:T(8,128)S(1)} %slice_add_fusion.2), channel_id=1, source_target_pairs={{0,8},{1,9},{2,10},{3,11},{4,12},{5,13},{6,14},{7,15},{8,0},{9,1},... | collective-permute-start | bytes 491528 | tf_op jit(solution)/shard_map/ppermute | solution.py:21
  47.0 6.9 %collective-permute-done.3.gate_ref = f32[5,64,128]{2,1,0:T(8,128)S(1)} collective-permute-done((f32[5,64,128]{2,1,0:T(8,128)S(1)}, f32[5,64,128]{2,1,0:T(8,128)S(1)}, u32[]{:S(2)}, u32[]{:S(2)}) %collective-permute-start.3) | collective-permute-done | bytes 163872 | tf_op jit(solution)/shard_map/ppermute | solution.py:21
  53.9 0.0 copy-done.3
  54.0 0.9 collective-permute-start.4
  54.9 0.0 copy-done.4
  54.9 4.1 %collective-permute-done.4.gate_ref = f32[4,64,128]{2,1,0:T(8,128)S(1)} collective-permute-done((f32[4,64,128]{2,1,0:T(8,128)S(1)}, f32[4,64,128]{2,1,0:T(8,128)S(1)}, u32[]{:S(2)}, u32[]{:S(2)}) %collective-permute-start.4) | collective-permute-done | bytes 131104 | tf_op jit(solution)/shard_map/ppermute | solution.py:21
  59.0 1.5 %collective-permute-start.5 = (f32[3,64,128]{2,1,0:T(8,128)S(1)}, f32[3,64,128]{2,1,0:T(8,128)S(1)}, u32[]{:S(2)}, u32[]{:S(2)}) collective-permute-start(f32[3,64,128]{2,1,0:T(8,128)S(1)} %slice_add_fusion.4), channel_id=1, source_target_pairs={{0,32},{1,33},{2,34},{3,35},{4,36},{5,37},{6,38},{7,39},{8,40},{9,... | collective-permute-start | bytes 294920 | tf_op jit(solution)/shard_map/ppermute | solution.py:21
  60.5 4.7 %collective-permute-done.5.gate_ref = f32[3,64,128]{2,1,0:T(8,128)S(1)} collective-permute-done((f32[3,64,128]{2,1,0:T(8,128)S(1)}, f32[3,64,128]{2,1,0:T(8,128)S(1)}, u32[]{:S(2)}, u32[]{:S(2)}) %collective-permute-start.5) | collective-permute-done | bytes 98336 | tf_op jit(solution)/shard_map/ppermute | solution.py:21
  65.2 1.9 %collective-permute-start.6 = (f32[2,64,128]{2,1,0:T(8,128)S(1)}, f32[2,64,128]{2,1,0:T(8,128)S(1)}, u32[]{:S(2)}, u32[]{:S(2)}) collective-permute-start(f32[2,64,128]{2,1,0:T(8,128)S(1)} %slice_add_fusion.5), channel_id=1, source_target_pairs={{0,64},{1,65},{2,66},{3,67},{4,68},{5,69},{6,70},{7,71},{8,72},{9,... | collective-permute-start | bytes 196616 | tf_op jit(solution)/shard_map/ppermute | solution.py:21
  67.1 2.5 %collective-permute-done.6.gate_ref = f32[2,64,128]{2,1,0:T(8,128)S(1)} collective-permute-done((f32[2,64,128]{2,1,0:T(8,128)S(1)}, f32[2,64,128]{2,1,0:T(8,128)S(1)}, u32[]{:S(2)}, u32[]{:S(2)}) %collective-permute-start.6) | collective-permute-done | bytes 65568 | tf_op jit(solution)/shard_map/ppermute | solution.py:21
  69.6 0.0 copy-start.10
  69.6 3.8 %collective-permute-start.7 = (f32[1,64,128]{2,1,0:T(8,128)S(1)}, f32[1,64,128]{2,1,0:T(8,128)S(1)}, u32[]{:S(2)}, u32[]{:S(2)}) collective-permute-start(f32[1,64,128]{2,1,0:T(8,128)S(1)} %get-tuple-element.16), channel_id=1, source_target_pairs={{0,128},{1,129},{2,130},{3,131},{4,132},{5,133},{6,134},{7,135},{8... | collective-permute-start | bytes 98312 | tf_op jit(solution)/shard_map/ppermute | solution.py:21
  73.4 0.6 broadcast_in_dim.44.gate_ref
  74.0 0.0 copy-done.5
  74.0 0.0 copy-done.6
  74.0 0.0 copy-done.10
  74.0 4.9 %shard_map.82.refs_0_ = f32[4096,64]{1,0:T(8,128)} custom-call(bf16[4096,192]{1,0:T(8,128)(2,1)} %copy-done.1, bf16[4096,192]{1,0:T(8,128)(2,1)} %copy-done.1, bf16[4096,64]{1,0:T(8,128)(2,1)} %copy-done.2, f32[8,128]{1,0:T(8,128)} %broadcast_in_dim.44.gate_ref), custom_call_target="tpu_custom_call" | custom-call | tf_op jit(solution)/shard_map/pallas_call | solution.py:80
  78.8 0.0 copy-done.7
  78.8 0.0 copy-done.8
  78.9 0.6 copy.17
  79.5 4.9 %shard_map.83.refs_0_ = f32[4096,64]{1,0:T(8,128)} custom-call(bf16[4096,192]{1,0:T(8,128)(2,1)} %copy-done.1, bf16[4096,192]{1,0:T(8,128)(2,1)} %copy-done.1, bf16[4096,64]{1,0:T(8,128)(2,1)} %copy-done.2, f32[8,64,128]{2,1,0:T(8,128)} %copy-done.3, f32[4096,64]{1,0:T(8,128)} %shard_map.82.refs_0_), custom_call_target="tpu_custom_call", output_to_operand_aliasing={{}: (4, {})} | custom-call | tf_op jit(solution)/shard_map/pallas_call | solution.py:80
  84.3 4.8 %shard_map.84.refs_0_ = f32[4096,64]{1,0:T(8,128)} custom-call(bf16[4096,192]{1,0:T(8,128)(2,1)} %copy-done.1, bf16[4096,192]{1,0:T(8,128)(2,1)} %copy-done.1, bf16[4096,64]{1,0:T(8,128)(2,1)} %copy-done.2, f32[7,64,128]{2,1,0:T(8,128)} %copy-done.4, f32[4096,64]{1,0:T(8,128)} %shard_map.83.refs_0_), custom_call_target="tpu_custom_call", output_to_operand_aliasing={{}: (4, {})} | custom-call | tf_op jit(solution)/shard_map/pallas_call | solution.py:80
  89.2 4.8 %shard_map.85.refs_0_ = f32[4096,64]{1,0:T(8,128)} custom-call(bf16[4096,192]{1,0:T(8,128)(2,1)} %copy-done.1, bf16[4096,192]{1,0:T(8,128)(2,1)} %copy-done.1, bf16[4096,64]{1,0:T(8,128)(2,1)} %copy-done.2, f32[6,64,128]{2,1,0:T(8,128)} %copy-done.5, f32[4096,64]{1,0:T(8,128)} %shard_map.84.refs_0_), custom_call_target="tpu_custom_call", output_to_operand_aliasing={{}: (4, {})} | custom-call | tf_op jit(solution)/shard_map/pallas_call | solution.py:80
  94.0 4.9 %shard_map.86.refs_0_ = f32[4096,64]{1,0:T(8,128)} custom-call(bf16[4096,192]{1,0:T(8,128)(2,1)} %copy-done.1, bf16[4096,192]{1,0:T(8,128)(2,1)} %copy-done.1, bf16[4096,64]{1,0:T(8,128)(2,1)} %copy-done.2, f32[5,64,128]{2,1,0:T(8,128)} %copy-done.6, f32[4096,64]{1,0:T(8,128)} %shard_map.85.refs_0_), custom_call_target="tpu_custom_call", output_to_operand_aliasing={{}: (4, {})} | custom-call | tf_op jit(solution)/shard_map/pallas_call | solution.py:80
  98.9 4.8 %shard_map.87.refs_0_ = f32[4096,64]{1,0:T(8,128)} custom-call(bf16[4096,192]{1,0:T(8,128)(2,1)} %copy-done.1, bf16[4096,192]{1,0:T(8,128)(2,1)} %copy-done.1, bf16[4096,64]{1,0:T(8,128)(2,1)} %copy-done.2, f32[4,64,128]{2,1,0:T(8,128)} %copy-done.7, f32[4096,64]{1,0:T(8,128)} %shard_map.86.refs_0_), custom_call_target="tpu_custom_call", output_to_operand_aliasing={{}: (4, {})} | custom-call | tf_op jit(solution)/shard_map/pallas_call | solution.py:80
  103.7 4.8 %shard_map.88.refs_0_ = f32[4096,64]{1,0:T(8,128)} custom-call(bf16[4096,192]{1,0:T(8,128)(2,1)} %copy-done.1, bf16[4096,192]{1,0:T(8,128)(2,1)} %copy-done.1, bf16[4096,64]{1,0:T(8,128)(2,1)} %copy-done.2, f32[3,64,128]{2,1,0:T(8,128)} %copy-done.8, f32[4096,64]{1,0:T(8,128)} %shard_map.87.refs_0_), custom_call_target="tpu_custom_call", output_to_operand_aliasing={{}: (4, {})} | custom-call | tf_op jit(solution)/shard_map/pallas_call | solution.py:80
  108.6 4.9 %shard_map.89 = f32[4096,64]{1,0:T(8,128)} custom-call(bf16[4096,192]{1,0:T(8,128)(2,1)} %copy-done.1, bf16[4096,192]{1,0:T(8,128)(2,1)} %copy-done.1, bf16[4096,64]{1,0:T(8,128)(2,1)} %copy-done.2, f32[2,64,128]{2,1,0:T(8,128)} %copy-done.9, f32[4096,64]{1,0:T(8,128)} %shard_map.88.refs_0_), custom_call_target="tpu_custom_call", output_to_operand_aliasing={{}: (4, {})} | custom-call | tf_op jit(solution)/shard_map/pallas_call | solution.py:80
  113.5 0.0 collective-permute-done.7
  113.5 0.0 copy-start.15
  113.5 5.6 %fusion.15 = bf16[4096,64]{1,0:T(8,128)(2,1)S(1)} fusion(f32[4096,64]{1,0:T(8,128)} %shard_map.89, f32[2,2048,64]{2,1,0:T(8,128)S(1)} %copy.17, pred[4096]{0:T(1024)(128)(4,1)S(1)} %fusion.31, bf16[9,4096,128]{2,1,0:T(8,128)(2,1)} %param.12, f32[8,64,128]{2,1,0:T(8,128)S(1)} %constant_dynamic-update-slice_fusion, f32[8,128]{1,0:T(8,128)S(1)} %slice_multiply_fusion.8, ...), kind=kOutput, calls=%fused_computation.17 | convolution fusion | flops 538116096 | bytes 12328992 | tf_op jit(solution)/shard_map/lrk,lpk->rp/dot_general | solution.py:162
  119.2 14.6 %fusion.12 = bf16[4096,64]{0,1:T(8,128)(2,1)} fusion(bf16[4096,64]{1,0:T(8,128)(2,1)S(1)} %fusion.15, s32[4096]{0:T(1024)S(1)} %bitcast.45), kind=kOutput, calls=%fused_computation.12 | convolution fusion | flops 2164523008 | bytes 1064960 | tf_op jit(solution)/shard_map/dot_general | solution.py:169
  (39 shorter events, 0.3 us)
Async XLA Ops:
  0.0 1.3 copy-start
  0.0 2.4 %copy-start.14 = (s32[1,4096]{1,0:T(1,128)S(1)}, s32[1,4096]{1,0:T(1,128)}, u32[]{:S(2)}) copy-start(s32[1,4096]{1,0:T(1,128)} %param.10) | copy-start | bytes 49156
  0.0 2.4 %copy-start.13 = (bf16[4096,64]{0,1:T(8,128)(2,1)S(1)}, bf16[4096,64]{0,1:T(8,128)(2,1)}, u32[]{:S(2)}) copy-start(bf16[4096,64]{0,1:T(8,128)(2,1)} %param.8) | copy-start | bytes 1572868
  1.9 15.2 %slice-start = ((s8[9437184]{0:T(1024)(128)(4,1)}), s8[1048576]{0:T(1024)(128)(4,1)S(1)}, s32[]{:S(2)}) async-start(s8[9437184]{0:T(1024)(128)(4,1)} %bitcast.37), calls=%async_computation | async-start | bytes 2097152
  2.4 14.8 %slice-start.1 = ((s8[9437184]{0:T(1024)(128)(4,1)}), s8[4194304]{0:T(1024)(128)(4,1)S(1)}, s32[]{:S(2)}) async-start(s8[9437184]{0:T(1024)(128)(4,1)} %bitcast.37), calls=%async_computation.1 | async-start | bytes 8388608
  2.4 14.7 %slice-start.2 = ((s8[9437184]{0:T(1024)(128)(4,1)}), s8[4194304]{0:T(1024)(128)(4,1)S(1)}, s32[]{:S(2)}) async-start(s8[9437184]{0:T(1024)(128)(4,1)} %bitcast.37), calls=%async_computation.2 | async-start | bytes 8388608
  15.0 3.8 %copy-start.1 = (bf16[4096,192]{1,0:T(8,128)(2,1)}, bf16[4096,192]{1,0:T(8,128)(2,1)S(1)}, u32[]{:S(2)}) copy-start(bf16[4096,192]{1,0:T(8,128)(2,1)S(1)} %fusion.8.rows_ref.leaf_ref) | copy-start | bytes 4718596
  17.2 1.8 %copy-start.2 = (bf16[4096,64]{1,0:T(8,128)(2,1)}, bf16[4096,64]{1,0:T(8,128)(2,1)S(1)}, u32[]{:S(2)}) copy-start(bf16[4096,64]{1,0:T(8,128)(2,1)S(1)} %slice_select_fusion.vec_ref) | copy-start | bytes 1572868
  18.8 0.7 copy-start.12
  18.8 1.6 %collective-permute-start = (f32[8,64,128]{2,1,0:T(8,128)S(1)}, f32[8,64,128]{2,1,0:T(8,128)S(1)}, u32[]{:S(2)}, u32[]{:S(2)}) collective-permute-start(f32[8,64,128]{2,1,0:T(8,128)S(1)} %fusion.21), channel_id=1, source_target_pairs={{0,1},{1,0},{2,3},{3,2},{4,5},{5,4},{6,7},{7,6},{8,9},{9,8},{10,11... | collective-permute-start | bytes 786440 | tf_op jit(solution)/shard_map/ppermute | solution.py:21
  20.5 33.5 %copy-start.3 = (f32[8,64,128]{2,1,0:T(8,128)}, f32[8,64,128]{2,1,0:T(8,128)S(1)}, u32[]{:S(2)}) copy-start(f32[8,64,128]{2,1,0:T(8,128)S(1)} %collective-permute-done.gate_ref) | copy-start | bytes 786436
  20.5 7.9 %collective-permute-start.1 = (f32[7,64,128]{2,1,0:T(8,128)S(1)}, f32[7,64,128]{2,1,0:T(8,128)S(1)}, u32[]{:S(2)}, u32[]{:S(2)}) collective-permute-start(f32[7,64,128]{2,1,0:T(8,128)S(1)} %slice_add_fusion), channel_id=1, source_target_pairs={{0,2},{1,3},{2,0},{3,1},{4,6},{5,7},{6,4},{7,5},{8,10},{9,11},{10,... | collective-permute-start | bytes 688136 | tf_op jit(solution)/shard_map/ppermute | solution.py:21
  28.4 26.5 %copy-start.4 = (f32[7,64,128]{2,1,0:T(8,128)}, f32[7,64,128]{2,1,0:T(8,128)S(1)}, u32[]{:S(2)}) copy-start(f32[7,64,128]{2,1,0:T(8,128)S(1)} %collective-permute-done.1.gate_ref) | copy-start | bytes 688132
  28.4 12.1 %collective-permute-start.2 = (f32[6,64,128]{2,1,0:T(8,128)S(1)}, f32[6,64,128]{2,1,0:T(8,128)S(1)}, u32[]{:S(2)}, u32[]{:S(2)}) collective-permute-start(f32[6,64,128]{2,1,0:T(8,128)S(1)} %slice_add_fusion.1), channel_id=1, source_target_pairs={{0,4},{1,5},{2,6},{3,7},{4,0},{5,1},{6,2},{7,3},{8,12},{9,13},{10,... | collective-permute-start | bytes 589832 | tf_op jit(solution)/shard_map/ppermute | solution.py:21
  40.5 33.5 %copy-start.5 = (f32[6,64,128]{2,1,0:T(8,128)}, f32[6,64,128]{2,1,0:T(8,128)S(1)}, u32[]{:S(2)}) copy-start(f32[6,64,128]{2,1,0:T(8,128)S(1)} %collective-permute-done.2.gate_ref) | copy-start | bytes 589828
  40.5 13.4 %collective-permute-start.3 = (f32[5,64,128]{2,1,0:T(8,128)S(1)}, f32[5,64,128]{2,1,0:T(8,128)S(1)}, u32[]{:S(2)}, u32[]{:S(2)}) collective-permute-start(f32[5,64,128]{2,1,0:T(8,128)S(1)} %slice_add_fusion.2), channel_id=1, source_target_pairs={{0,8},{1,9},{2,10},{3,11},{4,12},{5,13},{6,14},{7,15},{8,0},{9,1},... | collective-permute-start | bytes 491528 | tf_op jit(solution)/shard_map/ppermute | solution.py:21
  53.9 20.1 %copy-start.6 = (f32[5,64,128]{2,1,0:T(8,128)}, f32[5,64,128]{2,1,0:T(8,128)S(1)}, u32[]{:S(2)}) copy-start(f32[5,64,128]{2,1,0:T(8,128)S(1)} %collective-permute-done.3.gate_ref) | copy-start | bytes 491524
  54.0 5.1 %collective-permute-start.4 = (f32[4,64,128]{2,1,0:T(8,128)S(1)}, f32[4,64,128]{2,1,0:T(8,128)S(1)}, u32[]{:S(2)}, u32[]{:S(2)}) collective-permute-start(f32[4,64,128]{2,1,0:T(8,128)S(1)} %slice_add_fusion.3), channel_id=1, source_target_pairs={{0,16},{1,17},{2,18},{3,19},{4,20},{5,21},{6,22},{7,23},{8,24},{9,... | collective-permute-start | bytes 393224 | tf_op jit(solution)/shard_map/ppermute | solution.py:21
  59.0 19.8 %copy-start.7 = (f32[4,64,128]{2,1,0:T(8,128)}, f32[4,64,128]{2,1,0:T(8,128)S(1)}, u32[]{:S(2)}) copy-start(f32[4,64,128]{2,1,0:T(8,128)S(1)} %collective-permute-done.4.gate_ref) | copy-start | bytes 393220
  59.0 6.2 %collective-permute-start.5 = (f32[3,64,128]{2,1,0:T(8,128)S(1)}, f32[3,64,128]{2,1,0:T(8,128)S(1)}, u32[]{:S(2)}, u32[]{:S(2)}) collective-permute-start(f32[3,64,128]{2,1,0:T(8,128)S(1)} %slice_add_fusion.4), channel_id=1, source_target_pairs={{0,32},{1,33},{2,34},{3,35},{4,36},{5,37},{6,38},{7,39},{8,40},{9,... | collective-permute-start | bytes 294920 | tf_op jit(solution)/shard_map/ppermute | solution.py:21
  65.2 13.6 %copy-start.8 = (f32[3,64,128]{2,1,0:T(8,128)}, f32[3,64,128]{2,1,0:T(8,128)S(1)}, u32[]{:S(2)}) copy-start(f32[3,64,128]{2,1,0:T(8,128)S(1)} %collective-permute-done.5.gate_ref) | copy-start | bytes 294916
  65.2 4.4 %collective-permute-start.6 = (f32[2,64,128]{2,1,0:T(8,128)S(1)}, f32[2,64,128]{2,1,0:T(8,128)S(1)}, u32[]{:S(2)}, u32[]{:S(2)}) collective-permute-start(f32[2,64,128]{2,1,0:T(8,128)S(1)} %slice_add_fusion.5), channel_id=1, source_target_pairs={{0,64},{1,65},{2,66},{3,67},{4,68},{5,69},{6,70},{7,71},{8,72},{9,... | collective-permute-start | bytes 196616 | tf_op jit(solution)/shard_map/ppermute | solution.py:21
  69.6 9.3 %copy-start.9 = (f32[2,64,128]{2,1,0:T(8,128)}, f32[2,64,128]{2,1,0:T(8,128)S(1)}, u32[]{:S(2)}) copy-start(f32[2,64,128]{2,1,0:T(8,128)S(1)} %collective-permute-done.6.gate_ref) | copy-start | bytes 196612
  69.6 4.4 %copy-start.10 = (f32[8,64,128]{2,1,0:T(8,128)}, f32[8,64,128]{2,1,0:T(8,128)S(1)}, u32[]{:S(2)}) copy-start(f32[8,64,128]{2,1,0:T(8,128)S(1)} %get-tuple-element.17) | copy-start | bytes 786436
  69.6 43.8 %collective-permute-start.7 = (f32[1,64,128]{2,1,0:T(8,128)S(1)}, f32[1,64,128]{2,1,0:T(8,128)S(1)}, u32[]{:S(2)}, u32[]{:S(2)}) collective-permute-start(f32[1,64,128]{2,1,0:T(8,128)S(1)} %get-tuple-element.16), channel_id=1, source_target_pairs={{0,128},{1,129},{2,130},{3,131},{4,132},{5,133},{6,134},{7,135},{8... | collective-permute-start | bytes 98312 | tf_op jit(solution)/shard_map/ppermute | solution.py:21
  108.6 4.9 %copy-start.11 = (f32[8,64,128]{2,1,0:T(8,128)S(1)}, f32[8,64,128]{2,1,0:T(8,128)}, u32[]{:S(2)}) copy-start(f32[8,64,128]{2,1,0:T(8,128)} %copy-done.10) | copy-start | bytes 786436
  108.6 4.9 %copy-start.16 = (f32[8]{0:T(128)S(1)}, f32[8]{0:T(128)}, u32[]{:S(2)}) copy-start(f32[8]{0:T(128)} %constant.36.clone) | copy-start | bytes 100
  113.5 5.7 %copy-start.15 = (s32[1,4096]{1,0:T(1,128)S(1)}, s32[1,4096]{1,0:T(1,128)}, u32[]{:S(2)}) copy-start(s32[1,4096]{1,0:T(1,128)} %param.10) | copy-start | bytes 49156

commit v9 on v7

--- a/solution.py
+++ b/solution.py
@@ -94,9 +94,12 @@
     device_count = lax.axis_size("leaf")
     device_levels = device_count.bit_length() - 1
     slot_order = tree_order[0]
-    onehot = (slot_order[:, None] == jnp.arange(per_device, dtype=jnp.int32)[None, :]).astype(
-        jnp.bfloat16
-    )
+    slot_limit = jnp.repeat(live_counts, LEAF)
+    within = jnp.arange(per_device, dtype=jnp.int32) % LEAF
+    live_rows = (within < slot_limit)[:, None]
+    onehot = (
+        (slot_order[:, None] == jnp.arange(per_device, dtype=jnp.int32)[None, :]) & live_rows
+    ).astype(jnp.bfloat16)
     lhs_features, rhs_features = gram_features(contexts / length_scale[:, None])
     table = lax.dot_general(
         onehot,
@@ -104,11 +107,7 @@
         (((1,), (0,)), ((), ())),
         preferred_element_type=jnp.float32,
     ).astype(jnp.bfloat16)
-    ordered = table[:, 2 * FEATURES :]
-    slot_limit = jnp.repeat(live_counts, LEAF)
-    within = jnp.arange(per_device, dtype=jnp.int32) % LEAF
-    live_rows = (within < slot_limit)[:, None]
-    masked = jnp.where(live_rows, ordered, jnp.zeros_like(ordered))
+    masked = table[:, 2 * FEATURES :]
 
     partials = jnp.einsum(
         "rp,lrk->lpk", masked, level_bases[local_levels:], preferred_element_type=jnp.float32

time: 112 us -> 112 us (level)
  other arithmetic: 4.54 us -> 2.39 us
  matrix products: 35 us -> 36.5 us
    select_n x1 -> x0, other arithmetic: 2.15 us -> none  [body(): masked = jnp.where(live_rows, ordered, jnp.zeros_like(ordered))]
    dot_general x1, matrix products: 12.5 us -> 14 us  [body(): lax.dot_general(onehot, jnp.concatenate([lhs_features, rhs_features.T, ve...]
where the time goes in v9:
time: 112 us; the launch traced here: 110 us
  Pallas kernels  38.8 us (35%)
  matrix products  36.5 us (33%)
  starting transfers between devices  18.7 us (17%)
  local copies, waits for them, and re-layouts  8.41 us (8%)
  waiting for transfers between devices  4.97 us (4%)
  other arithmetic  2.39 us (2%)
    pallas_call x8, Pallas kernels, dense_rows(): pl.pallas_call(dense_kernel, grid=(rows // BLOCK,), in_specs=in_specs, ou...  38.8 us
    ppermute x8, starting transfers between devices, swapped(): lax.ppermute(x, axis, [(i, i ^ 1 << bit) for i in range(lax.axis_size(axi...  18.7 us
    dot_general x1, matrix products, body(): jnp.dot(inverse, result, preferred_element_type=jnp.float32)  14.6 us
    dot_general x1, matrix products, body(): lax.dot_general(onehot, jnp.concatenate([lhs_features, rhs_features.T, ve...  14 us
    dot_general x1, matrix products, body(): jnp.einsum('lrk,lpk->rp', level_bases[local_levels:], weights, preferred_...  5.37 us
    ppermute x8, waiting for transfers between devices, swapped(): lax.ppermute(x, axis, [(i, i ^ 1 << bit) for i in range(lax.axis_size(axi...  4.97 us
    squeeze x7, local copies, waits for them, and re-layouts, body(): gate = received[0, :8]  4.82 us
  transfers between devices with their start and end apart: 8, of which 2 were waited for; matrix products, arithmetic and copies ran while one was open for 7% of the time, Pallas kernels for 35%

profile of v9, /device:TPU:6, one launch (start us, length us, event | category | flops | bytes accessed | tf_op | source)
XLA Modules:
  0.0 110.1 jit_solution(10194703675828885037)
XLA Ops:
  0.0 0.0 copy-start
  0.0 1.1 broadcast_multiply_fusion
  1.1 0.2 fusion.35
  1.3 0.0 copy-done
  1.3 0.1 broadcast_bitcast_fusion
  1.5 0.5 concatenate.11
  1.9 0.0 slice-start
  1.9 0.5 concatenate.12
  2.4 0.0 copy-done.5
  2.4 0.0 copy-done.4
  2.4 0.0 slice-start.1
  2.4 0.0 slice-start.2
  2.4 14.0 %fusion.11.rows_ref.leaf_ref = bf16[4096,192]{1,0:T(8,128)(2,1)S(1)} fusion(s32[4096]{0:T(1024)S(1)} %bitcast.58, pred[4096]{0:T(1024)(128)(4,1)S(1)} %fusion.36, bf16[4096,64]{0,1:T(8,128)(2,1)S(1)} %copy-done.4, bf16[4096,64]{0,1:T(8,128)(2,1)S(1)} %bitcast.56, bf16[4096,64]{0,1:T(8,128)(2,1)S(1)} %bitcast.55), kind=kOutput, calls=%fused_computation.12 | convolution fusion | flops 6481510400 | bytes 3166208 | tf_op jit(solution)/shard_map/dot_general | solution.py:104
  16.5 0.0 slice-done
  16.5 0.0 slice-done.1
  16.5 0.0 slice-done.2
  16.5 0.0 copy-start.1
  16.5 1.6 %fusion.26 = f32[8,64,128]{2,1,0:T(8,128)S(1)} fusion(bf16[9,4096,128]{2,1,0:T(8,128)(2,1)S(1)} %bitcast.52, bf16[4096,192]{1,0:T(8,128)(2,1)S(1)} %fusion.11.rows_ref.leaf_ref), kind=kOutput, calls=%fused_computation.25 | convolution fusion | flops 536870912 | bytes 9699328 | tf_op jit(solution)/shard_map/rp,lrk->lpk/dot_general | solution.py:112
  18.1 0.0 copy-start.3
  18.1 0.1 collective-permute-start
  18.2 0.0 copy-done.1
  18.2 0.1 slice.181.vec_ref
  18.3 0.0 copy-start.2
  18.3 0.1 slice.161
  18.4 0.4 copy-done.3
  18.8 0.5 fusion.51
  19.3 0.5 convolution_bitcast_fusion
  19.8 0.0 copy-done.2
  19.8 0.6 broadcast_in_dim.34.gate_ref
  20.4 4.8 %shard_map.82.refs_0_ = f32[4096,64]{1,0:T(8,128)} custom-call(bf16[4096,192]{1,0:T(8,128)(2,1)} %copy-done.1, bf16[4096,192]{1,0:T(8,128)(2,1)} %copy-done.1, bf16[4096,64]{1,0:T(8,128)(2,1)} %copy-done.2, f32[8,128]{1,0:T(8,128)} %broadcast_in_dim.34.gate_ref), custom_call_target="tpu_custom_call" | custom-call | tf_op jit(solution)/shard_map/pallas_call | solution.py:80
  25.3 0.6 copy.17
  25.9 0.0 collective-permute-done
  25.9 1.0 slice_add_fusion
  26.9 2.0 %collective-permute-start.1 = (f32[7,64,128]{2,1,0:T(8,128)S(1)}, f32[7,64,128]{2,1,0:T(8,128)S(1)}, u32[]{:S(2)}, u32[]{:S(2)}) collective-permute-start(f32[7,64,128]{2,1,0:T(8,128)S(1)} %slice_add_fusion), channel_id=1, source_target_pairs={{0,2},{1,3},{2,0},{3,1},{4,6},{5,7},{6,4},{7,5},{8,10},{9,11},{10,... | collective-permute-start | bytes 688136 | tf_op jit(solution)/shard_map/ppermute | solution.py:21
  28.9 1.3 %slice_bitcast_fusion.gate_ref = f32[8,128]{1,0:T(8,128)} fusion(f32[8,64,128]{2,1,0:T(8,128)} %collective-permute-done), kind=kLoop, calls=%fused_computation.82 | loop fusion | bytes 8192 | tf_op jit(solution)/shard_map/squeeze | solution.py:130
  30.1 4.9 %shard_map.83.refs_0_ = f32[4096,64]{1,0:T(8,128)} custom-call(bf16[4096,192]{1,0:T(8,128)(2,1)} %copy-done.1, bf16[4096,192]{1,0:T(8,128)(2,1)} %copy-done.1, bf16[4096,64]{1,0:T(8,128)(2,1)} %copy-done.2, f32[8,128]{1,0:T(8,128)} %slice_bitcast_fusion.gate_ref, f32[4096,64]{1,0:T(8,128)} %shard_map.82.refs_0_), custom_call_target="tpu_custom_call", output_to_operand_aliasing={{}: (4, {})} | custom-call | tf_op jit(solution)/shard_map/pallas_call | solution.py:80
  35.0 0.8 slice_dynamic-update-slice_fusion.6
  35.8 0.0 collective-permute-done.1
  35.8 3.5 %collective-permute-start.2 = (f32[6,64,128]{2,1,0:T(8,128)S(1)}, f32[6,64,128]{2,1,0:T(8,128)S(1)}, u32[]{:S(2)}, u32[]{:S(2)}) collective-permute-start(f32[6,64,128]{2,1,0:T(8,128)S(1)} %slice_add_fusion.1), channel_id=1, source_target_pairs={{0,4},{1,5},{2,6},{3,7},{4,0},{5,1},{6,2},{7,3},{8,12},{9,13},{10,... | collective-permute-start | bytes 589832 | tf_op jit(solution)/shard_map/ppermute | solution.py:21
  39.3 0.6 slice_bitcast_fusion.1.gate_ref
  39.9 4.8 %shard_map.84.refs_0_ = f32[4096,64]{1,0:T(8,128)} custom-call(bf16[4096,192]{1,0:T(8,128)(2,1)} %copy-done.1, bf16[4096,192]{1,0:T(8,128)(2,1)} %copy-done.1, bf16[4096,64]{1,0:T(8,128)(2,1)} %copy-done.2, f32[8,128]{1,0:T(8,128)} %slice_bitcast_fusion.1.gate_ref, f32[4096,64]{1,0:T(8,128)} %shard_map.83.refs_0_), custom_call_target="tpu_custom_call", output_to_operand_aliasing={{}: (4, {})} | custom-call | tf_op jit(solution)/shard_map/pallas_call | solution.py:80
  44.8 3.4 %collective-permute-done.2 = f32[6,64,128]{2,1,0:T(8,128)S(1)} collective-permute-done((f32[6,64,128]{2,1,0:T(8,128)S(1)}, f32[6,64,128]{2,1,0:T(8,128)S(1)}, u32[]{:S(2)}, u32[]{:S(2)}) %collective-permute-start.2) | collective-permute-done | bytes 196640 | tf_op jit(solution)/shard_map/ppermute | solution.py:21
  48.2 6.1 %collective-permute-start.3 = (f32[5,64,128]{2,1,0:T(8,128)S(1)}, f32[5,64,128]{2,1,0:T(8,128)S(1)}, u32[]{:S(2)}, u32[]{:S(2)}) collective-permute-start(f32[5,64,128]{2,1,0:T(8,128)S(1)} %slice_add_fusion.2), channel_id=1, source_target_pairs={{0,8},{1,9},{2,10},{3,11},{4,12},{5,13},{6,14},{7,15},{8,0},{9,1},... | collective-permute-start | bytes 491528 | tf_op jit(solution)/shard_map/ppermute | solution.py:21
  54.2 0.6 slice_bitcast_fusion.2.gate_ref
  54.8 4.9 %shard_map.85.refs_0_ = f32[4096,64]{1,0:T(8,128)} custom-call(bf16[4096,192]{1,0:T(8,128)(2,1)} %copy-done.1, bf16[4096,192]{1,0:T(8,128)(2,1)} %copy-done.1, bf16[4096,64]{1,0:T(8,128)(2,1)} %copy-done.2, f32[8,128]{1,0:T(8,128)} %slice_bitcast_fusion.2.gate_ref, f32[4096,64]{1,0:T(8,128)} %shard_map.84.refs_0_), custom_call_target="tpu_custom_call", output_to_operand_aliasing={{}: (4, {})} | custom-call | tf_op jit(solution)/shard_map/pallas_call | solution.py:80
  59.7 1.6 %collective-permute-done.3 = f32[5,64,128]{2,1,0:T(8,128)S(1)} collective-permute-done((f32[5,64,128]{2,1,0:T(8,128)S(1)}, f32[5,64,128]{2,1,0:T(8,128)S(1)}, u32[]{:S(2)}, u32[]{:S(2)}) %collective-permute-start.3) | collective-permute-done | bytes 163872 | tf_op jit(solution)/shard_map/ppermute | solution.py:21
  61.3 0.9 collective-permute-start.4
  62.2 0.6 slice_bitcast_fusion.3.gate_ref
  62.8 4.8 %shard_map.86.refs_0_ = f32[4096,64]{1,0:T(8,128)} custom-call(bf16[4096,192]{1,0:T(8,128)(2,1)} %copy-done.1, bf16[4096,192]{1,0:T(8,128)(2,1)} %copy-done.1, bf16[4096,64]{1,0:T(8,128)(2,1)} %copy-done.2, f32[8,128]{1,0:T(8,128)} %slice_bitcast_fusion.3.gate_ref, f32[4096,64]{1,0:T(8,128)} %shard_map.85.refs_0_), custom_call_target="tpu_custom_call", output_to_operand_aliasing={{}: (4, {})} | custom-call | tf_op jit(solution)/shard_map/pallas_call | solution.py:80
  67.6 0.0 collective-permute-done.4
  67.7 1.0 collective-permute-start.5
  68.7 0.6 slice_bitcast_fusion.4.gate_ref
  69.3 4.8 %shard_map.87.refs_0_ = f32[4096,64]{1,0:T(8,128)} custom-call(bf16[4096,192]{1,0:T(8,128)(2,1)} %copy-done.1, bf16[4096,192]{1,0:T(8,128)(2,1)} %copy-done.1, bf16[4096,64]{1,0:T(8,128)(2,1)} %copy-done.2, f32[8,128]{1,0:T(8,128)} %slice_bitcast_fusion.4.gate_ref, f32[4096,64]{1,0:T(8,128)} %shard_map.86.refs_0_), custom_call_target="tpu_custom_call", output_to_operand_aliasing={{}: (4, {})} | custom-call | tf_op jit(solution)/shard_map/pallas_call | solution.py:80
  74.2 0.0 collective-permute-done.5
  74.2 1.8 %collective-permute-start.6 = (f32[2,64,128]{2,1,0:T(8,128)S(1)}, f32[2,64,128]{2,1,0:T(8,128)S(1)}, u32[]{:S(2)}, u32[]{:S(2)}) collective-permute-start(f32[2,64,128]{2,1,0:T(8,128)S(1)} %slice_add_fusion.5), channel_id=1, source_target_pairs={{0,64},{1,65},{2,66},{3,67},{4,68},{5,69},{6,70},{7,71},{8,72},{9,... | collective-permute-start | bytes 196616 | tf_op jit(solution)/shard_map/ppermute | solution.py:21
  76.0 0.6 slice_bitcast_fusion.5.gate_ref
  76.6 4.8 %shard_map.88.refs_0_ = f32[4096,64]{1,0:T(8,128)} custom-call(bf16[4096,192]{1,0:T(8,128)(2,1)} %copy-done.1, bf16[4096,192]{1,0:T(8,128)(2,1)} %copy-done.1, bf16[4096,64]{1,0:T(8,128)(2,1)} %copy-done.2, f32[8,128]{1,0:T(8,128)} %slice_bitcast_fusion.5.gate_ref, f32[4096,64]{1,0:T(8,128)} %shard_map.87.refs_0_), custom_call_target="tpu_custom_call", output_to_operand_aliasing={{}: (4, {})} | custom-call | tf_op jit(solution)/shard_map/pallas_call | solution.py:80
  81.4 0.0 collective-permute-done.6
  81.5 3.2 %collective-permute-start.7 = (f32[1,64,128]{2,1,0:T(8,128)S(1)}, f32[1,64,128]{2,1,0:T(8,128)S(1)}, u32[]{:S(2)}, u32[]{:S(2)}) collective-permute-start(f32[1,64,128]{2,1,0:T(8,128)S(1)} %get-tuple-element.16), channel_id=1, source_target_pairs={{0,128},{1,129},{2,130},{3,131},{4,132},{5,133},{6,134},{7,135},{8... | collective-permute-start | bytes 98312 | tf_op jit(solution)/shard_map/ppermute | solution.py:21
  84.7 0.6 slice_bitcast_fusion.6.gate_ref
  85.3 4.9 %shard_map.89 = f32[4096,64]{1,0:T(8,128)} custom-call(bf16[4096,192]{1,0:T(8,128)(2,1)} %copy-done.1, bf16[4096,192]{1,0:T(8,128)(2,1)} %copy-done.1, bf16[4096,64]{1,0:T(8,128)(2,1)} %copy-done.2, f32[8,128]{1,0:T(8,128)} %slice_bitcast_fusion.6.gate_ref, f32[4096,64]{1,0:T(8,128)} %shard_map.88.refs_0_), custom_call_target="tpu_custom_call", output_to_operand_aliasing={{}: (4, {})} | custom-call | tf_op jit(solution)/shard_map/pallas_call | solution.py:80
  90.1 0.0 collective-permute-done.7
  90.2 5.4 %fusion.20 = bf16[4096,64]{1,0:T(8,128)(2,1)S(1)} fusion(f32[4096,64]{1,0:T(8,128)} %shard_map.89, f32[2,2048,64]{2,1,0:T(8,128)S(1)} %copy.17, pred[4096]{0:T(1024)(128)(4,1)S(1)} %fusion.36, bf16[9,4096,128]{2,1,0:T(8,128)(2,1)} %param.12, f32[8,64,128]{2,1,0:T(8,128)S(1)} %constant_dynamic-update-slice_fusion, f32[8,128]{1,0:T(8,128)S(1)} %slice_multiply_fusion.8, ...), kind=kOutput, calls=%fused_computation.19 | convolution fusion | flops 538116096 | bytes 12328992 | tf_op jit(solution)/shard_map/lrk,lpk->rp/dot_general | solution.py:161
  95.5 14.6 %fusion.17 = bf16[4096,64]{0,1:T(8,128)(2,1)} fusion(bf16[4096,64]{1,0:T(8,128)(2,1)S(1)} %fusion.20, s32[4096]{0:T(1024)S(1)} %bitcast.59), kind=kOutput, calls=%fused_computation.14 | convolution fusion | flops 2164523008 | bytes 1064960 | tf_op jit(solution)/shard_map/dot_general | solution.py:168
  (26 shorter events, 0.2 us)
Async XLA Ops:
  0.0 1.3 %copy-start = (s32[2]{0:T(128)S(1)}, s32[2]{0:T(128)}, u32[]{:S(2)}) copy-start(s32[2]{0:T(128)} %param.11) | copy-start | bytes 28
  0.0 2.4 %copy-start.5 = (s32[1,4096]{1,0:T(1,128)S(1)}, s32[1,4096]{1,0:T(1,128)}, u32[]{:S(2)}) copy-start(s32[1,4096]{1,0:T(1,128)} %param.10) | copy-start | bytes 49156
  0.0 2.4 %copy-start.4 = (bf16[4096,64]{0,1:T(8,128)(2,1)S(1)}, bf16[4096,64]{0,1:T(8,128)(2,1)}, u32[]{:S(2)}) copy-start(bf16[4096,64]{0,1:T(8,128)(2,1)} %param.8) | copy-start | bytes 1572868
  1.9 14.5 %slice-start = ((s8[9437184]{0:T(1024)(128)(4,1)}), s8[1048576]{0:T(1024)(128)(4,1)S(1)}, s32[]{:S(2)}) async-start(s8[9437184]{0:T(1024)(128)(4,1)} %bitcast.51), calls=%async_computation | async-start | bytes 2097152
  2.4 14.0 %slice-start.1 = ((s8[9437184]{0:T(1024)(128)(4,1)}), s8[4194304]{0:T(1024)(128)(4,1)S(1)}, s32[]{:S(2)}) async-start(s8[9437184]{0:T(1024)(128)(4,1)} %bitcast.51), calls=%async_computation.1 | async-start | bytes 8388608
  2.4 14.0 %slice-start.2 = ((s8[9437184]{0:T(1024)(128)(4,1)}), s8[4194304]{0:T(1024)(128)(4,1)S(1)}, s32[]{:S(2)}) async-start(s8[9437184]{0:T(1024)(128)(4,1)} %bitcast.51), calls=%async_computation.2 | async-start | bytes 8388608
  16.5 1.7 %copy-start.1 = (bf16[4096,192]{1,0:T(8,128)(2,1)}, bf16[4096,192]{1,0:T(8,128)(2,1)S(1)}, u32[]{:S(2)}) copy-start(bf16[4096,192]{1,0:T(8,128)(2,1)S(1)} %fusion.11.rows_ref.leaf_ref) | copy-start | bytes 4718596
  18.1 0.7 copy-start.3
  18.1 7.8 %collective-permute-start = (f32[8,64,128]{2,1,0:T(8,128)S(1)}, f32[8,64,128]{2,1,0:T(8,128)}, u32[]{:S(2)}, u32[]{:S(2)}) collective-permute-start(f32[8,64,128]{2,1,0:T(8,128)S(1)} %fusion.26), channel_id=1, source_target_pairs={{0,1},{1,0},{2,3},{3,2},{4,5},{5,4},{6,7},{7,6},{8,9},{9,8},{10,11... | collective-permute-start | bytes 786440 | tf_op jit(solution)/shard_map/ppermute | solution.py:21
  18.3 1.5 %copy-start.2 = (bf16[4096,64]{1,0:T(8,128)(2,1)}, bf16[4096,64]{1,0:T(8,128)(2,1)S(1)}, u32[]{:S(2)}) copy-start(bf16[4096,64]{1,0:T(8,128)(2,1)S(1)} %slice.181.vec_ref) | copy-start | bytes 1572868
  26.9 8.9 %collective-permute-start.1 = (f32[7,64,128]{2,1,0:T(8,128)S(1)}, f32[7,64,128]{2,1,0:T(8,128)S(1)}, u32[]{:S(2)}, u32[]{:S(2)}) collective-permute-start(f32[7,64,128]{2,1,0:T(8,128)S(1)} %slice_add_fusion), channel_id=1, source_target_pairs={{0,2},{1,3},{2,0},{3,1},{4,6},{5,7},{6,4},{7,5},{8,10},{9,11},{10,... | collective-permute-start | bytes 688136 | tf_op jit(solution)/shard_map/ppermute | solution.py:21
  35.8 12.4 %collective-permute-start.2 = (f32[6,64,128]{2,1,0:T(8,128)S(1)}, f32[6,64,128]{2,1,0:T(8,128)S(1)}, u32[]{:S(2)}, u32[]{:S(2)}) collective-permute-start(f32[6,64,128]{2,1,0:T(8,128)S(1)} %slice_add_fusion.1), channel_id=1, source_target_pairs={{0,4},{1,5},{2,6},{3,7},{4,0},{5,1},{6,2},{7,3},{8,12},{9,13},{10,... | collective-permute-start | bytes 589832 | tf_op jit(solution)/shard_map/ppermute | solution.py:21
  48.2 13.1 %collective-permute-start.3 = (f32[5,64,128]{2,1,0:T(8,128)S(1)}, f32[5,64,128]{2,1,0:T(8,128)S(1)}, u32[]{:S(2)}, u32[]{:S(2)}) collective-permute-start(f32[5,64,128]{2,1,0:T(8,128)S(1)} %slice_add_fusion.2), channel_id=1, source_target_pairs={{0,8},{1,9},{2,10},{3,11},{4,12},{5,13},{6,14},{7,15},{8,0},{9,1},... | collective-permute-start | bytes 491528 | tf_op jit(solution)/shard_map/ppermute | solution.py:21
  61.3 6.3 %collective-permute-start.4 = (f32[4,64,128]{2,1,0:T(8,128)S(1)}, f32[4,64,128]{2,1,0:T(8,128)S(1)}, u32[]{:S(2)}, u32[]{:S(2)}) collective-permute-start(f32[4,64,128]{2,1,0:T(8,128)S(1)} %slice_add_fusion.3), channel_id=1, source_target_pairs={{0,16},{1,17},{2,18},{3,19},{4,20},{5,21},{6,22},{7,23},{8,24},{9,... | collective-permute-start | bytes 393224 | tf_op jit(solution)/shard_map/ppermute | solution.py:21
  67.7 6.5 %collective-permute-start.5 = (f32[3,64,128]{2,1,0:T(8,128)S(1)}, f32[3,64,128]{2,1,0:T(8,128)S(1)}, u32[]{:S(2)}, u32[]{:S(2)}) collective-permute-start(f32[3,64,128]{2,1,0:T(8,128)S(1)} %slice_add_fusion.4), channel_id=1, source_target_pairs={{0,32},{1,33},{2,34},{3,35},{4,36},{5,37},{6,38},{7,39},{8,40},{9,... | collective-permute-start | bytes 294920 | tf_op jit(solution)/shard_map/ppermute | solution.py:21
  74.2 7.3 %collective-permute-start.6 = (f32[2,64,128]{2,1,0:T(8,128)S(1)}, f32[2,64,128]{2,1,0:T(8,128)S(1)}, u32[]{:S(2)}, u32[]{:S(2)}) collective-permute-start(f32[2,64,128]{2,1,0:T(8,128)S(1)} %slice_add_fusion.5), channel_id=1, source_target_pairs={{0,64},{1,65},{2,66},{3,67},{4,68},{5,69},{6,70},{7,71},{8,72},{9,... | collective-permute-start | bytes 196616 | tf_op jit(solution)/shard_map/ppermute | solution.py:21
  81.5 8.7 %collective-permute-start.7 = (f32[1,64,128]{2,1,0:T(8,128)S(1)}, f32[1,64,128]{2,1,0:T(8,128)S(1)}, u32[]{:S(2)}, u32[]{:S(2)}) collective-permute-start(f32[1,64,128]{2,1,0:T(8,128)S(1)} %get-tuple-element.16), channel_id=1, source_target_pairs={{0,128},{1,129},{2,130},{3,131},{4,132},{5,133},{6,134},{7,135},{8... | collective-permute-start | bytes 98312 | tf_op jit(solution)/shard_map/ppermute | solution.py:21
  85.3 4.9 %copy-start.6 = (f32[8]{0:T(128)S(1)}, f32[8]{0:T(128)}, u32[]{:S(2)}) copy-start(f32[8]{0:T(128)} %constant.35.clone) | copy-start | bytes 100
